TPU v7x, 256 devices: a whole 4x4x8 slice. The times are simulated.
256 devices in a mesh: tok: 16 (over z, core), tp: 16 (over x, y).
Axes of the slice: x: 4, y: 4, z: 8, core: 2. Of those that a mesh axis runs over, the one named last changes fastest.
Arguments:
- hidden_states: bfloat16 [32768, 1024], P(('tok', 'tp')), may hold values from -40 to 40
- first_gain: float32 [1024], replicated, may hold values from 0.1 to 1.9
- second_gain: float32 [1024], replicated, may hold values from 0.1 to 1.9
- w_query: bfloat16 [1024, 1024], P(None, 'tp'), may hold values from -1 to 1
- w_keyval: bfloat16 [1024, 1024], replicated, may hold values from -0.375 to 0.375
- w_out: bfloat16 [1024, 1024], P('tp'), may hold values from -0.75 to 0.75
- kv_cache: bfloat16 [384, 128, 1024], P('tok'), may hold values from -310 to 310
- page_table: int32 [32, 16], P('tok'), may hold values from 0 to 383, as said below
- cached_len: int32 [32], P('tok'), may hold values from 128 to 2048, as said below
- expert_ids: int32 [32768, 8], P(('tok', 'tp')), may hold values from 0 to 31, all different within a row; in each aligned block of 128 rows (0 to 127, 128 to 255, ...) at most 64 rows name the same one
- gate_weights: float32 [32768, 8], P(('tok', 'tp')), may hold values from 0.1 to 1
- w_gate_up: bfloat16 [32, 1024, 1024], P('tp', 'tok'), may hold values from -0.1875 to 0.1875
- w_down: bfloat16 [32, 512, 1024], P('tp', 'tok'), may hold values from -1 to 1
Outputs:
- layer_out: bfloat16 [32768, 1024], P(('tok', 'tp'))
Inputs may be any that keep to these rules, and one draw needn't show every extreme that they name: `page_table`: request r's entries are pages of its own tok index, rows 24 * (r // 2) to 24 * (r // 2 + 1) - 1; its first 8 entries are the same for all requests of that tok index, and all other entries name pages that no other entry names. `cached_len`: some request has exactly 2048 cached tokens. `expert_ids`: in the rows of one device (aligned blocks of 128 rows) no expert is named by more than 64 rows, and a row names 8 different experts.
All inputs are finite; a program needn't handle non-finite values.
Results may differ from a plain program's by a relative error of at most 0.017.
The roundings to bfloat16 on the way count: a program that leaves them out, or rounds other values in their place, can miss the bound.
Values may be sent and summed in bfloat16 or wider, within the bound.
No kernel may reach another device: no remote copies, remote signals or barrier semaphores. Data moves between devices by JAX's collectives and lax.ppermute only.
A program may use at most 128 MiB of HBM per device.

v0:
```python
import jax
import jax.numpy as jnp
from jax import lax
from jax.sharding import Mesh
from jax.sharding import PartitionSpec as P

D = 1024
HEADS = 16
KV_HEADS = 8
HEAD_DIM = 64
EXPERTS = 32
FF_EXPERT = 512
TOP = 8
NEW = 1024
MAX_CACHED = 2048
REQ_DEV = 2


ATTN_SCALE = 0.015625
EPSILON = 1e-06
THETA = 10000.0

TOK = ("tz", "tc")
TP = ("ra", "rb")


def rms_norm(values, gain):
    wide = values.astype(jnp.float32)
    factor = lax.rsqrt(jnp.mean(wide * wide, axis=-1, keepdims=True) + EPSILON)
    return (wide * factor * gain).astype(jnp.bfloat16)


def rotate(values, positions):
    row_count = values.shape[0]
    shaped = values.reshape(row_count, -1, HEAD_DIM)
    half_dim = HEAD_DIM // 2
    exponent = jnp.arange(half_dim).astype(jnp.float32) * (2.0 / HEAD_DIM)
    frequency = jnp.power(THETA, -exponent)
    angles = positions.astype(jnp.float32)[:, None] * frequency[None, :]
    cosine = jnp.cos(angles)[:, None, :]
    sine_part = jnp.sin(angles)[:, None, :]
    leading = shaped[..., :half_dim]
    trailing = shaped[..., half_dim:]
    turned = jnp.concatenate(
        [leading * cosine - trailing * sine_part, trailing * cosine + leading * sine_part], axis=-1
    )
    return turned.reshape(row_count, -1)


def gather_rows(piece, axis_name, count):
    send = jnp.broadcast_to(piece[None], (count,) + piece.shape)
    return lax.all_to_all(send, axis_name, split_axis=0, concat_axis=0, tiled=True)


def shards(
    hidden_states,
    first_gain,
    second_gain,
    w_query,
    w_keyval,
    w_out,
    kv_cache,
    page_table,
    cached_len,
    expert_ids,
    gate_weights,
    w_gate_up,
    w_down,
):
    tok_rows = hidden_states.shape[0]
    tp_size = lax.axis_size(TP)
    core = lax.axis_index("tc")
    local_req = lax.axis_index("ra")
    block = lax.axis_index("rb")
    kv_cols = KV_HEADS * HEAD_DIM
    group_size = HEADS // KV_HEADS

    half_rows = D // 2
    wq_half = lax.dynamic_slice_in_dim(w_query, core * half_rows, half_rows, 0)
    wo_half = lax.dynamic_slice_in_dim(w_out, core * half_rows, half_rows, 1)
    lanes = 128
    pieces = gather_rows(
        jnp.concatenate([wq_half.reshape(-1, lanes), wo_half.reshape(-1, lanes)], axis=0),
        TP,
        tp_size,
    )
    q_rows = wq_half.size // lanes
    wq_mine = jnp.transpose(
        pieces[:, :q_rows].reshape(tp_size, half_rows, HEAD_DIM), (1, 0, 2)
    ).reshape(half_rows, D)
    wo_mine = pieces[:, q_rows:].reshape(D, half_rows)
    wq_other, wo_other = lax.ppermute((wq_mine, wo_mine), "tc", [(0, 1), (1, 0)])
    gate_up_full = lax.all_gather(w_gate_up, TOK, axis=1, tiled=True)
    down_full = lax.all_gather(w_down, TOK, axis=1, tiled=True)

    normed = rms_norm(hidden_states, first_gain)
    length = cached_len[local_req]
    positions = length + block * tok_rows + jnp.arange(tok_rows, dtype=jnp.int32)
    keyval = jnp.dot(normed, w_keyval, preferred_element_type=jnp.float32)
    new_kv = jnp.concatenate(
        [rotate(keyval[:, :kv_cols], positions), keyval[:, kv_cols:]], axis=1
    ).astype(jnp.bfloat16)
    request_kv = gather_rows(new_kv, "rb", lax.axis_size("rb")).reshape(NEW, 2 * kv_cols)
    other_core = 1 - core
    q_wide = jnp.dot(
        lax.dynamic_slice_in_dim(normed, core * half_rows, half_rows, 1),
        wq_mine,
        preferred_element_type=jnp.float32,
    ) + jnp.dot(
        lax.dynamic_slice_in_dim(normed, other_core * half_rows, half_rows, 1),
        wq_other,
        preferred_element_type=jnp.float32,
    )
    queries = rotate(q_wide, positions).astype(jnp.bfloat16)

    local_pages = page_table[local_req] - lax.axis_index(TOK) * kv_cache.shape[0]
    cached = jnp.take(kv_cache, local_pages, axis=0).reshape(MAX_CACHED, 2 * kv_cols)
    keys_total = jnp.concatenate([cached[:, :kv_cols], request_kv[:, :kv_cols]], axis=0).reshape(
        MAX_CACHED + NEW, KV_HEADS, HEAD_DIM
    )
    values_total = jnp.concatenate(
        [cached[:, kv_cols:], request_kv[:, kv_cols:]], axis=0
    ).reshape(MAX_CACHED + NEW, KV_HEADS, HEAD_DIM)
    grouped_q = queries.reshape(tok_rows, KV_HEADS, group_size, HEAD_DIM)
    scores = (
        jnp.einsum("qgpd,kgd->gpqk", grouped_q, keys_total, preferred_element_type=jnp.float32)
        * ATTN_SCALE
    )
    key_index = jnp.arange(MAX_CACHED + NEW, dtype=jnp.int32)
    query_pos = block * tok_rows + jnp.arange(tok_rows, dtype=jnp.int32)
    allowed = jnp.where(
        key_index[None, :] < MAX_CACHED,
        key_index[None, :] < length,
        key_index[None, :] - MAX_CACHED <= query_pos[:, None],
    )
    scores = jnp.where(allowed, scores, -1e30)
    top_score = jnp.max(scores, axis=-1, keepdims=True)
    weights = jnp.exp(scores - top_score)
    probs = (weights / jnp.sum(weights, axis=-1, keepdims=True)).astype(jnp.bfloat16)
    attended = (
        jnp.einsum("gpqk,kgd->qgpd", probs, values_total, preferred_element_type=jnp.float32)
        .astype(jnp.bfloat16)
        .reshape(tok_rows, HEADS * HEAD_DIM)
    )
    out_mine = jnp.dot(attended, wo_mine, preferred_element_type=jnp.float32)
    out_other = jnp.dot(attended, wo_other, preferred_element_type=jnp.float32)
    first = core == 0
    projected_out = jnp.concatenate(
        [jnp.where(first, out_mine, out_other), jnp.where(first, out_other, out_mine)], axis=1
    )
    middle = (hidden_states.astype(jnp.float32) + projected_out).astype(jnp.bfloat16)
    normed_two = rms_norm(middle, second_gain)

    experts_local = EXPERTS // tp_size
    capacity = 2 * tok_rows * TOP // EXPERTS
    expert_range = jnp.arange(EXPERTS, dtype=jnp.int32)
    onehot = (expert_ids[:, :, None] == expert_range[None, None, :]).astype(jnp.int32)
    per_token = jnp.sum(onehot, axis=1)
    earlier = jnp.cumsum(per_token, axis=0) - per_token
    slot_ids = jnp.sum(onehot * earlier[:, None, :], axis=2)
    target = expert_ids * capacity + slot_ids
    outgoing_rows = jnp.broadcast_to(normed_two[:, None, :], (tok_rows, TOP, D))
    send_buffer = jnp.zeros((EXPERTS * capacity, D), jnp.bfloat16).at[target].set(outgoing_rows)
    send_buffer = send_buffer.reshape(tp_size, experts_local, capacity, D)
    returned = []
    for local in range(experts_local):
        received = lax.all_to_all(
            send_buffer[:, local], TP, split_axis=0, concat_axis=0, tiled=True
        ).reshape(tp_size * capacity, D)
        both = jnp.dot(received, gate_up_full[local], preferred_element_type=jnp.float32)
        activated = (jax.nn.silu(both[:, :FF_EXPERT]) * both[:, FF_EXPERT:]).astype(jnp.bfloat16)
        produced = jnp.dot(
            activated, down_full[local], preferred_element_type=jnp.float32
        ).astype(jnp.bfloat16)
        returned.append(
            lax.all_to_all(
                produced.reshape(tp_size, capacity, D), TP, split_axis=0, concat_axis=0, tiled=True
            )
        )
    returned = jnp.stack(returned, axis=1)
    returned = returned.reshape(EXPERTS * capacity, D)
    picked = returned[target]
    mixture = jnp.einsum("tk,tkd->td", gate_weights, picked.astype(jnp.float32))
    return (middle.astype(jnp.float32) + mixture).astype(jnp.bfloat16)


def solution(mesh):
    tok_size, tp_size = mesh.devices.shape
    group = tp_size // REQ_DEV
    split = Mesh(mesh.devices.reshape(tok_size // 2, 2, REQ_DEV, group), TOK + TP)
    in_specs = (
        P(TOK + TP, None),
        P(),
        P(),
        P(None, TP),
        P(),
        P(TP, None),
        P(TOK, None, None),
        P(TOK, None),
        P(TOK),
        P(TOK + TP, None),
        P(TOK + TP, None),
        P(TP, TOK, None),
        P(TP, TOK, None),
    )
    out_specs = P(TOK + TP, None)
    return jax.shard_map(shards, mesh=split, in_specs=in_specs, out_specs=out_specs, check_vma=False)
```

profile of v0, /device:TPU:224, one launch (start us, length us, event | category | flops | bytes accessed | tf_op | source)
XLA Modules:
  0.0 296.7 jit_solution(15382464340707534592)
XLA Ops:
  6.5 0.7 all-gather.3.cloned.1.call-update
  7.3 1.1 fusion.23
  8.4 1.1 fusion.25
  11.9 1.6 broadcast_in_dim.52
  13.6 5.5 %all-to-all-start = ((bf16[8,128,1024]{1,2,0:T(8,128)(2,1)}), bf16[8,128,1024]{1,2,0:T(8,128)(2,1)S(1)}, u32[]{:S(2)}, u32[]{:S(2)}) async-start(bf16[8,128,1024]{1,2,0:T(8,128)(2,1)} %broadcast_in_dim.52), calls=%async_computation | async-start | bytes 4194304 | tf_op jit(solution)/shard_map/all_to_all | solution.py:52
  19.1 0.7 all-gather.5.cloned.1.call-update
  21.5 23.7 %all-to-all-done = bf16[8,128,1024]{1,2,0:T(8,128)(2,1)S(1)} async-done(((bf16[8,128,1024]{1,2,0:T(8,128)(2,1)}), bf16[8,128,1024]{1,2,0:T(8,128)(2,1)S(1)}, u32[]{:S(2)}, u32[]{:S(2)}) %all-to-all-start) | async-done | bytes 2097184 | tf_op jit(solution)/shard_map/all_to_all | solution.py:52
  45.1 1.7 broadcast_in_dim.56
  46.8 5.5 %all-to-all-start.1 = ((bf16[16,512,128]{2,1,0:T(8,128)(2,1)}), bf16[16,512,128]{2,1,0:T(8,128)(2,1)}, u32[]{:S(2)}, u32[]{:S(2)}) async-start(bf16[16,512,128]{2,1,0:T(8,128)(2,1)} %broadcast_in_dim.56), calls=%async_computation.1 | async-start | bytes 4194304 | tf_op jit(solution)/shard_map/all_to_all | solution.py:52
  52.3 5.5 %gather_fusion = bf16[16,128,1024]{2,1,0:T(8,128)(2,1)} fusion(bf16[24,128,1024]{2,1,0:T(8,128)(2,1)} %param.19, s32[1024]{0:T(1024)S(1)} %pad_clamp_fusion), kind=kCustom, calls=%fused_computation | custom fusion | bytes 8388672 | tf_op jit(solution)/shard_map/jit(_take)/gather | solution.py:117
  57.9 6.6 %copy.56 = bf16[2048,1024]{0,1:T(8,128)(2,1)} copy(bf16[2048,1024]{1,0:T(8,128)(2,1)} %bitcast.92) | data formatting | bytes 8388608 | tf_op jit(solution)/shard_map/jit(_take)/gather | solution.py:117
  64.6 2.6 broadcast_select_fusion
  67.2 2.4 fusion.43
  69.6 3.5 %compare_select_fusion = pred[128,3072]{0,1:T(8,128)(4,1)} fusion(s32[128]{0:T(128)S(1)} %iota_add_fusion.1, s32[3072]{0:T(1024)S(1)} %iota_add_fusion, pred[3072]{0:T(1024)(128)(4,1)S(1)} %get-tuple-element.27, pred[3072]{0:T(1024)(128)(4,1)S(1)} %get-tuple-element.28), kind=kLoop, calls=%fused_computation.34 | loop fusion | flops 786432 | bytes 412160 | tf_op jit(solution)/shard_map/jit(_where)/select_n | solution.py:131
  73.1 2.6 copy.60
  75.7 6.7 %all-to-all-done.1 = bf16[16,512,128]{2,1,0:T(8,128)(2,1)} async-done(((bf16[16,512,128]{2,1,0:T(8,128)(2,1)}), bf16[16,512,128]{2,1,0:T(8,128)(2,1)}, u32[]{:S(2)}, u32[]{:S(2)}) %all-to-all-start.1) | async-done | bytes 2097184 | tf_op jit(solution)/shard_map/all_to_all | solution.py:52
  82.4 2.7 fusion.44
  85.1 0.8 reshape.221
  85.9 0.8 copy.64
  86.9 3.0 %fusion.45 = (bf16[1024,512]{1,0:T(8,128)(2,1)}, bf16[1024,512]{1,0:T(8,128)(2,1)}) fusion(bf16[1024,1024]{1,0:T(8,128)(2,1)} %bitcast.94), kind=kLoop, calls=%fused_computation.103 | loop fusion | bytes 4194304 | tf_op jit(solution)/shard_map/slice | solution.py:118
  89.9 2.4 copy.61
  92.3 2.3 copy.62
  94.6 4.4 %pad_maximum_fusion.1 = (bf16[3072,512]{0,1:T(8,128)(2,1)}, bf16[3072,512]{0,1:T(8,128)(2,1)}) fusion(bf16[1024,512]{0,1:T(8,128)(2,1)} %copy.61, bf16[2048,512]{0,1:T(8,128)(2,1)} %get-tuple-element.10, bf16[1024,512]{0,1:T(8,128)(2,1)} %copy.62, bf16[2048,512]{0,1:T(8,128)(2,1)S(1)} %copy-done.2), kind=kLoop, calls=%fused_computation.14 | loop fusion | flops 12582912 | bytes 12582912 | tf_op jit(solution)/shard_map/concatenate | solution.py:121
  99.0 1.7 reshape.225
  100.7 0.8 collective-permute-start.1
  102.0 1.8 convolution_add_fusion
  104.0 13.9 %fusion.46 = (f32[8,2,128]{2,1,0:T(2,128)S(1)}, f32[8,2,128,3072]{2,3,1,0:T(8,128)}) fusion(pred[128,3072]{0,1:T(8,128)(4,1)S(1)} %copy-done.5, bf16[3072,8,64,1]{0,2,3,1:T(8,128)(2,1)} %bitcast.99, bf16[128,8,2,64]{0,3,2,1:T(8,128)(2,1)S(1)} %bitcast.109), kind=kOutput, calls=%fused_computation.104 | convolution fusion | flops 830475264 | bytes 28975104 | tf_op jit(solution)/shard_map/sub | solution.py:138
  117.9 11.4 %fusion.17 = bf16[8,64,2,128]{3,1,2,0:T(8,128)(2,1)S(1)} fusion(bf16[3072,8,64,1]{0,2,3,1:T(8,128)(2,1)} %bitcast.98, f32[8,2,128,3072]{2,3,1,0:T(8,128)} %get-tuple-element.24, f32[8,2,128]{2,1,0:T(2,128)S(1)} %get-tuple-element.23), kind=kOutput, calls=%fused_computation.36 | convolution fusion | flops 818020352 | bytes 28581888 | tf_op jit(solution)/shard_map/gpqk,kgd->qgpd/dot_general | solution.py:141
  129.7 1.6 broadcast_select_fusion.2
  131.6 7.9 %scatter_custom_fusion = bf16[2048,1024]{1,0:T(8,128)(2,1)} fusion(s32[1024]{0:T(1024)S(1)} %reshape.250, bf16[]{:T(256)} %constant.78.clone.1, bf16[128,1024]{1,0:T(8,128)(2,1)S(1)} %fusion.29), kind=kCustom, calls=%fused_computation.29 | custom fusion | bytes 4456450 | tf_op jit(solution)/shard_map/scatter | solution.py:163
  139.5 4.2 %slice_bitcast_fusion.5 = (bf16[16,64,1024]{2,1,0:T(8,128)(2,1)}, bf16[16,64,1024]{2,1,0:T(8,128)(2,1)S(1)}) fusion(bf16[16,2,64,1024]{3,2,1,0:T(8,128)(2,1)} %bitcast.91), kind=kLoop, calls=%fused_computation.26 | loop fusion | bytes 8388608 | tf_op jit(solution)/shard_map/squeeze | solution.py:168
  143.7 32.2 %all_to_all.30 = bf16[16,64,1024]{2,1,0:T(8,128)(2,1)} all-to-all(bf16[16,64,1024]{2,1,0:T(8,128)(2,1)S(1)} %get-tuple-element.8), channel_id=1, replica_groups=mesh['tz'=8,'tc'=2,'ra'=2,'rb'=8] {'ra','rb'}, dimensions={0} | all-to-all | bytes 4194304 | tf_op jit(solution)/shard_map/all_to_all | solution.py:167
  175.9 3.7 %all-to-all-start.2 = ((bf16[16,64,1024]{2,1,0:T(8,128)(2,1)}), bf16[16,64,1024]{2,1,0:T(8,128)(2,1)S(1)}, u32[]{:S(2)}, u32[]{:S(2)}) async-start(bf16[16,64,1024]{2,1,0:T(8,128)(2,1)} %get-tuple-element.7), calls=%async_computation.2 | async-start | bytes 4194304 | tf_op jit(solution)/shard_map/all_to_all | solution.py:167
  179.7 6.5 %fusion.9 = f32[1024,1024]{1,0:T(8,128)} fusion(bf16[1024,1024]{1,0:T(8,128)(2,1)} %bitcast.103, bf16[2,1024,1024]{2,1,0:T(8,128)(2,1)} %all-gather.3.cloned.1.call-done), kind=kOutput, calls=%fused_computation.20 | convolution fusion | flops 2147483648 | bytes 8388608 | tf_op jit(solution)/shard_map/dot_general | solution.py:170
  186.2 5.1 %convolution_convert_fusion = bf16[1024,1024]{1,0:T(8,128)(2,1)} fusion(f32[1024,1024]{1,0:T(8,128)} %fusion.9, bf16[2,512,1024]{2,1,0:T(8,128)(2,1)} %all-gather.5.cloned.1.call-done), kind=kOutput, calls=%fused_computation.32 | convolution fusion | flops 1077936128 | bytes 7340032 | tf_op jit(solution)/shard_map/dot_general | solution.py:172
  191.3 17.2 %all-to-all-done.2 = bf16[16,64,1024]{2,1,0:T(8,128)(2,1)S(1)} async-done(((bf16[16,64,1024]{2,1,0:T(8,128)(2,1)}), bf16[16,64,1024]{2,1,0:T(8,128)(2,1)S(1)}, u32[]{:S(2)}, u32[]{:S(2)}) %all-to-all-start.2) | async-done | bytes 2097184 | tf_op jit(solution)/shard_map/all_to_all | solution.py:167
  208.4 1.3 copy-done.4
  209.7 3.8 %all-to-all-start.5 = ((bf16[16,64,1024]{2,1,0:T(8,128)(2,1)}), bf16[16,64,1024]{2,1,0:T(8,128)(2,1)S(1)}, u32[]{:S(2)}, u32[]{:S(2)}) async-start(bf16[16,64,1024]{2,1,0:T(8,128)(2,1)} %bitcast.101), calls=%async_computation.5 | async-start | bytes 4194304 | tf_op jit(solution)/shard_map/all_to_all | solution.py:176
  213.5 4.7 %fusion.11 = f32[1024,1024]{1,0:T(8,128)S(1)} fusion(bf16[1024,1024]{1,0:T(8,128)(2,1)} %bitcast.100, bf16[2,1024,1024]{2,1,0:T(8,128)(2,1)} %all-gather.3.cloned.1.call-done), kind=kOutput, calls=%fused_computation.25 | convolution fusion | flops 2147483648 | bytes 8388608 | tf_op jit(solution)/shard_map/dot_general | solution.py:170
  218.2 2.6 convolution_convert_fusion.1
  220.9 20.3 %all-to-all-done.5 = bf16[16,64,1024]{2,1,0:T(8,128)(2,1)S(1)} async-done(((bf16[16,64,1024]{2,1,0:T(8,128)(2,1)}), bf16[16,64,1024]{2,1,0:T(8,128)(2,1)S(1)}, u32[]{:S(2)}, u32[]{:S(2)}) %all-to-all-start.5) | async-done | bytes 2097184 | tf_op jit(solution)/shard_map/all_to_all | solution.py:176
  241.2 4.6 %all-to-all-start.3 = ((bf16[16,64,1024]{2,1,0:T(8,128)(2,1)}), bf16[16,64,1024]{2,1,0:T(8,128)(2,1)}, u32[]{:S(2)}, u32[]{:S(2)}) async-start(bf16[16,64,1024]{2,1,0:T(8,128)(2,1)} %bitcast.102), calls=%async_computation.3 | async-start | bytes 4194304 | tf_op jit(solution)/shard_map/all_to_all | solution.py:176
  245.9 27.5 %all-to-all-done.3 = bf16[16,64,1024]{2,1,0:T(8,128)(2,1)} async-done(((bf16[16,64,1024]{2,1,0:T(8,128)(2,1)}), bf16[16,64,1024]{2,1,0:T(8,128)(2,1)}, u32[]{:S(2)}, u32[]{:S(2)}) %all-to-all-start.3) | async-done | bytes 2097184 | tf_op jit(solution)/shard_map/all_to_all | solution.py:176
  273.5 2.0 pad_maximum_fusion
  275.4 2.4 copy.71
  277.8 8.9 %gather_fusion.1 = bf16[1024,1024]{1,0:T(8,128)(2,1)} fusion(bf16[2048,1024]{1,0:T(8,128)(2,1)} %bitcast.90, s32[1024]{0:T(1024)S(1)} %broadcast_clamp_fusion), kind=kCustom, calls=%fused_computation.1 | custom fusion | bytes 4198400 | tf_op jit(solution)/shard_map/gather | solution.py:182
  286.7 2.3 fusion.12
  289.0 0.8 fusion.30
  (80 shorter events, 5.1 us)
Async XLA Ops:
  6.5 2.9 copy-start
  6.5 173.1 %all-gather.3.cloned.1.call-start = ((), (), s32[]{:S(2)}) async-start(), calls=%async_computation.6 | async-start | bytes 4456448 | tf_op jit(solution)/shard_map/all_gather | solution.py:93
  9.5 0.7 copy-start.13
  13.5 6.3 %copy-start.7 = (bf16[64,1024]{1,0:T(8,128)(2,1)S(1)}, bf16[64,1024]{1,0:T(8,128)(2,1)}, u32[]{:S(2)}) copy-start(bf16[64,1024]{1,0:T(8,128)(2,1)} %param.18) | copy-start | bytes 393220
  13.5 6.4 %copy-start.8 = (bf16[1024,64]{0,1:T(8,128)(2,1)S(1)}, bf16[1024,64]{0,1:T(8,128)(2,1)}, u32[]{:S(2)}) copy-start(bf16[1024,64]{0,1:T(8,128)(2,1)} %param.16) | copy-start | bytes 393220
  13.5 6.7 %copy-start.6 = (s32[128,8]{0,1:T(8,128)S(1)}, s32[128,8]{0,1:T(8,128)}, u32[]{:S(2)}) copy-start(s32[128,8]{0,1:T(8,128)} %param.22) | copy-start | bytes 12292
  13.5 7.0 %copy-start.11 = (s32[2,16]{1,0:T(2,128)S(1)}, s32[2,16]{1,0:T(2,128)}, u32[]{:S(2)}) copy-start(s32[2,16]{1,0:T(2,128)} %param.20) | copy-start | bytes 388
  13.6 31.6 %all-to-all-start = ((bf16[8,128,1024]{1,2,0:T(8,128)(2,1)}), bf16[8,128,1024]{1,2,0:T(8,128)(2,1)S(1)}, u32[]{:S(2)}, u32[]{:S(2)}) async-start(bf16[8,128,1024]{1,2,0:T(8,128)(2,1)} %broadcast_in_dim.52), calls=%async_computation | async-start | bytes 4194304 | tf_op jit(solution)/shard_map/all_to_all | solution.py:52
  19.1 167.1 %all-gather.5.cloned.1.call-start = ((), (), s32[]{:S(2)}) async-start(), calls=%async_computation.7 | async-start | bytes 2228224 | tf_op jit(solution)/shard_map/all_gather | solution.py:94
  46.8 35.5 %all-to-all-start.1 = ((bf16[16,512,128]{2,1,0:T(8,128)(2,1)}), bf16[16,512,128]{2,1,0:T(8,128)(2,1)}, u32[]{:S(2)}, u32[]{:S(2)}) async-start(bf16[16,512,128]{2,1,0:T(8,128)(2,1)} %broadcast_in_dim.56), calls=%async_computation.1 | async-start | bytes 4194304 | tf_op jit(solution)/shard_map/all_to_all | solution.py:52
  86.8 15.1 %collective-permute-start = (bf16[512,1024]{0,1:T(8,128)(2,1)S(1)}, bf16[512,1024]{0,1:T(8,128)(2,1)}, u32[]{:S(2)}, u32[]{:S(2)}) collective-permute-start(bf16[512,1024]{0,1:T(8,128)(2,1)S(1)} %bitcast.96), channel_id=1, source_target_pairs={{0,16},{16,0},{1,17},{17,1},{2,18},{18,2},{3,19},{19,3},{4,20},{20... | collective-permute-start | bytes 3145736 | tf_op jit(solution)/shard_map/ppermute | solution.py:92
  89.9 4.7 %copy-start.2 = (bf16[2048,512]{0,1:T(8,128)(2,1)S(1)}, bf16[2048,512]{0,1:T(8,128)(2,1)}, u32[]{:S(2)}) copy-start(bf16[2048,512]{0,1:T(8,128)(2,1)} %get-tuple-element.9) | copy-start | bytes 6291460
  100.7 29.0 %collective-permute-start.1 = (bf16[1024,512]{1,0:T(8,128)(2,1)S(1)}, bf16[1024,512]{1,0:T(8,128)(2,1)}, u32[]{:S(2)}, u32[]{:S(2)}) collective-permute-start(bf16[1024,512]{1,0:T(8,128)(2,1)S(1)} %reshape.225), channel_id=1, source_target_pairs={{0,16},{16,0},{1,17},{17,1},{2,18},{18,2},{3,19},{19,3},{4,20},{20... | collective-permute-start | bytes 3145736 | tf_op jit(solution)/shard_map/ppermute | solution.py:92
  101.9 2.1 copy-start.5
  129.3 1.9 copy-start.3
  129.3 2.1 copy-start.9
  175.9 32.5 %all-to-all-start.2 = ((bf16[16,64,1024]{2,1,0:T(8,128)(2,1)}), bf16[16,64,1024]{2,1,0:T(8,128)(2,1)S(1)}, u32[]{:S(2)}, u32[]{:S(2)}) async-start(bf16[16,64,1024]{2,1,0:T(8,128)(2,1)} %get-tuple-element.7), calls=%async_computation.2 | async-start | bytes 4194304 | tf_op jit(solution)/shard_map/all_to_all | solution.py:167
  208.4 1.3 copy-start.4
  209.7 31.4 %all-to-all-start.5 = ((bf16[16,64,1024]{2,1,0:T(8,128)(2,1)}), bf16[16,64,1024]{2,1,0:T(8,128)(2,1)S(1)}, u32[]{:S(2)}, u32[]{:S(2)}) async-start(bf16[16,64,1024]{2,1,0:T(8,128)(2,1)} %bitcast.101), calls=%async_computation.5 | async-start | bytes 4194304 | tf_op jit(solution)/shard_map/all_to_all | solution.py:176
  213.5 4.7 %copy-start.12 = (bf16[2,512,1024]{2,1,0:T(8,128)(2,1)S(1)}, bf16[2,512,1024]{2,1,0:T(8,128)(2,1)}, u32[]{:S(2)}) copy-start(bf16[2,512,1024]{2,1,0:T(8,128)(2,1)} %all-gather.5.cloned.1.call-done) | copy-start | bytes 6291460
  241.2 4.6 %copy-start.10 = (f32[128,8]{0,1:T(8,128)S(1)}, f32[128,8]{0,1:T(8,128)}, u32[]{:S(2)}) copy-start(f32[128,8]{0,1:T(8,128)} %param.23) | copy-start | bytes 12292
  241.2 32.3 %all-to-all-start.3 = ((bf16[16,64,1024]{2,1,0:T(8,128)(2,1)}), bf16[16,64,1024]{2,1,0:T(8,128)(2,1)}, u32[]{:S(2)}, u32[]{:S(2)}) async-start(bf16[16,64,1024]{2,1,0:T(8,128)(2,1)} %bitcast.102), calls=%async_computation.3 | async-start | bytes 4194304 | tf_op jit(solution)/shard_map/all_to_all | solution.py:176
  277.8 12.0 %copy-start.1 = (bf16[1024,1024]{1,0:T(8,128)(2,1)S(1)}, bf16[1024,1024]{1,0:T(8,128)(2,1)}, u32[]{:S(2)}) copy-start(bf16[1024,1024]{1,0:T(8,128)(2,1)} %param.17) | copy-start | bytes 6291460
Sparse Core Ops, SparseCore 0:
  9.2 41.0 all-gather.2
  52.1 37.3 all-gather.4
where the time goes:
time: 298 us; the launch traced here: 297 us
  waiting for transfers between devices  96.8 us (32%)
  local copies, waits for them, and re-layouts  61 us (20%)
  matrix products  51.1 us (17%)
  blocking collectives  32.2 us (11%)
  starting transfers between devices  23.9 us (8%)
  other arithmetic  17.1 us (6%)
  between operations  14.6 us (5%)
    all_to_all x2, waiting for transfers between devices, shards(): lax.all_to_all(produced.reshape(tp_size, capacity, D), TP, split_axis=0,...  47.8 us
    all_to_all x1, blocking collectives, shards(): lax.all_to_all(send_buffer[:, local], TP, split_axis=0, concat_axis=0, ti...  32.2 us
    all_to_all x2, waiting for transfers between devices, gather_rows(): lax.all_to_all(send, axis_name, split_axis=0, concat_axis=0, tiled=True)  30.3 us
    all_to_all x1, waiting for transfers between devices, shards(): lax.all_to_all(send_buffer[:, local], TP, split_axis=0, concat_axis=0, ti...  17.2 us
    sub x1, matrix products, shards(): weights = jnp.exp(scores - top_score)  13.9 us
    gather x2, local copies, waits for them, and re-layouts, shards(): jnp.take(kv_cache, local_pages, axis=0).reshape(MAX_CACHED, 2 * kv_cols)  12.1 us
    dot_general x1, matrix products, shards(): jnp.einsum('gpqk,kgd->qgpd', probs, values_total, preferred_element_type=...  11.4 us
    dot_general x2, matrix products, shards(): jnp.dot(received, gate_up_full[local], preferred_element_type=jnp.float32)  11.2 us
  transfers between devices with their start and end apart: 9, of which 5 were waited for; matrix products, arithmetic and copies ran while one was open for 38% of the time, Pallas kernels for 0%

commit v1 on v0

--- a/solution.py
+++ b/solution.py
@@ -159,9 +159,14 @@
     earlier = jnp.cumsum(per_token, axis=0) - per_token
     slot_ids = jnp.sum(onehot * earlier[:, None, :], axis=2)
     target = expert_ids * capacity + slot_ids
-    outgoing_rows = jnp.broadcast_to(normed_two[:, None, :], (tok_rows, TOP, D))
-    send_buffer = jnp.zeros((EXPERTS * capacity, D), jnp.bfloat16).at[target].set(outgoing_rows)
-    send_buffer = send_buffer.reshape(tp_size, experts_local, capacity, D)
+    slot_range = jnp.arange(EXPERTS * capacity, dtype=jnp.int32)
+    hits = target[None, :, :] == slot_range[:, None, None]
+    choose = jnp.any(hits, axis=2).astype(jnp.bfloat16)
+    send_buffer = (
+        jnp.dot(choose, normed_two, preferred_element_type=jnp.float32)
+        .astype(jnp.bfloat16)
+        .reshape(tp_size, experts_local, capacity, D)
+    )
     returned = []
     for local in range(experts_local):
         received = lax.all_to_all(
@@ -179,8 +184,15 @@
         )
     returned = jnp.stack(returned, axis=1)
     returned = returned.reshape(EXPERTS * capacity, D)
-    picked = returned[target]
-    mixture = jnp.einsum("tk,tkd->td", gate_weights, picked.astype(jnp.float32))
+    mixing = jnp.sum(
+        jnp.where(hits, gate_weights[None, :, :], 0.0), axis=2
+    ).T
+    mixture = jnp.dot(
+        mixing,
+        returned.astype(jnp.float32),
+        precision=lax.Precision.HIGHEST,
+        preferred_element_type=jnp.float32,
+    )
     return (middle.astype(jnp.float32) + mixture).astype(jnp.bfloat16)
 
 

time: 298 us -> 278 us (0.933)
  local copies, waits for them, and re-layouts: 61 us -> 39.2 us
  other arithmetic: 17.1 us -> 35.9 us
  waiting for transfers between devices: 96.8 us -> 78 us
    reduce_sum x0 -> x1, other arithmetic: none -> 10.8 us  [shards(): mixing = jnp.sum(jnp.where(hits, gate_weights[None, :, :], 0.0), axis=2).T]
    all_to_all x2, waiting for transfers between devices: 47.8 us -> 37 us  [shards(): lax.all_to_all(produced.reshape(tp_size, capacity, D), TP, split_axis=0,...]
    gather x1 -> x0, local copies, waits for them, and re-layouts: 8.9 us -> none  [shards(): picked = returned[target]]
    reduce_or x0 -> x1, other arithmetic: none -> 8.12 us  [shards(): choose = jnp.any(hits, axis=2).astype(jnp.bfloat16)]
    all_to_all x2, waiting for transfers between devices: 30.3 us -> 22.4 us  [gather_rows(): lax.all_to_all(send, axis_name, split_axis=0, concat_axis=0, tiled=True)]
    scatter x1 -> x0, local copies, waits for them, and re-layouts: 7.9 us -> none  [shards(): jnp.zeros((EXPERTS * capacity, D), jnp.bfloat16).at[target]]
  transfers between devices with their start and end apart: 9 -> 9, of which waited for: 5 -> 5; matrix products, arithmetic and copies ran while one was open for 38% -> 44% of each run, Pallas kernels for 0% -> 0%
where the time goes in v1:
time: 278 us; the launch traced here: 277 us
  waiting for transfers between devices  78 us (28%)
  matrix products  52.9 us (19%)
  local copies, waits for them, and re-layouts  39.2 us (14%)
  other arithmetic  35.9 us (13%)
  blocking collectives  32.2 us (12%)
  starting transfers between devices  24 us (9%)
  between operations  14.6 us (5%)
    all_to_all x2, waiting for transfers between devices, shards(): lax.all_to_all(produced.reshape(tp_size, capacity, D), TP, split_axis=0,...  37 us
    all_to_all x1, blocking collectives, shards(): lax.all_to_all(send_buffer[:, local], TP, split_axis=0, concat_axis=0, ti...  32.2 us
    all_to_all x2, waiting for transfers between devices, gather_rows(): lax.all_to_all(send, axis_name, split_axis=0, concat_axis=0, tiled=True)  22.4 us
    all_to_all x1, waiting for transfers between devices, shards(): lax.all_to_all(send_buffer[:, local], TP, split_axis=0, concat_axis=0, ti...  17.1 us
    sub x1, matrix products, shards(): weights = jnp.exp(scores - top_score)  13.9 us
    gather x2, local copies, waits for them, and re-layouts, shards(): jnp.take(kv_cache, local_pages, axis=0).reshape(MAX_CACHED, 2 * kv_cols)  12.1 us
    dot_general x1, matrix products, shards(): jnp.einsum('gpqk,kgd->qgpd', probs, values_total, preferred_element_type=...  11.4 us
    dot_general x2, matrix products, shards(): jnp.dot(received, gate_up_full[local], preferred_element_type=jnp.float32)  11.2 us
  transfers between devices with their start and end apart: 9, of which 5 were waited for; matrix products, arithmetic and copies ran while one was open for 44% of the time, Pallas kernels for 0%

profile of v1, /device:TPU:224, one launch (start us, length us, event | category | flops | bytes accessed | tf_op | source)
XLA Modules:
  0.0 276.7 jit_solution(12495761553405381133)
XLA Ops:
  6.5 0.7 all-gather.3.cloned.1.call-update
  7.3 1.1 fusion.19
  8.4 1.1 fusion.21
  11.9 1.6 broadcast_in_dim.54
  13.6 5.5 %all-to-all-start = ((bf16[8,128,1024]{1,2,0:T(8,128)(2,1)}), bf16[8,128,1024]{1,2,0:T(8,128)(2,1)S(1)}, u32[]{:S(2)}, u32[]{:S(2)}) async-start(bf16[8,128,1024]{1,2,0:T(8,128)(2,1)} %broadcast_in_dim.54), calls=%async_computation | async-start | bytes 4194304 | tf_op jit(solution)/shard_map/all_to_all | solution.py:52
  19.1 0.7 all-gather.5.cloned.1.call-update
  20.7 0.7 iota_compare_fusion.2
  21.4 8.1 %fusion.6 = pred[2048,128]{1,0:T(8,128)(4,1)} fusion(s32[128,8]{0,1:T(8,128)S(1)} %multiply_add_fusion), kind=kLoop, calls=%fused_computation.12 | loop fusion | flops 3932160 | bytes 266240 | tf_op jit(solution)/shard_map/reduce_or | solution.py:164
  29.6 15.5 %all-to-all-done = bf16[8,128,1024]{1,2,0:T(8,128)(2,1)S(1)} async-done(((bf16[8,128,1024]{1,2,0:T(8,128)(2,1)}), bf16[8,128,1024]{1,2,0:T(8,128)(2,1)S(1)}, u32[]{:S(2)}, u32[]{:S(2)}) %all-to-all-start) | async-done | bytes 2097184 | tf_op jit(solution)/shard_map/all_to_all | solution.py:52
  45.1 1.7 broadcast_in_dim.94
  46.8 5.4 %all-to-all-start.1 = ((bf16[16,512,128]{2,1,0:T(8,128)(2,1)}), bf16[16,512,128]{2,1,0:T(8,128)(2,1)}, u32[]{:S(2)}, u32[]{:S(2)}) async-start(bf16[16,512,128]{2,1,0:T(8,128)(2,1)} %broadcast_in_dim.94), calls=%async_computation.1 | async-start | bytes 4194304 | tf_op jit(solution)/shard_map/all_to_all | solution.py:52
  52.3 5.6 %gather_fusion = bf16[16,128,1024]{2,1,0:T(8,128)(2,1)} fusion(bf16[24,128,1024]{2,1,0:T(8,128)(2,1)} %param.19, s32[1024]{0:T(1024)S(1)} %pad_clamp_fusion), kind=kCustom, calls=%fused_computation | custom fusion | bytes 8388672 | tf_op jit(solution)/shard_map/jit(_take)/gather | solution.py:117
  57.9 6.6 %copy.57 = bf16[2048,1024]{0,1:T(8,128)(2,1)} copy(bf16[2048,1024]{1,0:T(8,128)(2,1)} %bitcast.85) | data formatting | bytes 8388608 | tf_op jit(solution)/shard_map/jit(_take)/gather | solution.py:117
  64.4 2.6 broadcast_select_fusion
  67.0 2.4 fusion.41
  69.4 3.5 %compare_select_fusion = pred[128,3072]{0,1:T(8,128)(4,1)} fusion(s32[128]{0:T(128)S(1)} %iota_add_fusion.1, s32[3072]{0:T(1024)S(1)} %iota_add_fusion, pred[3072]{0:T(1024)(128)(4,1)S(1)} %get-tuple-element.27, pred[3072]{0:T(1024)(128)(4,1)S(1)} %get-tuple-element.28), kind=kLoop, calls=%fused_computation.31 | loop fusion | flops 786432 | bytes 412160 | tf_op jit(solution)/shard_map/jit(_where)/select_n | solution.py:131
  72.9 2.6 copy.61
  75.5 6.8 %all-to-all-done.1 = bf16[16,512,128]{2,1,0:T(8,128)(2,1)} async-done(((bf16[16,512,128]{2,1,0:T(8,128)(2,1)}), bf16[16,512,128]{2,1,0:T(8,128)(2,1)}, u32[]{:S(2)}, u32[]{:S(2)}) %all-to-all-start.1) | async-done | bytes 2097184 | tf_op jit(solution)/shard_map/all_to_all | solution.py:52
  82.4 2.7 fusion.42
  85.1 0.8 reshape.222
  85.9 0.8 copy.65
  86.9 3.0 %fusion.43 = (bf16[1024,512]{1,0:T(8,128)(2,1)}, bf16[1024,512]{1,0:T(8,128)(2,1)}) fusion(bf16[1024,1024]{1,0:T(8,128)(2,1)} %bitcast.87), kind=kLoop, calls=%fused_computation.100 | loop fusion | bytes 4194304 | tf_op jit(solution)/shard_map/slice | solution.py:118
  89.9 2.4 copy.62
  92.3 2.3 copy.63
  94.6 4.4 %pad_maximum_fusion.1 = (bf16[3072,512]{0,1:T(8,128)(2,1)}, bf16[3072,512]{0,1:T(8,128)(2,1)}) fusion(bf16[1024,512]{0,1:T(8,128)(2,1)} %copy.62, bf16[2048,512]{0,1:T(8,128)(2,1)} %get-tuple-element.10, bf16[1024,512]{0,1:T(8,128)(2,1)} %copy.63, bf16[2048,512]{0,1:T(8,128)(2,1)S(1)} %copy-done.3), kind=kLoop, calls=%fused_computation.16 | loop fusion | flops 12582912 | bytes 12582912 | tf_op jit(solution)/shard_map/concatenate | solution.py:121
  99.0 1.7 reshape.226
  100.7 0.8 collective-permute-start.1
  101.9 1.7 convolution_add_fusion
  104.0 13.9 %fusion.44 = (f32[8,2,128]{2,1,0:T(2,128)S(1)}, f32[8,2,128,3072]{2,3,1,0:T(8,128)}) fusion(pred[128,3072]{0,1:T(8,128)(4,1)} %compare_select_fusion, bf16[3072,8,64,1]{0,2,3,1:T(8,128)(2,1)} %bitcast.92, bf16[128,8,2,64]{0,3,2,1:T(8,128)(2,1)S(1)} %bitcast.102), kind=kOutput, calls=%fused_computation.101 | convolution fusion | flops 830475264 | bytes 28975104 | tf_op jit(solution)/shard_map/sub | solution.py:138
  117.9 11.4 %fusion.14 = bf16[8,64,2,128]{3,1,2,0:T(8,128)(2,1)S(1)} fusion(bf16[3072,8,64,1]{0,2,3,1:T(8,128)(2,1)} %bitcast.91, f32[8,2,128,3072]{2,3,1,0:T(8,128)} %get-tuple-element.24, f32[8,2,128]{2,1,0:T(2,128)S(1)} %get-tuple-element.23), kind=kOutput, calls=%fused_computation.35 | convolution fusion | flops 818020352 | bytes 28581888 | tf_op jit(solution)/shard_map/gpqk,kgd->qgpd/dot_general | solution.py:141
  129.7 1.6 broadcast_select_fusion.2
  131.5 1.3 convolution_convert_fusion
  132.8 1.8 slice_bitcast_fusion.5
  134.6 32.2 %all_to_all.30 = bf16[16,64,1024]{2,1,0:T(8,128)(2,1)} all-to-all(bf16[16,64,1024]{2,1,0:T(8,128)(2,1)S(1)} %get-tuple-element.7), channel_id=1, replica_groups=mesh['tz'=8,'tc'=2,'ra'=2,'rb'=8] {'ra','rb'}, dimensions={0} | all-to-all | bytes 4194304 | tf_op jit(solution)/shard_map/all_to_all | solution.py:172
  166.8 3.7 %all-to-all-start.4 = ((bf16[16,64,1024]{2,1,0:T(8,128)(2,1)}), bf16[16,64,1024]{2,1,0:T(8,128)(2,1)S(1)}, u32[]{:S(2)}, u32[]{:S(2)}) async-start(bf16[16,64,1024]{2,1,0:T(8,128)(2,1)} %get-tuple-element.8), calls=%async_computation.4 | async-start | bytes 4194304 | tf_op jit(solution)/shard_map/all_to_all | solution.py:172
  170.6 6.5 %fusion.12 = f32[1024,1024]{1,0:T(8,128)} fusion(bf16[1024,1024]{1,0:T(8,128)(2,1)} %bitcast.96, bf16[2,1024,1024]{2,1,0:T(8,128)(2,1)} %all-gather.3.cloned.1.call-done), kind=kOutput, calls=%fused_computation.27 | convolution fusion | flops 2147483648 | bytes 8388608 | tf_op jit(solution)/shard_map/dot_general | solution.py:175
  177.1 5.1 %convolution_convert_fusion.2 = bf16[1024,1024]{1,0:T(8,128)(2,1)} fusion(f32[1024,1024]{1,0:T(8,128)} %fusion.12, bf16[2,512,1024]{2,1,0:T(8,128)(2,1)} %all-gather.5.cloned.1.call-done), kind=kOutput, calls=%fused_computation.30 | convolution fusion | flops 1077936128 | bytes 7340032 | tf_op jit(solution)/shard_map/dot_general | solution.py:177
  182.2 17.1 %all-to-all-done.4 = bf16[16,64,1024]{2,1,0:T(8,128)(2,1)S(1)} async-done(((bf16[16,64,1024]{2,1,0:T(8,128)(2,1)}), bf16[16,64,1024]{2,1,0:T(8,128)(2,1)S(1)}, u32[]{:S(2)}, u32[]{:S(2)}) %all-to-all-start.4) | async-done | bytes 2097184 | tf_op jit(solution)/shard_map/all_to_all | solution.py:172
  199.3 1.3 copy-done.5
  200.7 3.9 %all-to-all-start.3 = ((bf16[16,64,1024]{2,1,0:T(8,128)(2,1)}), bf16[16,64,1024]{2,1,0:T(8,128)(2,1)S(1)}, u32[]{:S(2)}, u32[]{:S(2)}) async-start(bf16[16,64,1024]{2,1,0:T(8,128)(2,1)} %bitcast.94), calls=%async_computation.3 | async-start | bytes 4194304 | tf_op jit(solution)/shard_map/all_to_all | solution.py:181
  204.6 4.7 %fusion.10 = f32[1024,1024]{1,0:T(8,128)S(1)} fusion(bf16[1024,1024]{1,0:T(8,128)(2,1)} %bitcast.93, bf16[2,1024,1024]{2,1,0:T(8,128)(2,1)} %all-gather.3.cloned.1.call-done), kind=kOutput, calls=%fused_computation.22 | convolution fusion | flops 2147483648 | bytes 8388608 | tf_op jit(solution)/shard_map/dot_general | solution.py:175
  209.3 2.6 convolution_convert_fusion.1
  212.0 20.2 %all-to-all-done.3 = bf16[16,64,1024]{2,1,0:T(8,128)(2,1)S(1)} async-done(((bf16[16,64,1024]{2,1,0:T(8,128)(2,1)}), bf16[16,64,1024]{2,1,0:T(8,128)(2,1)S(1)}, u32[]{:S(2)}, u32[]{:S(2)}) %all-to-all-start.3) | async-done | bytes 2097184 | tf_op jit(solution)/shard_map/all_to_all | solution.py:181
  232.1 4.4 %all-to-all-start.5 = ((bf16[16,64,1024]{2,1,0:T(8,128)(2,1)}), bf16[16,64,1024]{2,1,0:T(8,128)(2,1)}, u32[]{:S(2)}, u32[]{:S(2)}) async-start(bf16[16,64,1024]{2,1,0:T(8,128)(2,1)} %bitcast.95), calls=%async_computation.5 | async-start | bytes 4194304 | tf_op jit(solution)/shard_map/all_to_all | solution.py:181
  236.6 10.8 %select_reduce_fusion = f32[2048,128]{1,0:T(8,128)S(1)} fusion(f32[128,8]{0,1:T(8,128)S(1)} %copy-done.10, s32[128,8]{0,1:T(8,128)S(1)} %multiply_add_fusion), kind=kLoop, calls=%fused_computation.10 | loop fusion | flops 6029312 | bytes 1056768 | tf_op jit(solution)/shard_map/reduce_sum | solution.py:187
  247.4 16.9 %all-to-all-done.5 = bf16[16,64,1024]{2,1,0:T(8,128)(2,1)} async-done(((bf16[16,64,1024]{2,1,0:T(8,128)(2,1)}), bf16[16,64,1024]{2,1,0:T(8,128)(2,1)}, u32[]{:S(2)}, u32[]{:S(2)}) %all-to-all-start.5) | async-done | bytes 2097184 | tf_op jit(solution)/shard_map/all_to_all | solution.py:181
  264.3 2.8 pad_maximum_fusion
  267.1 2.8 %fusion.13 = bf16[128,1024]{1,0:T(8,128)(2,1)} fusion(f32[2048,128]{1,0:T(8,128)S(1)} %select_reduce_fusion, bf16[2048,1024]{1,0:T(8,128)(2,1)S(1)} %bitcast.84, bf16[128,1024]{1,0:T(8,128)(2,1)S(1)} %get-tuple-element.6), kind=kOutput, calls=%fused_computation.34 | convolution fusion | flops 3221618688 | bytes 5767168 | tf_op jit(solution)/shard_map/dot_general | solution.py:190
  (76 shorter events, 4.0 us)
Async XLA Ops:
  6.5 2.9 %copy-start = (bf16[1024,1024]{1,0:T(8,128)(2,1)S(1)}, bf16[1024,1024]{1,0:T(8,128)(2,1)}, u32[]{:S(2)}) copy-start(bf16[1024,1024]{1,0:T(8,128)(2,1)} %param.17) | copy-start | bytes 6291460
  6.5 3.6 %copy-start.14 = (s32[2]{0:T(128)S(1)}, s32[2]{0:T(128)}, u32[]{:S(2)}) copy-start(s32[2]{0:T(128)} %param.21) | copy-start | bytes 28
  6.5 164.0 %all-gather.3.cloned.1.call-start = ((), (), s32[]{:S(2)}) async-start(), calls=%async_computation.6 | async-start | bytes 4456448 | tf_op jit(solution)/shard_map/all_gather | solution.py:93
  11.9 7.9 %copy-start.8 = (bf16[1024,64]{0,1:T(8,128)(2,1)S(1)}, bf16[1024,64]{0,1:T(8,128)(2,1)}, u32[]{:S(2)}) copy-start(bf16[1024,64]{0,1:T(8,128)(2,1)} %param.16) | copy-start | bytes 393220
  11.9 8.2 %copy-start.9 = (bf16[64,1024]{1,0:T(8,128)(2,1)S(1)}, bf16[64,1024]{1,0:T(8,128)(2,1)}, u32[]{:S(2)}) copy-start(bf16[64,1024]{1,0:T(8,128)(2,1)} %param.18) | copy-start | bytes 393220
  13.6 6.7 %copy-start.7 = (s32[128,8]{0,1:T(8,128)S(1)}, s32[128,8]{0,1:T(8,128)}, u32[]{:S(2)}) copy-start(s32[128,8]{0,1:T(8,128)} %param.22) | copy-start | bytes 12292
  13.6 7.0 %copy-start.12 = (s32[2,16]{1,0:T(2,128)S(1)}, s32[2,16]{1,0:T(2,128)}, u32[]{:S(2)}) copy-start(s32[2,16]{1,0:T(2,128)} %param.20) | copy-start | bytes 388
  13.6 31.6 %all-to-all-start = ((bf16[8,128,1024]{1,2,0:T(8,128)(2,1)}), bf16[8,128,1024]{1,2,0:T(8,128)(2,1)S(1)}, u32[]{:S(2)}, u32[]{:S(2)}) async-start(bf16[8,128,1024]{1,2,0:T(8,128)(2,1)} %broadcast_in_dim.54), calls=%async_computation | async-start | bytes 4194304 | tf_op jit(solution)/shard_map/all_to_all | solution.py:52
  19.1 158.0 %all-gather.5.cloned.1.call-start = ((), (), s32[]{:S(2)}) async-start(), calls=%async_computation.7 | async-start | bytes 2228224 | tf_op jit(solution)/shard_map/all_gather | solution.py:94
  46.8 35.5 %all-to-all-start.1 = ((bf16[16,512,128]{2,1,0:T(8,128)(2,1)}), bf16[16,512,128]{2,1,0:T(8,128)(2,1)}, u32[]{:S(2)}, u32[]{:S(2)}) async-start(bf16[16,512,128]{2,1,0:T(8,128)(2,1)} %broadcast_in_dim.94), calls=%async_computation.1 | async-start | bytes 4194304 | tf_op jit(solution)/shard_map/all_to_all | solution.py:52
  86.8 15.1 %collective-permute-start = (bf16[512,1024]{0,1:T(8,128)(2,1)S(1)}, bf16[512,1024]{0,1:T(8,128)(2,1)}, u32[]{:S(2)}, u32[]{:S(2)}) collective-permute-start(bf16[512,1024]{0,1:T(8,128)(2,1)S(1)} %bitcast.89), channel_id=1, source_target_pairs={{0,16},{16,0},{1,17},{17,1},{2,18},{18,2},{3,19},{19,3},{4,20},{20... | collective-permute-start | bytes 3145736 | tf_op jit(solution)/shard_map/ppermute | solution.py:92
  89.9 4.7 %copy-start.3 = (bf16[2048,512]{0,1:T(8,128)(2,1)S(1)}, bf16[2048,512]{0,1:T(8,128)(2,1)}, u32[]{:S(2)}) copy-start(bf16[2048,512]{0,1:T(8,128)(2,1)} %get-tuple-element.9) | copy-start | bytes 6291460
  100.7 29.0 %collective-permute-start.1 = (bf16[1024,512]{1,0:T(8,128)(2,1)S(1)}, bf16[1024,512]{1,0:T(8,128)(2,1)}, u32[]{:S(2)}, u32[]{:S(2)}) collective-permute-start(bf16[1024,512]{1,0:T(8,128)(2,1)S(1)} %reshape.226), channel_id=1, source_target_pairs={{0,16},{16,0},{1,17},{17,1},{2,18},{18,2},{3,19},{19,3},{4,20},{20... | collective-permute-start | bytes 3145736 | tf_op jit(solution)/shard_map/ppermute | solution.py:92
  129.3 2.0 copy-start.4
  129.3 2.1 copy-start.6
  129.3 2.1 copy-start.11
  166.8 32.5 %all-to-all-start.4 = ((bf16[16,64,1024]{2,1,0:T(8,128)(2,1)}), bf16[16,64,1024]{2,1,0:T(8,128)(2,1)S(1)}, u32[]{:S(2)}, u32[]{:S(2)}) async-start(bf16[16,64,1024]{2,1,0:T(8,128)(2,1)} %get-tuple-element.8), calls=%async_computation.4 | async-start | bytes 4194304 | tf_op jit(solution)/shard_map/all_to_all | solution.py:172
  199.3 1.3 copy-start.5
  200.7 31.5 %all-to-all-start.3 = ((bf16[16,64,1024]{2,1,0:T(8,128)(2,1)}), bf16[16,64,1024]{2,1,0:T(8,128)(2,1)S(1)}, u32[]{:S(2)}, u32[]{:S(2)}) async-start(bf16[16,64,1024]{2,1,0:T(8,128)(2,1)} %bitcast.94), calls=%async_computation.3 | async-start | bytes 4194304 | tf_op jit(solution)/shard_map/all_to_all | solution.py:181
  204.6 4.7 %copy-start.13 = (bf16[2,512,1024]{2,1,0:T(8,128)(2,1)S(1)}, bf16[2,512,1024]{2,1,0:T(8,128)(2,1)}, u32[]{:S(2)}) copy-start(bf16[2,512,1024]{2,1,0:T(8,128)(2,1)} %all-gather.5.cloned.1.call-done) | copy-start | bytes 6291460
  212.0 24.6 %copy-start.10 = (f32[128,8]{0,1:T(8,128)S(1)}, f32[128,8]{0,1:T(8,128)}, u32[]{:S(2)}) copy-start(f32[128,8]{0,1:T(8,128)} %param.23) | copy-start | bytes 12292
  232.1 32.1 %copy-start.2 = (bf16[16,64,1024]{2,1,0:T(8,128)(2,1)}, bf16[16,64,1024]{2,1,0:T(8,128)(2,1)S(1)}, u32[]{:S(2)}) copy-start(bf16[16,64,1024]{2,1,0:T(8,128)(2,1)S(1)} %all-to-all-done.3) | copy-start | bytes 6291460
  232.1 32.1 %all-to-all-start.5 = ((bf16[16,64,1024]{2,1,0:T(8,128)(2,1)}), bf16[16,64,1024]{2,1,0:T(8,128)(2,1)}, u32[]{:S(2)}, u32[]{:S(2)}) async-start(bf16[16,64,1024]{2,1,0:T(8,128)(2,1)} %bitcast.95), calls=%async_computation.5 | async-start | bytes 4194304 | tf_op jit(solution)/shard_map/all_to_all | solution.py:181
  264.3 5.5 %copy-start.1 = (bf16[1024,1024]{1,0:T(8,128)(2,1)S(1)}, bf16[1024,1024]{1,0:T(8,128)(2,1)}, u32[]{:S(2)}) copy-start(bf16[1024,1024]{1,0:T(8,128)(2,1)} %param.17) | copy-start | bytes 6291460
Sparse Core Ops, SparseCore 0:
  9.2 41.0 all-gather.2
  52.1 37.3 all-gather.4

commit v2 on v1

--- a/solution.py
+++ b/solution.py
@@ -1,6 +1,8 @@
 import jax
 import jax.numpy as jnp
 from jax import lax
+from jax.experimental import pallas as pl
+from jax.experimental.pallas import tpu as pltpu
 from jax.sharding import Mesh
 from jax.sharding import PartitionSpec as P
 
@@ -45,6 +47,48 @@
         [leading * cosine - trailing * sine_part, trailing * cosine + leading * sine_part], axis=-1
     )
     return turned.reshape(row_count, -1)
+
+
+def attention_kernel(meta, q_ref, kc_ref, vc_ref, kn_ref, vn_ref, o_ref):
+    length = meta[0]
+    first_query = meta[1]
+    query = q_ref[0]
+    rows = query.shape[0]
+    contract = (((1,), (1,)), ((), ()))
+    s_old = lax.dot_general(query, kc_ref[0], contract, preferred_element_type=jnp.float32) * ATTN_SCALE
+    s_new = lax.dot_general(query, kn_ref[0], contract, preferred_element_type=jnp.float32) * ATTN_SCALE
+    old_index = lax.broadcasted_iota(jnp.int32, s_old.shape, 1)
+    s_old = jnp.where(old_index < length, s_old, -1e30)
+    new_index = lax.broadcasted_iota(jnp.int32, s_new.shape, 1)
+    query_index = lax.broadcasted_iota(jnp.int32, s_new.shape, 0) % (rows // 2) + first_query
+    s_new = jnp.where(new_index <= query_index, s_new, -1e30)
+    top = jnp.maximum(jnp.max(s_old, axis=1, keepdims=True), jnp.max(s_new, axis=1, keepdims=True))
+    e_old = jnp.exp(s_old - top)
+    e_new = jnp.exp(s_new - top)
+    total = jnp.sum(e_old, axis=1, keepdims=True) + jnp.sum(e_new, axis=1, keepdims=True)
+    p_old = (e_old / total).astype(jnp.bfloat16)
+    p_new = (e_new / total).astype(jnp.bfloat16)
+    mixed = jnp.dot(p_old, vc_ref[0], preferred_element_type=jnp.float32) + jnp.dot(
+        p_new, vn_ref[0], preferred_element_type=jnp.float32
+    )
+    o_ref[0] = mixed.astype(o_ref.dtype)
+
+
+def attend(meta, q, kc, vc, kn, vn):
+    groups, rows, _ = q.shape
+    old = kc.shape[1]
+    new = kn.shape[1]
+    spec = lambda n: pl.BlockSpec((1, n, HEAD_DIM), lambda c, m: (c, 0, 0))
+    return pl.pallas_call(
+        attention_kernel,
+        grid_spec=pltpu.PrefetchScalarGridSpec(
+            num_scalar_prefetch=1,
+            grid=(groups,),
+            in_specs=[spec(rows), spec(old), spec(old), spec(new), spec(new)],
+            out_specs=spec(rows),
+        ),
+        out_shape=jax.ShapeDtypeStruct(q.shape, jnp.bfloat16),
+    )(meta, q, kc, vc, kn, vn)
 
 
 def gather_rows(piece, axis_name, count):
@@ -115,31 +159,21 @@
 
     local_pages = page_table[local_req] - lax.axis_index(TOK) * kv_cache.shape[0]
     cached = jnp.take(kv_cache, local_pages, axis=0).reshape(MAX_CACHED, 2 * kv_cols)
-    keys_total = jnp.concatenate([cached[:, :kv_cols], request_kv[:, :kv_cols]], axis=0).reshape(
-        MAX_CACHED + NEW, KV_HEADS, HEAD_DIM
-    )
-    values_total = jnp.concatenate(
-        [cached[:, kv_cols:], request_kv[:, kv_cols:]], axis=0
-    ).reshape(MAX_CACHED + NEW, KV_HEADS, HEAD_DIM)
-    grouped_q = queries.reshape(tok_rows, KV_HEADS, group_size, HEAD_DIM)
-    scores = (
-        jnp.einsum("qgpd,kgd->gpqk", grouped_q, keys_total, preferred_element_type=jnp.float32)
-        * ATTN_SCALE
-    )
-    key_index = jnp.arange(MAX_CACHED + NEW, dtype=jnp.int32)
-    query_pos = block * tok_rows + jnp.arange(tok_rows, dtype=jnp.int32)
-    allowed = jnp.where(
-        key_index[None, :] < MAX_CACHED,
-        key_index[None, :] < length,
-        key_index[None, :] - MAX_CACHED <= query_pos[:, None],
-    )
-    scores = jnp.where(allowed, scores, -1e30)
-    top_score = jnp.max(scores, axis=-1, keepdims=True)
-    weights = jnp.exp(scores - top_score)
-    probs = (weights / jnp.sum(weights, axis=-1, keepdims=True)).astype(jnp.bfloat16)
+    def heads_major(rows):
+        return rows.reshape(rows.shape[0], 2, KV_HEADS, HEAD_DIM).transpose(1, 2, 0, 3)
+
+    cached_heads = heads_major(cached)
+    new_heads = heads_major(request_kv)
+    grouped_q = (
+        queries.reshape(tok_rows, KV_HEADS, group_size, HEAD_DIM)
+        .transpose(1, 2, 0, 3)
+        .reshape(KV_HEADS, group_size * tok_rows, HEAD_DIM)
+    )
+    meta = jnp.stack([length, block * tok_rows]).astype(jnp.int32)
+    mixed = attend(meta, grouped_q, cached_heads[0], cached_heads[1], new_heads[0], new_heads[1])
     attended = (
-        jnp.einsum("gpqk,kgd->qgpd", probs, values_total, preferred_element_type=jnp.float32)
-        .astype(jnp.bfloat16)
+        mixed.reshape(KV_HEADS, group_size, tok_rows, HEAD_DIM)
+        .transpose(2, 0, 1, 3)
         .reshape(tok_rows, HEADS * HEAD_DIM)
     )
     out_mine = jnp.dot(attended, wo_mine, preferred_element_type=jnp.float32)

time: 278 us -> 270 us (0.971)
  matrix products: 52.9 us -> 27.6 us
  waiting for transfers between devices: 78 us -> 60.9 us
  Pallas kernels: 0 us -> 16.9 us
  local copies, waits for them, and re-layouts: 39.2 us -> 55.7 us
  other arithmetic: 35.9 us -> 32.6 us
    all_to_all x2, waiting for transfers between devices: 22.4 us -> 5.46 us  [gather_rows(): lax.all_to_all(send, axis_name, split_axis=0, concat_axis=0, tiled=True)]
    pallas_call x0 -> x1, Pallas kernels: none -> 16.9 us  [attend(): pl.pallas_call(attention_kernel, grid_spec=pltpu.PrefetchScalarGridSpec(n...]
    sub x1 -> x0, matrix products: 13.9 us -> none  [shards(): weights = jnp.exp(scores - top_score)]
    dot_general x1 -> x0, matrix products: 11.4 us -> none  [shards(): jnp.einsum('gpqk,kgd->qgpd', probs, values_total, preferred_element_type=...]
    squeeze x0 -> x2, local copies, waits for them, and re-layouts: none -> 10.5 us  [the longest x1 5.83 us: shards(): cached_heads[1]]
    slice x4 -> x0, local copies, waits for them, and re-layouts: 10 us -> none  [the longest x2 5.26 us: shards(): request_kv[:, :kv_cols]]
    transpose x0 -> x1, other arithmetic: none -> 9.28 us  [heads_major(): rows.reshape(rows.shape[0], 2, KV_HEADS, HEAD_DIM).transpose(1, 2, 0, 3)]
    another operation x0 -> x2, local copies, waits for them, and re-layouts: none -> 5.98 us  [heads_major(): rows.reshape(rows.shape[0], 2, KV_HEADS, HEAD_DIM).transpose(1, 2, 0, 3)]
  transfers between devices with their start and end apart: 9 -> 9, of which waited for: 5 -> 5; matrix products, arithmetic and copies ran while one was open for 44% -> 41% of each run, Pallas kernels for 0% -> 6%
where the time goes in v2:
time: 270 us; the launch traced here: 269 us
  waiting for transfers between devices  60.9 us (23%)
  local copies, waits for them, and re-layouts  55.7 us (21%)
  blocking collectives  34.3 us (13%)
  other arithmetic  32.6 us (12%)
  matrix products  27.6 us (10%)
  starting transfers between devices  26 us (10%)
  Pallas kernels  16.9 us (6%)
  between operations  14.6 us (5%)
    all_to_all x2, waiting for transfers between devices, shards(): lax.all_to_all(produced.reshape(tp_size, capacity, D), TP, split_axis=0,...  36.7 us
    all_to_all x1, blocking collectives, shards(): lax.all_to_all(send_buffer[:, local], TP, split_axis=0, concat_axis=0, ti...  34.3 us
    all_to_all x1, waiting for transfers between devices, shards(): lax.all_to_all(send_buffer[:, local], TP, split_axis=0, concat_axis=0, ti...  17.3 us
    gather x2, local copies, waits for them, and re-layouts, shards(): jnp.take(kv_cache, local_pages, axis=0).reshape(MAX_CACHED, 2 * kv_cols)  17.3 us
    pallas_call x1, Pallas kernels, attend(): pl.pallas_call(attention_kernel, grid_spec=pltpu.PrefetchScalarGridSpec(n...  16.9 us
    all_to_all x2, starting transfers between devices, gather_rows(): lax.all_to_all(send, axis_name, split_axis=0, concat_axis=0, tiled=True)  12.8 us
    dot_general x2, matrix products, shards(): jnp.dot(received, gate_up_full[local], preferred_element_type=jnp.float32)  11.2 us
    reduce_sum x1, other arithmetic, shards(): mixing = jnp.sum(jnp.where(hits, gate_weights[None, :, :], 0.0), axis=2).T  10.8 us
  transfers between devices with their start and end apart: 9, of which 5 were waited for; matrix products, arithmetic and copies ran while one was open for 41% of the time, Pallas kernels for 6%

profile of v2, /device:TPU:224, one launch (start us, length us, event | category | flops | bytes accessed | tf_op | source)
XLA Modules:
  0.0 268.5 jit_solution(4859802891994195510)
XLA Ops:
  6.5 0.7 all-gather.3.cloned.1.call-update
  7.3 0.8 constant_dynamic-slice_fusion.1
  8.2 0.9 constant_dynamic-slice_fusion.2
  9.3 1.8 broadcast_in_dim.26
  11.1 7.2 %all-to-all-start = ((bf16[16,512,128]{2,1,0:T(8,128)(2,1)}), bf16[16,512,128]{2,1,0:T(8,128)(2,1)}, u32[]{:S(2)}, u32[]{:S(2)}) async-start(bf16[16,512,128]{2,1,0:T(8,128)(2,1)} %broadcast_in_dim.26), calls=%async_computation | async-start | bytes 4194304 | tf_op jit(solution)/shard_map/all_to_all | solution.py:96
  18.4 0.7 all-gather.5.cloned.1.call-update
  19.4 0.4 fusion.32
  19.9 0.7 dynamic_slice.18
  20.6 5.5 %gather_fusion = bf16[16,128,1024]{2,1,0:T(8,128)(2,1)} fusion(bf16[24,128,1024]{2,1,0:T(8,128)(2,1)} %param.19, s32[1024]{0:T(1024)S(1)} %pad_clamp_fusion), kind=kCustom, calls=%fused_computation | custom fusion | bytes 8388672 | tf_op jit(solution)/shard_map/jit(_take)/gather | solution.py:161
  26.2 11.7 %reshape.215 = bf16[2048,2,8,64]{3,2,1,0:T(8,128)(2,1)} reshape(bf16[16,128,1024]{2,1,0:T(8,128)(2,1)} %gather_fusion) | data formatting | bytes 8388608 | tf_op jit(solution)/shard_map/jit(_take)/gather | solution.py:161
  39.4 9.3 %fusion = bf16[2,8,2048,64]{3,2,1,0:T(8,128)(2,1)} fusion(bf16[2048,2,8,64]{3,2,1,0:T(8,128)(2,1)} %reshape.215, pred[2048]{0:T(1024)(128)(4,1)S(1)} %broadcast_bitcast_fusion), kind=kLoop, calls=%fused_computation.2 | loop fusion | flops 2097152 | bytes 8390656 | tf_op jit(solution)/shard_map/transpose | solution.py:163
  48.8 1.6 broadcast_in_dim.31
  50.4 5.6 %all-to-all-start.1 = ((bf16[8,128,1024]{1,2,0:T(8,128)(2,1)}), bf16[8,128,1024]{1,2,0:T(8,128)(2,1)}, u32[]{:S(2)}, u32[]{:S(2)}) async-start(bf16[8,128,1024]{1,2,0:T(8,128)(2,1)} %broadcast_in_dim.31), calls=%async_computation.1 | async-start | bytes 4194304 | tf_op jit(solution)/shard_map/all_to_all | solution.py:96
  56.3 1.4 pad_add_fusion.meta
  57.7 5.8 %slice_bitcast_fusion = (bf16[8,2048,64]{2,1,0:T(8,128)(2,1)}, bf16[8,2048,64]{2,1,0:T(8,128)(2,1)}) fusion(bf16[2,8,2048,64]{3,2,1,0:T(8,128)(2,1)} %fusion), kind=kLoop, calls=%fused_computation.6 | loop fusion | bytes 8388608 | tf_op jit(solution)/shard_map/squeeze | solution.py:173
  63.5 2.8 %fusion.31 = (bf16[16,256,128]{2,1,0:T(8,128)(2,1)}, bf16[16,256,128]{2,1,0:T(8,128)(2,1)S(1)}) fusion(bf16[16,512,128]{2,1,0:T(8,128)(2,1)} %all-to-all-done), kind=kLoop, calls=%fused_computation.84 | loop fusion | bytes 4194304 | tf_op jit(solution)/shard_map/slice | solution.py:135
  66.3 0.8 reshape.193
  67.1 0.8 copy.48
  68.3 8.1 %fusion.1 = pred[2048,128]{1,0:T(8,128)(4,1)} fusion(s32[128,8]{0,1:T(8,128)S(1)} %multiply_add_fusion), kind=kLoop, calls=%fused_computation.5 | loop fusion | flops 3932160 | bytes 266240 | tf_op jit(solution)/shard_map/reduce_or | solution.py:198
  76.4 5.4 %all-to-all-done.1 = bf16[8,128,1024]{1,2,0:T(8,128)(2,1)} async-done(((bf16[8,128,1024]{1,2,0:T(8,128)(2,1)}), bf16[8,128,1024]{1,2,0:T(8,128)(2,1)}, u32[]{:S(2)}, u32[]{:S(2)}) %all-to-all-start.1) | async-done | bytes 2097184 | tf_op jit(solution)/shard_map/all_to_all | solution.py:96
  81.8 4.3 %copy.56 = bf16[8,128,1024]{1,0,2:T(8,128)(2,1)} copy(bf16[8,128,1024]{1,2,0:T(8,128)(2,1)} %all-to-all-done.1) | data formatting | bytes 4194304 | tf_op jit(solution)/shard_map/all_to_all | solution.py:96
  86.1 2.8 %reshape_reshape.4 = bf16[1024,2,8,64]{0,3,2,1:T(8,128)(2,1)S(1)} reshape(bf16[8,128,1024]{1,0,2:T(8,128)(2,1)} %copy.56) | data formatting | bytes 4194304 | tf_op jit(solution)/shard_map/reshape;reshape | solution.py:163
  88.9 3.2 %copy.57 = bf16[1024,2,8,64]{3,0,2,1:T(8,128)(2,1)} copy(bf16[1024,2,8,64]{0,3,2,1:T(8,128)(2,1)S(1)} %reshape_reshape.4) | data formatting | bytes 4194304 | tf_op jit(solution)/shard_map/reshape;reshape | solution.py:163
  92.0 4.7 %slice_bitcast_fusion.8 = (bf16[8,1024,64]{2,1,0:T(8,128)(2,1)}, bf16[8,1024,64]{2,1,0:T(8,128)(2,1)}) fusion(bf16[2,8,1024,64]{3,2,1,0:T(8,128)(2,1)} %bitcast.75), kind=kLoop, calls=%fused_computation.20 | loop fusion | bytes 4194304 | tf_op jit(solution)/shard_map/squeeze | solution.py:173
  96.7 0.6 reshape.200
  97.7 0.5 fusion.22
  98.2 1.7 convolution_add_fusion
  100.2 1.0 copy.50
  101.3 16.9 %shard_map.127 = bf16[8,256,64]{2,1,0:T(8,128)(2,1)} custom-call(s32[2]{0:T(128)} %pad_add_fusion.meta, bf16[8,256,64]{2,1,0:T(8,128)(2,1)} %bitcast.87, bf16[8,2048,64]{2,1,0:T(8,128)(2,1)} %get-tuple-element.8.kc_ref, bf16[8,2048,64]{2,1,0:T(8,128)(2,1)} %get-tuple-element.7.vc_ref, bf16[8,1024,64]{2,1,0:T(8,128)(2,1)} %get-tuple-element.12.kn_ref, ...), custom_call_target="tpu_custom_call" | custom-call | tf_op jit(solution)/shard_map/pallas_call | solution.py:82
  118.2 1.3 copy.58
  119.8 1.6 broadcast_select_fusion.1
  121.6 1.3 convolution_convert_fusion
  122.9 1.9 slice_bitcast_fusion.7
  124.8 34.3 %all_to_all.30 = bf16[16,64,1024]{2,1,0:T(8,128)(2,1)} all-to-all(bf16[16,64,1024]{2,1,0:T(8,128)(2,1)S(1)} %get-tuple-element.10), channel_id=1, replica_groups=mesh['tz'=8,'tc'=2,'ra'=2,'rb'=8] {'ra','rb'}, dimensions={0} | all-to-all | bytes 4194304 | tf_op jit(solution)/shard_map/all_to_all | solution.py:206
  159.1 3.7 %all-to-all-start.2 = ((bf16[16,64,1024]{2,1,0:T(8,128)(2,1)}), bf16[16,64,1024]{2,1,0:T(8,128)(2,1)S(1)}, u32[]{:S(2)}, u32[]{:S(2)}) async-start(bf16[16,64,1024]{2,1,0:T(8,128)(2,1)} %get-tuple-element.9), calls=%async_computation.2 | async-start | bytes 4194304 | tf_op jit(solution)/shard_map/all_to_all | solution.py:206
  162.8 6.5 %fusion.3 = f32[1024,1024]{1,0:T(8,128)} fusion(bf16[1024,1024]{1,0:T(8,128)(2,1)} %bitcast.85, bf16[2,1024,1024]{2,1,0:T(8,128)(2,1)} %all-gather.3.cloned.1.call-done), kind=kOutput, calls=%fused_computation.13 | convolution fusion | flops 2147483648 | bytes 8388608 | tf_op jit(solution)/shard_map/dot_general | solution.py:209
  169.4 5.1 %convolution_convert_fusion.1 = bf16[1024,1024]{1,0:T(8,128)(2,1)} fusion(f32[1024,1024]{1,0:T(8,128)} %fusion.3, bf16[2,512,1024]{2,1,0:T(8,128)(2,1)} %all-gather.5.cloned.1.call-done), kind=kOutput, calls=%fused_computation.22 | convolution fusion | flops 1077936128 | bytes 7340032 | tf_op jit(solution)/shard_map/dot_general | solution.py:211
  174.5 17.3 %all-to-all-done.2 = bf16[16,64,1024]{2,1,0:T(8,128)(2,1)S(1)} async-done(((bf16[16,64,1024]{2,1,0:T(8,128)(2,1)}), bf16[16,64,1024]{2,1,0:T(8,128)(2,1)S(1)}, u32[]{:S(2)}, u32[]{:S(2)}) %all-to-all-start.2) | async-done | bytes 2097184 | tf_op jit(solution)/shard_map/all_to_all | solution.py:206
  191.8 1.3 copy-done.5
  193.2 4.0 %all-to-all-start.5 = ((bf16[16,64,1024]{2,1,0:T(8,128)(2,1)}), bf16[16,64,1024]{2,1,0:T(8,128)(2,1)S(1)}, u32[]{:S(2)}, u32[]{:S(2)}) async-start(bf16[16,64,1024]{2,1,0:T(8,128)(2,1)} %bitcast.83), calls=%async_computation.5 | async-start | bytes 4194304 | tf_op jit(solution)/shard_map/all_to_all | solution.py:215
  197.2 4.7 %fusion.5 = f32[1024,1024]{1,0:T(8,128)S(1)} fusion(bf16[1024,1024]{1,0:T(8,128)(2,1)} %bitcast.82, bf16[2,1024,1024]{2,1,0:T(8,128)(2,1)} %all-gather.3.cloned.1.call-done), kind=kOutput, calls=%fused_computation.18 | convolution fusion | flops 2147483648 | bytes 8388608 | tf_op jit(solution)/shard_map/dot_general | solution.py:209
  201.9 2.6 convolution_convert_fusion.2
  204.5 20.2 %all-to-all-done.5 = bf16[16,64,1024]{2,1,0:T(8,128)(2,1)S(1)} async-done(((bf16[16,64,1024]{2,1,0:T(8,128)(2,1)}), bf16[16,64,1024]{2,1,0:T(8,128)(2,1)S(1)}, u32[]{:S(2)}, u32[]{:S(2)}) %all-to-all-start.5) | async-done | bytes 2097184 | tf_op jit(solution)/shard_map/all_to_all | solution.py:215
  224.7 4.8 %all-to-all-start.3 = ((bf16[16,64,1024]{2,1,0:T(8,128)(2,1)}), bf16[16,64,1024]{2,1,0:T(8,128)(2,1)}, u32[]{:S(2)}, u32[]{:S(2)}) async-start(bf16[16,64,1024]{2,1,0:T(8,128)(2,1)} %bitcast.84), calls=%async_computation.3 | async-start | bytes 4194304 | tf_op jit(solution)/shard_map/all_to_all | solution.py:215
  229.6 10.8 %select_reduce_fusion = f32[2048,128]{1,0:T(8,128)S(1)} fusion(f32[128,8]{0,1:T(8,128)S(1)} %copy-done.9, s32[128,8]{0,1:T(8,128)S(1)} %multiply_add_fusion), kind=kLoop, calls=%fused_computation.3 | loop fusion | flops 6029312 | bytes 1056768 | tf_op jit(solution)/shard_map/reduce_sum | solution.py:221
  240.4 16.5 %all-to-all-done.3 = bf16[16,64,1024]{2,1,0:T(8,128)(2,1)} async-done(((bf16[16,64,1024]{2,1,0:T(8,128)(2,1)}), bf16[16,64,1024]{2,1,0:T(8,128)(2,1)}, u32[]{:S(2)}, u32[]{:S(2)}) %all-to-all-start.3) | async-done | bytes 2097184 | tf_op jit(solution)/shard_map/all_to_all | solution.py:215
  256.9 2.0 pad_maximum_fusion
  258.9 2.8 %fusion.6 = bf16[128,1024]{1,0:T(8,128)(2,1)} fusion(f32[2048,128]{1,0:T(8,128)S(1)} %select_reduce_fusion, bf16[2048,1024]{1,0:T(8,128)(2,1)S(1)} %bitcast.74, bf16[128,1024]{1,0:T(8,128)(2,1)S(1)} %get-tuple-element.6), kind=kOutput, calls=%fused_computation.26 | convolution fusion | flops 3221618688 | bytes 5767168 | tf_op jit(solution)/shard_map/dot_general | solution.py:224
  (71 shorter events, 3.3 us)
Async XLA Ops:
  6.5 12.9 %copy-start = (bf16[1024,1024]{1,0:T(8,128)(2,1)S(1)}, bf16[1024,1024]{1,0:T(8,128)(2,1)}, u32[]{:S(2)}) copy-start(bf16[1024,1024]{1,0:T(8,128)(2,1)} %param.17) | copy-start | bytes 6291460
  6.5 156.3 %all-gather.3.cloned.1.call-start = ((), (), s32[]{:S(2)}) async-start(), calls=%async_computation.6 | async-start | bytes 4456448 | tf_op jit(solution)/shard_map/all_gather | solution.py:137
  11.1 8.0 %copy-start.3 = (bf16[128,1024]{1,0:T(8,128)(2,1)S(1)}, bf16[128,1024]{1,0:T(8,128)(2,1)}, u32[]{:S(2)}) copy-start(bf16[128,1024]{1,0:T(8,128)(2,1)} %param.13) | copy-start | bytes 786436
  11.1 8.2 %copy-start.8 = (f32[1024]{0:T(1024)S(1)}, f32[1024]{0:T(1024)}, u32[]{:S(2)}) copy-start(f32[1024]{0:T(1024)} %param.14) | copy-start | bytes 12292
  11.1 37.7 %all-to-all-start = ((bf16[16,512,128]{2,1,0:T(8,128)(2,1)}), bf16[16,512,128]{2,1,0:T(8,128)(2,1)}, u32[]{:S(2)}, u32[]{:S(2)}) async-start(bf16[16,512,128]{2,1,0:T(8,128)(2,1)} %broadcast_in_dim.26), calls=%async_computation | async-start | bytes 4194304 | tf_op jit(solution)/shard_map/all_to_all | solution.py:96
  18.3 151.0 %all-gather.5.cloned.1.call-start = ((), (), s32[]{:S(2)}) async-start(), calls=%async_computation.7 | async-start | bytes 2228224 | tf_op jit(solution)/shard_map/all_gather | solution.py:138
  19.2 0.7 copy-start.13
  19.3 1.4 copy-start.11
  50.4 5.6 %copy-start.7 = (s32[128,8]{0,1:T(8,128)S(1)}, s32[128,8]{0,1:T(8,128)}, u32[]{:S(2)}) copy-start(s32[128,8]{0,1:T(8,128)} %param.22) | copy-start | bytes 12292
  50.4 31.4 %all-to-all-start.1 = ((bf16[8,128,1024]{1,2,0:T(8,128)(2,1)}), bf16[8,128,1024]{1,2,0:T(8,128)(2,1)}, u32[]{:S(2)}, u32[]{:S(2)}) async-start(bf16[8,128,1024]{1,2,0:T(8,128)(2,1)} %broadcast_in_dim.31), calls=%async_computation.1 | async-start | bytes 4194304 | tf_op jit(solution)/shard_map/all_to_all | solution.py:96
  68.0 30.2 %collective-permute-start = (bf16[512,1024]{0,1:T(8,128)(2,1)S(1)}, bf16[512,1024]{0,1:T(8,128)(2,1)}, u32[]{:S(2)}, u32[]{:S(2)}) collective-permute-start(bf16[512,1024]{0,1:T(8,128)(2,1)S(1)} %bitcast.78), channel_id=1, source_target_pairs={{0,16},{16,0},{1,17},{17,1},{2,18},{18,2},{3,19},{19,3},{4,20},{20... | collective-permute-start | bytes 3145736 | tf_op jit(solution)/shard_map/ppermute | solution.py:136
  92.0 4.7 %copy-start.2 = (bf16[16,256,128]{2,1,0:T(8,128)(2,1)S(1)}, bf16[16,256,128]{2,1,0:T(8,128)(2,1)}, u32[]{:S(2)}) copy-start(bf16[16,256,128]{2,1,0:T(8,128)(2,1)} %get-tuple-element.13) | copy-start | bytes 3145732
  97.4 22.4 %collective-permute-start.1 = (bf16[1024,512]{1,0:T(8,128)(2,1)S(1)}, bf16[1024,512]{1,0:T(8,128)(2,1)}, u32[]{:S(2)}, u32[]{:S(2)}) collective-permute-start(bf16[1024,512]{1,0:T(8,128)(2,1)S(1)} %reshape.200), channel_id=1, source_target_pairs={{0,16},{16,0},{1,17},{17,1},{2,18},{18,2},{3,19},{19,3},{4,20},{20... | collective-permute-start | bytes 3145736 | tf_op jit(solution)/shard_map/ppermute | solution.py:136
  118.2 3.2 %copy-start.4 = (bf16[128,1024]{1,0:T(8,128)(2,1)S(1)}, bf16[128,1024]{1,0:T(8,128)(2,1)}, u32[]{:S(2)}) copy-start(bf16[128,1024]{1,0:T(8,128)(2,1)} %param.13) | copy-start | bytes 786436
  119.5 2.1 copy-start.6
  119.5 2.1 copy-start.10
  159.1 32.7 %all-to-all-start.2 = ((bf16[16,64,1024]{2,1,0:T(8,128)(2,1)}), bf16[16,64,1024]{2,1,0:T(8,128)(2,1)S(1)}, u32[]{:S(2)}, u32[]{:S(2)}) async-start(bf16[16,64,1024]{2,1,0:T(8,128)(2,1)} %get-tuple-element.9), calls=%async_computation.2 | async-start | bytes 4194304 | tf_op jit(solution)/shard_map/all_to_all | solution.py:206
  191.8 1.3 copy-start.5
  193.2 31.6 %all-to-all-start.5 = ((bf16[16,64,1024]{2,1,0:T(8,128)(2,1)}), bf16[16,64,1024]{2,1,0:T(8,128)(2,1)S(1)}, u32[]{:S(2)}, u32[]{:S(2)}) async-start(bf16[16,64,1024]{2,1,0:T(8,128)(2,1)} %bitcast.83), calls=%async_computation.5 | async-start | bytes 4194304 | tf_op jit(solution)/shard_map/all_to_all | solution.py:215
  197.2 4.7 %copy-start.12 = (bf16[2,512,1024]{2,1,0:T(8,128)(2,1)S(1)}, bf16[2,512,1024]{2,1,0:T(8,128)(2,1)}, u32[]{:S(2)}) copy-start(bf16[2,512,1024]{2,1,0:T(8,128)(2,1)} %all-gather.5.cloned.1.call-done) | copy-start | bytes 6291460
  224.7 4.9 %copy-start.9 = (f32[128,8]{0,1:T(8,128)S(1)}, f32[128,8]{0,1:T(8,128)}, u32[]{:S(2)}) copy-start(f32[128,8]{0,1:T(8,128)} %param.23) | copy-start | bytes 12292
  224.7 32.2 %all-to-all-start.3 = ((bf16[16,64,1024]{2,1,0:T(8,128)(2,1)}), bf16[16,64,1024]{2,1,0:T(8,128)(2,1)}, u32[]{:S(2)}, u32[]{:S(2)}) async-start(bf16[16,64,1024]{2,1,0:T(8,128)(2,1)} %bitcast.84), calls=%async_computation.3 | async-start | bytes 4194304 | tf_op jit(solution)/shard_map/all_to_all | solution.py:215
  258.9 2.8 %copy-start.1 = (bf16[1024,1024]{1,0:T(8,128)(2,1)S(1)}, bf16[1024,1024]{1,0:T(8,128)(2,1)}, u32[]{:S(2)}) copy-start(bf16[1024,1024]{1,0:T(8,128)(2,1)} %param.17) | copy-start | bytes 6291460
Sparse Core Ops, SparseCore 0:
  9.2 41.0 all-gather.2
  52.1 37.4 all-gather.4

commit v3 on v2

--- a/solution.py
+++ b/solution.py
@@ -55,8 +55,8 @@
     query = q_ref[0]
     rows = query.shape[0]
     contract = (((1,), (1,)), ((), ()))
-    s_old = lax.dot_general(query, kc_ref[0], contract, preferred_element_type=jnp.float32) * ATTN_SCALE
-    s_new = lax.dot_general(query, kn_ref[0], contract, preferred_element_type=jnp.float32) * ATTN_SCALE
+    s_old = lax.dot_general(query, kc_ref[...], contract, preferred_element_type=jnp.float32) * ATTN_SCALE
+    s_new = lax.dot_general(query, kn_ref[...], contract, preferred_element_type=jnp.float32) * ATTN_SCALE
     old_index = lax.broadcasted_iota(jnp.int32, s_old.shape, 1)
     s_old = jnp.where(old_index < length, s_old, -1e30)
     new_index = lax.broadcasted_iota(jnp.int32, s_new.shape, 1)
@@ -68,24 +68,28 @@
     total = jnp.sum(e_old, axis=1, keepdims=True) + jnp.sum(e_new, axis=1, keepdims=True)
     p_old = (e_old / total).astype(jnp.bfloat16)
     p_new = (e_new / total).astype(jnp.bfloat16)
-    mixed = jnp.dot(p_old, vc_ref[0], preferred_element_type=jnp.float32) + jnp.dot(
-        p_new, vn_ref[0], preferred_element_type=jnp.float32
+    mixed = jnp.dot(p_old, vc_ref[...], preferred_element_type=jnp.float32) + jnp.dot(
+        p_new, vn_ref[...], preferred_element_type=jnp.float32
     )
     o_ref[0] = mixed.astype(o_ref.dtype)
 
 
 def attend(meta, q, kc, vc, kn, vn):
     groups, rows, _ = q.shape
-    old = kc.shape[1]
-    new = kn.shape[1]
-    spec = lambda n: pl.BlockSpec((1, n, HEAD_DIM), lambda c, m: (c, 0, 0))
+    old = kc.shape[0]
+    new = kn.shape[0]
+    lanes = 2 * HEAD_DIM
+    values_at = KV_HEADS * HEAD_DIM // lanes
+    spec = pl.BlockSpec((1, rows, lanes), lambda c, m: (c, 0, 0))
+    keys = lambda n: pl.BlockSpec((n, lanes), lambda c, m: (0, c // 2))
+    values = lambda n: pl.BlockSpec((n, lanes), lambda c, m: (0, values_at + c // 2))
     return pl.pallas_call(
         attention_kernel,
         grid_spec=pltpu.PrefetchScalarGridSpec(
             num_scalar_prefetch=1,
             grid=(groups,),
-            in_specs=[spec(rows), spec(old), spec(old), spec(new), spec(new)],
-            out_specs=spec(rows),
+            in_specs=[spec, keys(old), values(old), keys(new), values(new)],
+            out_specs=spec,
         ),
         out_shape=jax.ShapeDtypeStruct(q.shape, jnp.bfloat16),
     )(meta, q, kc, vc, kn, vn)
@@ -159,20 +163,21 @@
 
     local_pages = page_table[local_req] - lax.axis_index(TOK) * kv_cache.shape[0]
     cached = jnp.take(kv_cache, local_pages, axis=0).reshape(MAX_CACHED, 2 * kv_cols)
-    def heads_major(rows):
-        return rows.reshape(rows.shape[0], 2, KV_HEADS, HEAD_DIM).transpose(1, 2, 0, 3)
-
-    cached_heads = heads_major(cached)
-    new_heads = heads_major(request_kv)
     grouped_q = (
         queries.reshape(tok_rows, KV_HEADS, group_size, HEAD_DIM)
         .transpose(1, 2, 0, 3)
         .reshape(KV_HEADS, group_size * tok_rows, HEAD_DIM)
     )
+    blank = jnp.zeros_like(grouped_q)
+    odd = (jnp.arange(KV_HEADS) % 2 == 1)[:, None, None]
+    padded_q = jnp.concatenate(
+        [jnp.where(odd, blank, grouped_q), jnp.where(odd, grouped_q, blank)], axis=2
+    )
     meta = jnp.stack([length, block * tok_rows]).astype(jnp.int32)
-    mixed = attend(meta, grouped_q, cached_heads[0], cached_heads[1], new_heads[0], new_heads[1])
+    mixed = attend(meta, padded_q, cached, cached, request_kv, request_kv)
     attended = (
-        mixed.reshape(KV_HEADS, group_size, tok_rows, HEAD_DIM)
+        jnp.where(odd, mixed[:, :, HEAD_DIM:], mixed[:, :, :HEAD_DIM])
+        .reshape(KV_HEADS, group_size, tok_rows, HEAD_DIM)
         .transpose(2, 0, 1, 3)
         .reshape(tok_rows, HEADS * HEAD_DIM)
     )

time: 270 us -> 248 us (0.919)
  local copies, waits for them, and re-layouts: 55.7 us -> 26.3 us
  waiting for transfers between devices: 60.9 us -> 73.9 us
  other arithmetic: 32.6 us -> 29.9 us
    all_to_all x2, waiting for transfers between devices: 5.46 us -> 18.4 us  [gather_rows(): lax.all_to_all(send, axis_name, split_axis=0, concat_axis=0, tiled=True)]
    gather x2 -> x1, local copies, waits for them, and re-layouts: 17.3 us -> 5.57 us  [shards(): jnp.take(kv_cache, local_pages, axis=0).reshape(MAX_CACHED, 2 * kv_cols)]
    squeeze x2 -> x0, local copies, waits for them, and re-layouts: 10.5 us -> none  [the longest x1 5.83 us: shards(): cached_heads[1]]
    transpose x1 -> x0, other arithmetic: 9.28 us -> none  [heads_major(): rows.reshape(rows.shape[0], 2, KV_HEADS, HEAD_DIM).transpose(1, 2, 0, 3)]
    another operation x2 -> x0, local copies, waits for them, and re-layouts: 5.98 us -> none  [heads_major(): rows.reshape(rows.shape[0], 2, KV_HEADS, HEAD_DIM).transpose(1, 2, 0, 3)]
    all_to_all x1 -> x0, local copies, waits for them, and re-layouts: 4.3 us -> none  [gather_rows(): lax.all_to_all(send, axis_name, split_axis=0, concat_axis=0, tiled=True)]
    select_n x1 -> x2, other arithmetic: 0.01 us -> 3.93 us  [shards(): jnp.take(kv_cache, local_pages, axis=0).reshape(MAX_CACHED, 2 * kv_cols)]
  transfers between devices with their start and end apart: 9 -> 9, of which waited for: 5 -> 4; matrix products, arithmetic and copies ran while one was open for 41% -> 31% of each run, Pallas kernels for 6% -> 7%
where the time goes in v3:
time: 248 us; the launch traced here: 247 us
  waiting for transfers between devices  73.9 us (30%)
  blocking collectives  34 us (14%)
  other arithmetic  29.9 us (12%)
  matrix products  27.6 us (11%)
  local copies, waits for them, and re-layouts  26.3 us (11%)
  starting transfers between devices  23.9 us (10%)
  Pallas kernels  17 us (7%)
  between operations  14.6 us (6%)
    all_to_all x2, waiting for transfers between devices, shards(): lax.all_to_all(produced.reshape(tp_size, capacity, D), TP, split_axis=0,...  37 us
    all_to_all x1, blocking collectives, shards(): lax.all_to_all(send_buffer[:, local], TP, split_axis=0, concat_axis=0, ti...  34 us
    all_to_all x2, waiting for transfers between devices, gather_rows(): lax.all_to_all(send, axis_name, split_axis=0, concat_axis=0, tiled=True)  18.4 us
    all_to_all x1, waiting for transfers between devices, shards(): lax.all_to_all(send_buffer[:, local], TP, split_axis=0, concat_axis=0, ti...  17 us
    pallas_call x1, Pallas kernels, attend(): pl.pallas_call(attention_kernel, grid_spec=pltpu.PrefetchScalarGridSpec(n...  17 us
    dot_general x2, matrix products, shards(): jnp.dot(received, gate_up_full[local], preferred_element_type=jnp.float32)  11.2 us
    all_to_all x2, starting transfers between devices, gather_rows(): lax.all_to_all(send, axis_name, split_axis=0, concat_axis=0, tiled=True)  10.8 us
    reduce_sum x1, other arithmetic, shards(): mixing = jnp.sum(jnp.where(hits, gate_weights[None, :, :], 0.0), axis=2).T  10.8 us
  transfers between devices with their start and end apart: 9, of which 4 were waited for; matrix products, arithmetic and copies ran while one was open for 31% of the time, Pallas kernels for 7%

profile of v3, /device:TPU:224, one launch (start us, length us, event | category | flops | bytes accessed | tf_op | source)
XLA Modules:
  0.0 247.3 jit_solution(15189198262751416515)
XLA Ops:
  6.5 0.7 all-gather.3.cloned.1.call-update
  7.3 0.8 constant_dynamic-slice_fusion.2
  8.4 0.9 constant_dynamic-slice_fusion.1
  9.3 1.8 broadcast_in_dim.80
  11.1 7.2 %all-to-all-start = ((bf16[16,512,128]{2,1,0:T(8,128)(2,1)}), bf16[16,512,128]{2,1,0:T(8,128)(2,1)}, u32[]{:S(2)}, u32[]{:S(2)}) async-start(bf16[16,512,128]{2,1,0:T(8,128)(2,1)} %broadcast_in_dim.80), calls=%async_computation | async-start | bytes 4194304 | tf_op jit(solution)/shard_map/all_to_all | solution.py:100
  18.3 0.7 all-gather.5.cloned.1.call-update
  19.4 0.6 dynamic_slice.18
  20.6 0.4 fusion.32
  22.2 8.1 %fusion = pred[2048,128]{1,0:T(8,128)(4,1)} fusion(s32[128,8]{0,1:T(8,128)S(1)} %multiply_add_fusion), kind=kLoop, calls=%fused_computation.3 | loop fusion | flops 3932160 | bytes 266240 | tf_op jit(solution)/shard_map/reduce_or | solution.py:203
  30.4 18.4 %all-to-all-done = bf16[16,512,128]{2,1,0:T(8,128)(2,1)} async-done(((bf16[16,512,128]{2,1,0:T(8,128)(2,1)}), bf16[16,512,128]{2,1,0:T(8,128)(2,1)}, u32[]{:S(2)}, u32[]{:S(2)}) %all-to-all-start) | async-done | bytes 2097184 | tf_op jit(solution)/shard_map/all_to_all | solution.py:100
  48.7 1.6 broadcast_in_dim.85
  50.3 3.6 %all-to-all-start.1 = ((bf16[8,128,1024]{2,1,0:T(8,128)(2,1)}), bf16[8,128,1024]{2,1,0:T(8,128)(2,1)S(1)}, u32[]{:S(2)}, u32[]{:S(2)}) async-start(bf16[8,128,1024]{2,1,0:T(8,128)(2,1)} %broadcast_in_dim.85), calls=%async_computation.1 | async-start | bytes 4194304 | tf_op jit(solution)/shard_map/all_to_all | solution.py:100
  53.9 2.7 %fusion.31 = (bf16[16,256,128]{2,1,0:T(8,128)(2,1)}, bf16[16,256,128]{2,1,0:T(8,128)(2,1)S(1)}) fusion(bf16[16,512,128]{2,1,0:T(8,128)(2,1)} %all-to-all-done), kind=kLoop, calls=%fused_computation.85 | loop fusion | bytes 4194304 | tf_op jit(solution)/shard_map/slice | solution.py:139
  56.7 1.8 reshape.207
  58.5 1.9 copy.29
  60.5 5.6 %gather_fusion = bf16[16,128,1024]{2,1,0:T(8,128)(2,1)} fusion(bf16[24,128,1024]{2,1,0:T(8,128)(2,1)} %param.19, s32[1024]{0:T(1024)S(1)} %pad_clamp_fusion), kind=kCustom, calls=%fused_computation | custom fusion | bytes 8388672 | tf_op jit(solution)/shard_map/jit(_take)/gather | solution.py:165
  66.1 1.3 pad_add_fusion.meta
  67.4 3.9 %bitcast_select_fusion.kc_ref.vc_ref = bf16[2048,1024]{1,0:T(8,128)(2,1)} fusion(bf16[16,128,1024]{2,1,0:T(8,128)(2,1)} %gather_fusion, pred[2048]{0:T(1024)(128)(4,1)S(1)} %broadcast_bitcast_fusion), kind=kLoop, calls=%fused_computation.5 | loop fusion | flops 2097152 | bytes 8390656 | tf_op jit(solution)/shard_map/jit(_take)/select_n | solution.py:165
  71.3 2.5 %reshape.215 = bf16[1024,512]{1,0:T(8,128)(2,1)} reshape(bf16[16,256,128]{2,1,0:T(8,128)(2,1)} %get-tuple-element.9) | data formatting | bytes 2097152 | tf_op jit(solution)/shard_map/reshape | solution.py:139
  73.8 0.6 collective-permute-start.1
  74.4 0.5 fusion.21
  74.9 1.7 convolution_add_fusion
  76.6 0.2 copy.30
  76.9 0.3 copy.31
  77.3 1.1 pad_maximum_fusion.1.q_ref
  78.4 1.4 copy-done.2
  79.8 17.0 %shard_map.127 = bf16[8,256,128]{2,1,0:T(8,128)(2,1)} custom-call(s32[2]{0:T(128)} %pad_add_fusion.meta, bf16[8,256,128]{2,1,0:T(8,128)(2,1)} %pad_maximum_fusion.1.q_ref, bf16[2048,1024]{1,0:T(8,128)(2,1)} %bitcast_select_fusion.kc_ref.vc_ref, bf16[2048,1024]{1,0:T(8,128)(2,1)} %bitcast_select_fusion.kc_ref.vc_ref, bf16[1024,1024]{1,0:T(8,128)(2,1)} %bitcast.65, ...), custom_call_target="tpu_custom_call" | custom-call | tf_op jit(solution)/shard_map/pallas_call | solution.py:86
  96.8 1.5 slice_select_fusion
  98.3 0.2 copy.34
  98.6 0.3 fusion.33
  98.9 1.6 broadcast_select_fusion.1
  100.7 1.3 convolution_convert_fusion
  102.0 1.9 slice_bitcast_fusion.5
  103.9 34.0 %all_to_all.30 = bf16[16,64,1024]{2,1,0:T(8,128)(2,1)} all-to-all(bf16[16,64,1024]{2,1,0:T(8,128)(2,1)S(1)} %get-tuple-element.7), channel_id=1, replica_groups=mesh['tz'=8,'tc'=2,'ra'=2,'rb'=8] {'ra','rb'}, dimensions={0} | all-to-all | bytes 4194304 | tf_op jit(solution)/shard_map/all_to_all | solution.py:211
  137.9 3.9 %all-to-all-start.4 = ((bf16[16,64,1024]{2,1,0:T(8,128)(2,1)}), bf16[16,64,1024]{2,1,0:T(8,128)(2,1)S(1)}, u32[]{:S(2)}, u32[]{:S(2)}) async-start(bf16[16,64,1024]{2,1,0:T(8,128)(2,1)} %get-tuple-element.8), calls=%async_computation.4 | async-start | bytes 4194304 | tf_op jit(solution)/shard_map/all_to_all | solution.py:211
  141.8 6.5 %fusion.4 = f32[1024,1024]{1,0:T(8,128)} fusion(bf16[1024,1024]{1,0:T(8,128)(2,1)} %bitcast.78, bf16[2,1024,1024]{2,1,0:T(8,128)(2,1)} %all-gather.3.cloned.1.call-done), kind=kOutput, calls=%fused_computation.15 | convolution fusion | flops 2147483648 | bytes 8388608 | tf_op jit(solution)/shard_map/dot_general | solution.py:214
  148.3 5.2 %convolution_convert_fusion.2 = bf16[1024,1024]{1,0:T(8,128)(2,1)} fusion(f32[1024,1024]{1,0:T(8,128)} %fusion.4, bf16[2,512,1024]{2,1,0:T(8,128)(2,1)} %all-gather.5.cloned.1.call-done), kind=kOutput, calls=%fused_computation.18 | convolution fusion | flops 1077936128 | bytes 7340032 | tf_op jit(solution)/shard_map/dot_general | solution.py:216
  153.5 17.0 %all-to-all-done.4 = bf16[16,64,1024]{2,1,0:T(8,128)(2,1)S(1)} async-done(((bf16[16,64,1024]{2,1,0:T(8,128)(2,1)}), bf16[16,64,1024]{2,1,0:T(8,128)(2,1)S(1)}, u32[]{:S(2)}, u32[]{:S(2)}) %all-to-all-start.4) | async-done | bytes 2097184 | tf_op jit(solution)/shard_map/all_to_all | solution.py:211
  170.5 1.3 copy-done.6
  171.9 3.7 %all-to-all-start.3 = ((bf16[16,64,1024]{2,1,0:T(8,128)(2,1)}), bf16[16,64,1024]{2,1,0:T(8,128)(2,1)S(1)}, u32[]{:S(2)}, u32[]{:S(2)}) async-start(bf16[16,64,1024]{2,1,0:T(8,128)(2,1)} %bitcast.76), calls=%async_computation.3 | async-start | bytes 4194304 | tf_op jit(solution)/shard_map/all_to_all | solution.py:220
  175.6 4.7 %fusion.2 = f32[1024,1024]{1,0:T(8,128)S(1)} fusion(bf16[1024,1024]{1,0:T(8,128)(2,1)} %bitcast.75, bf16[2,1024,1024]{2,1,0:T(8,128)(2,1)} %all-gather.3.cloned.1.call-done), kind=kOutput, calls=%fused_computation.10 | convolution fusion | flops 2147483648 | bytes 8388608 | tf_op jit(solution)/shard_map/dot_general | solution.py:214
  180.3 2.6 %convolution_convert_fusion.1 = bf16[1024,1024]{1,0:T(8,128)(2,1)} fusion(f32[1024,1024]{1,0:T(8,128)S(1)} %fusion.2, bf16[2,512,1024]{2,1,0:T(8,128)(2,1)S(1)} %copy-done.13), kind=kOutput, calls=%fused_computation.17 | convolution fusion | flops 1077936128 | bytes 7340032 | tf_op jit(solution)/shard_map/dot_general | solution.py:216
  183.0 20.3 %all-to-all-done.3 = bf16[16,64,1024]{2,1,0:T(8,128)(2,1)S(1)} async-done(((bf16[16,64,1024]{2,1,0:T(8,128)(2,1)}), bf16[16,64,1024]{2,1,0:T(8,128)(2,1)S(1)}, u32[]{:S(2)}, u32[]{:S(2)}) %all-to-all-start.3) | async-done | bytes 2097184 | tf_op jit(solution)/shard_map/all_to_all | solution.py:220
  203.3 4.8 %all-to-all-start.5 = ((bf16[16,64,1024]{2,1,0:T(8,128)(2,1)}), bf16[16,64,1024]{2,1,0:T(8,128)(2,1)}, u32[]{:S(2)}, u32[]{:S(2)}) async-start(bf16[16,64,1024]{2,1,0:T(8,128)(2,1)} %bitcast.77), calls=%async_computation.5 | async-start | bytes 4194304 | tf_op jit(solution)/shard_map/all_to_all | solution.py:220
  208.1 10.8 %select_reduce_fusion = f32[2048,128]{1,0:T(8,128)S(1)} fusion(f32[128,8]{0,1:T(8,128)S(1)} %copy-done.10, s32[128,8]{0,1:T(8,128)S(1)} %multiply_add_fusion), kind=kLoop, calls=%fused_computation.1 | loop fusion | flops 6029312 | bytes 1056768 | tf_op jit(solution)/shard_map/reduce_sum | solution.py:226
  218.9 16.7 %all-to-all-done.5 = bf16[16,64,1024]{2,1,0:T(8,128)(2,1)} async-done(((bf16[16,64,1024]{2,1,0:T(8,128)(2,1)}), bf16[16,64,1024]{2,1,0:T(8,128)(2,1)}, u32[]{:S(2)}, u32[]{:S(2)}) %all-to-all-start.5) | async-done | bytes 2097184 | tf_op jit(solution)/shard_map/all_to_all | solution.py:220
  235.7 2.0 pad_maximum_fusion
  237.6 2.8 %fusion.5 = bf16[128,1024]{1,0:T(8,128)(2,1)} fusion(f32[2048,128]{1,0:T(8,128)S(1)} %select_reduce_fusion, bf16[2048,1024]{1,0:T(8,128)(2,1)S(1)} %bitcast.68, bf16[128,1024]{1,0:T(8,128)(2,1)S(1)} %get-tuple-element.6), kind=kOutput, calls=%fused_computation.21 | convolution fusion | flops 3221618688 | bytes 5767168 | tf_op jit(solution)/shard_map/dot_general | solution.py:229
  (70 shorter events, 2.2 us)
Async XLA Ops:
  6.5 14.1 %copy-start = (bf16[1024,1024]{1,0:T(8,128)(2,1)S(1)}, bf16[1024,1024]{1,0:T(8,128)(2,1)}, u32[]{:S(2)}) copy-start(bf16[1024,1024]{1,0:T(8,128)(2,1)} %param.17) | copy-start | bytes 6291460
  6.5 135.2 %all-gather.3.cloned.1.call-start = ((), (), s32[]{:S(2)}) async-start(), calls=%async_computation.6 | async-start | bytes 4456448 | tf_op jit(solution)/shard_map/all_gather | solution.py:141
  11.0 8.0 %copy-start.4 = (bf16[128,1024]{1,0:T(8,128)(2,1)S(1)}, bf16[128,1024]{1,0:T(8,128)(2,1)}, u32[]{:S(2)}) copy-start(bf16[128,1024]{1,0:T(8,128)(2,1)} %param.13) | copy-start | bytes 786436
  11.1 8.2 %copy-start.9 = (f32[1024]{0:T(1024)S(1)}, f32[1024]{0:T(1024)}, u32[]{:S(2)}) copy-start(f32[1024]{0:T(1024)} %param.14) | copy-start | bytes 12292
  11.1 8.3 %copy-start.14 = (s32[2]{0:T(128)S(1)}, s32[2]{0:T(128)}, u32[]{:S(2)}) copy-start(s32[2]{0:T(128)} %param.21) | copy-start | bytes 28
  11.1 37.7 %all-to-all-start = ((bf16[16,512,128]{2,1,0:T(8,128)(2,1)}), bf16[16,512,128]{2,1,0:T(8,128)(2,1)}, u32[]{:S(2)}, u32[]{:S(2)}) async-start(bf16[16,512,128]{2,1,0:T(8,128)(2,1)} %broadcast_in_dim.80), calls=%async_computation | async-start | bytes 4194304 | tf_op jit(solution)/shard_map/all_to_all | solution.py:100
  18.3 130.0 %all-gather.5.cloned.1.call-start = ((), (), s32[]{:S(2)}) async-start(), calls=%async_computation.7 | async-start | bytes 2228224 | tf_op jit(solution)/shard_map/all_gather | solution.py:142
  20.6 1.0 copy-start.8
  21.1 0.9 copy-start.12
  50.3 28.1 %all-to-all-start.1 = ((bf16[8,128,1024]{2,1,0:T(8,128)(2,1)}), bf16[8,128,1024]{2,1,0:T(8,128)(2,1)S(1)}, u32[]{:S(2)}, u32[]{:S(2)}) async-start(bf16[8,128,1024]{2,1,0:T(8,128)(2,1)} %broadcast_in_dim.85), calls=%async_computation.1 | async-start | bytes 4194304 | tf_op jit(solution)/shard_map/all_to_all | solution.py:100
  60.4 14.4 %collective-permute-start = (bf16[512,1024]{0,1:T(8,128)(2,1)S(1)}, bf16[512,1024]{0,1:T(8,128)(2,1)}, u32[]{:S(2)}, u32[]{:S(2)}) collective-permute-start(bf16[512,1024]{0,1:T(8,128)(2,1)S(1)} %bitcast.71), channel_id=1, source_target_pairs={{0,16},{16,0},{1,17},{17,1},{2,18},{18,2},{3,19},{19,3},{4,20},{20... | collective-permute-start | bytes 3145736 | tf_op jit(solution)/shard_map/ppermute | solution.py:140
  73.8 25.1 %collective-permute-start.1 = (bf16[1024,512]{1,0:T(8,128)(2,1)}, bf16[1024,512]{1,0:T(8,128)(2,1)}, u32[]{:S(2)}, u32[]{:S(2)}) collective-permute-start(bf16[1024,512]{1,0:T(8,128)(2,1)} %reshape.215), channel_id=1, source_target_pairs={{0,16},{16,0},{1,17},{17,1},{2,18},{18,2},{3,19},{19,3},{4,20},{20... | collective-permute-start | bytes 3145736 | tf_op jit(solution)/shard_map/ppermute | solution.py:140
  78.4 1.4 copy-start.2
  96.8 1.7 copy-start.3
  98.3 2.2 copy-start.5
  98.5 2.1 copy-start.7
  98.6 2.1 copy-start.11
  137.9 32.6 %all-to-all-start.4 = ((bf16[16,64,1024]{2,1,0:T(8,128)(2,1)}), bf16[16,64,1024]{2,1,0:T(8,128)(2,1)S(1)}, u32[]{:S(2)}, u32[]{:S(2)}) async-start(bf16[16,64,1024]{2,1,0:T(8,128)(2,1)} %get-tuple-element.8), calls=%async_computation.4 | async-start | bytes 4194304 | tf_op jit(solution)/shard_map/all_to_all | solution.py:211
  170.5 1.3 copy-start.6
  171.9 31.4 %all-to-all-start.3 = ((bf16[16,64,1024]{2,1,0:T(8,128)(2,1)}), bf16[16,64,1024]{2,1,0:T(8,128)(2,1)S(1)}, u32[]{:S(2)}, u32[]{:S(2)}) async-start(bf16[16,64,1024]{2,1,0:T(8,128)(2,1)} %bitcast.76), calls=%async_computation.3 | async-start | bytes 4194304 | tf_op jit(solution)/shard_map/all_to_all | solution.py:220
  175.6 4.7 %copy-start.13 = (bf16[2,512,1024]{2,1,0:T(8,128)(2,1)S(1)}, bf16[2,512,1024]{2,1,0:T(8,128)(2,1)}, u32[]{:S(2)}) copy-start(bf16[2,512,1024]{2,1,0:T(8,128)(2,1)} %all-gather.5.cloned.1.call-done) | copy-start | bytes 6291460
  203.3 4.8 %copy-start.10 = (f32[128,8]{0,1:T(8,128)S(1)}, f32[128,8]{0,1:T(8,128)}, u32[]{:S(2)}) copy-start(f32[128,8]{0,1:T(8,128)} %param.23) | copy-start | bytes 12292
  203.3 32.4 %all-to-all-start.5 = ((bf16[16,64,1024]{2,1,0:T(8,128)(2,1)}), bf16[16,64,1024]{2,1,0:T(8,128)(2,1)}, u32[]{:S(2)}, u32[]{:S(2)}) async-start(bf16[16,64,1024]{2,1,0:T(8,128)(2,1)} %bitcast.77), calls=%async_computation.5 | async-start | bytes 4194304 | tf_op jit(solution)/shard_map/all_to_all | solution.py:220
  237.6 2.8 %copy-start.1 = (bf16[1024,1024]{1,0:T(8,128)(2,1)S(1)}, bf16[1024,1024]{1,0:T(8,128)(2,1)}, u32[]{:S(2)}) copy-start(bf16[1024,1024]{1,0:T(8,128)(2,1)} %param.17) | copy-start | bytes 6291460
Sparse Core Ops, SparseCore 0:
  9.2 40.9 all-gather.2
  52.0 37.6 all-gather.4

commit v4 on v3

--- a/solution.py
+++ b/solution.py
@@ -126,18 +126,6 @@
     half_rows = D // 2
     wq_half = lax.dynamic_slice_in_dim(w_query, core * half_rows, half_rows, 0)
     wo_half = lax.dynamic_slice_in_dim(w_out, core * half_rows, half_rows, 1)
-    lanes = 128
-    pieces = gather_rows(
-        jnp.concatenate([wq_half.reshape(-1, lanes), wo_half.reshape(-1, lanes)], axis=0),
-        TP,
-        tp_size,
-    )
-    q_rows = wq_half.size // lanes
-    wq_mine = jnp.transpose(
-        pieces[:, :q_rows].reshape(tp_size, half_rows, HEAD_DIM), (1, 0, 2)
-    ).reshape(half_rows, D)
-    wo_mine = pieces[:, q_rows:].reshape(D, half_rows)
-    wq_other, wo_other = lax.ppermute((wq_mine, wo_mine), "tc", [(0, 1), (1, 0)])
     gate_up_full = lax.all_gather(w_gate_up, TOK, axis=1, tiled=True)
     down_full = lax.all_gather(w_down, TOK, axis=1, tiled=True)
 
@@ -148,7 +136,24 @@
     new_kv = jnp.concatenate(
         [rotate(keyval[:, :kv_cols], positions), keyval[:, kv_cols:]], axis=1
     ).astype(jnp.bfloat16)
-    request_kv = gather_rows(new_kv, "rb", lax.axis_size("rb")).reshape(NEW, 2 * kv_cols)
+    group = lax.axis_size("rb")
+    packed = jnp.concatenate([new_kv, wq_half.reshape(-1, D), wo_half.reshape(-1, D)], axis=0)
+    got = gather_rows(packed, "rb", group)
+    request_kv = got[:, :tok_rows].reshape(NEW, 2 * kv_cols)
+    weight_rows = wq_half.size // D
+    wq_near = got[:, tok_rows : tok_rows + weight_rows].reshape(group, half_rows, HEAD_DIM)
+    wo_near = got[:, tok_rows + weight_rows :].reshape(group, HEAD_DIM, half_rows)
+    wq_far, wo_far = lax.ppermute((wq_near, wo_near), "ra", [(0, 1), (1, 0)])
+    lead = local_req == 0
+    wq_all = jnp.where(
+        lead, jnp.concatenate([wq_near, wq_far]), jnp.concatenate([wq_far, wq_near])
+    )
+    wo_all = jnp.where(
+        lead, jnp.concatenate([wo_near, wo_far]), jnp.concatenate([wo_far, wo_near])
+    )
+    wq_mine = jnp.transpose(wq_all, (1, 0, 2)).reshape(half_rows, D)
+    wo_mine = wo_all.reshape(D, half_rows)
+    wq_other, wo_other = lax.ppermute((wq_mine, wo_mine), "tc", [(0, 1), (1, 0)])
     other_core = 1 - core
     q_wide = jnp.dot(
         lax.dynamic_slice_in_dim(normed, core * half_rows, half_rows, 1),

time: 248 us -> 275 us (1.11)
  waiting for transfers between devices: 73.9 us -> 102 us
  local copies, waits for them, and re-layouts: 26.3 us -> 21.2 us
  other arithmetic: 29.9 us -> 34.1 us
    all_to_all x2 -> x1, waiting for transfers between devices: 18.4 us -> 36.1 us  [gather_rows(): lax.all_to_all(send, axis_name, split_axis=0, concat_axis=0, tiled=True)]
    ppermute x0 -> x2, waiting for transfers between devices: none -> 10.2 us  [shards(): wq_far, wo_far = lax.ppermute((wq_near, wo_near), 'ra', [(0, 1), (1, 0)])]
    ppermute x0 -> x2, starting transfers between devices: none -> 5.63 us  [shards(): wq_far, wo_far = lax.ppermute((wq_near, wo_near), 'ra', [(0, 1), (1, 0)])]
    all_to_all x2 -> x1, starting transfers between devices: 10.8 us -> 5.53 us  [gather_rows(): lax.all_to_all(send, axis_name, split_axis=0, concat_axis=0, tiled=True)]
    reshape x4 -> x6, local copies, waits for them, and re-layouts: 4.49 us -> 1.45 us  [the longest x2 0.99 us: shards(): got[:, tok_rows:tok_rows + weight_rows].reshape(group, half_rows, HEAD_DIM)]
  transfers between devices with their start and end apart: 9 -> 10, of which waited for: 4 -> 6; matrix products, arithmetic and copies ran while one was open for 31% -> 28% of each run, Pallas kernels for 7% -> 6%
where the time goes in v4:
time: 275 us
  waiting for transfers between devices  102 us (37%)
  blocking collectives  34.2 us (12%)
  other arithmetic  34.1 us (12%)
  matrix products  27.7 us (10%)
  starting transfers between devices  24.1 us (9%)
  local copies, waits for them, and re-layouts  21.2 us (8%)
  Pallas kernels  17 us (6%)
  between operations  14.6 us (5%)
    all_to_all x2, waiting for transfers between devices, shards(): lax.all_to_all(produced.reshape(tp_size, capacity, D), TP, split_axis=0,...  36.7 us
    all_to_all x1, waiting for transfers between devices, gather_rows(): lax.all_to_all(send, axis_name, split_axis=0, concat_axis=0, tiled=True)  36.1 us
    all_to_all x1, blocking collectives, shards(): lax.all_to_all(send_buffer[:, local], TP, split_axis=0, concat_axis=0, ti...  34.2 us
    all_to_all x1, waiting for transfers between devices, shards(): lax.all_to_all(send_buffer[:, local], TP, split_axis=0, concat_axis=0, ti...  17.3 us
    pallas_call x1, Pallas kernels, attend(): pl.pallas_call(attention_kernel, grid_spec=pltpu.PrefetchScalarGridSpec(n...  17 us
    dot_general x2, matrix products, shards(): jnp.dot(received, gate_up_full[local], preferred_element_type=jnp.float32)  11.2 us
    reduce_sum x1, other arithmetic, shards(): mixing = jnp.sum(jnp.where(hits, gate_weights[None, :, :], 0.0), axis=2).T  10.8 us
    ppermute x2, waiting for transfers between devices, shards(): wq_far, wo_far = lax.ppermute((wq_near, wo_near), 'ra', [(0, 1), (1, 0)])  10.2 us
  transfers between devices with their start and end apart: 10, of which 6 were waited for; matrix products, arithmetic and copies ran while one was open for 28% of the time, Pallas kernels for 6%

profile of v4, /device:TPU:224, one launch (start us, length us, event | category | flops | bytes accessed | tf_op | source)
XLA Modules:
  0.0 274.6 jit_solution(12904124674894043759)
XLA Ops:
  6.5 0.7 all-gather.3.cloned.1.call-update
  7.3 1.1 fusion.11
  8.4 1.1 fusion.13
  9.5 0.4 fusion.37
  10.1 0.6 dynamic_slice.18
  12.2 2.1 broadcast_in_dim.74
  14.3 5.5 %all-to-all-start = ((bf16[8,192,1024]{2,1,0:T(8,128)(2,1)}), bf16[8,192,1024]{2,1,0:T(8,128)(2,1)}, u32[]{:S(2)}, u32[]{:S(2)}) async-start(bf16[8,192,1024]{2,1,0:T(8,128)(2,1)} %broadcast_in_dim.74), calls=%async_computation | async-start | bytes 6291456 | tf_op jit(solution)/shard_map/all_to_all | solution.py:100
  19.9 0.7 all-gather.5.cloned.1.call-update
  21.1 36.1 %all-to-all-done = bf16[8,192,1024]{2,1,0:T(8,128)(2,1)} async-done(((bf16[8,192,1024]{2,1,0:T(8,128)(2,1)}), bf16[8,192,1024]{2,1,0:T(8,128)(2,1)}, u32[]{:S(2)}, u32[]{:S(2)}) %all-to-all-start) | async-done | bytes 3145760 | tf_op jit(solution)/shard_map/all_to_all | solution.py:100
  57.2 1.3 fusion.36
  58.5 0.7 reshape.210
  59.2 0.3 copy.45
  59.5 2.8 %collective-permute-start = (bf16[8,512,64]{1,2,0:T(8,128)(2,1)S(1)}, bf16[8,512,64]{1,2,0:T(8,128)(2,1)S(1)}, u32[]{:S(2)}, u32[]{:S(2)}) collective-permute-start(bf16[8,512,64]{1,2,0:T(8,128)(2,1)S(1)} %copy.45), channel_id=1, source_target_pairs={{0,8},{8,0},{1,9},{9,1},{2,10},{10,2},{3,11},{11,3},{4,12},{12,4},... | collective-permute-start | bytes 1572872 | tf_op jit(solution)/shard_map/ppermute | solution.py:146
  62.3 8.1 %fusion = pred[2048,128]{1,0:T(8,128)(4,1)} fusion(s32[128,8]{0,1:T(8,128)S(1)} %multiply_add_fusion), kind=kLoop, calls=%fused_computation.3 | loop fusion | flops 3932160 | bytes 266240 | tf_op jit(solution)/shard_map/reduce_or | solution.py:208
  70.5 4.2 %collective-permute-done = bf16[8,512,64]{1,2,0:T(8,128)(2,1)S(1)} collective-permute-done((bf16[8,512,64]{1,2,0:T(8,128)(2,1)S(1)}, bf16[8,512,64]{1,2,0:T(8,128)(2,1)S(1)}, u32[]{:S(2)}, u32[]{:S(2)}) %collective-permute-start) | collective-permute-done | bytes 524320 | tf_op jit(solution)/shard_map/ppermute | solution.py:146
  74.6 0.5 copy.46
  75.1 2.2 fusion.5
  77.4 1.9 copy.48
  79.4 1.3 pad_add_fusion.meta
  80.7 5.6 %gather_fusion = bf16[16,128,1024]{2,1,0:T(8,128)(2,1)} fusion(bf16[24,128,1024]{2,1,0:T(8,128)(2,1)} %param.19, s32[1024]{0:T(1024)S(1)} %pad_clamp_fusion), kind=kCustom, calls=%fused_computation | custom fusion | bytes 8388672 | tf_op jit(solution)/shard_map/jit(_take)/gather | solution.py:170
  86.6 2.8 %collective-permute-start.2 = (bf16[8,64,512]{2,1,0:T(8,128)(2,1)S(1)}, bf16[8,64,512]{2,1,0:T(8,128)(2,1)S(1)}, u32[]{:S(2)}, u32[]{:S(2)}) collective-permute-start(bf16[8,64,512]{2,1,0:T(8,128)(2,1)S(1)} %reshape.217), channel_id=1, source_target_pairs={{0,8},{8,0},{1,9},{9,1},{2,10},{10,2},{3,11},{11,3},{4,12},{12,4},... | collective-permute-start | bytes 1572872 | tf_op jit(solution)/shard_map/ppermute | solution.py:146
  89.4 3.9 %bitcast_select_fusion.kc_ref.vc_ref = bf16[2048,1024]{1,0:T(8,128)(2,1)} fusion(bf16[16,128,1024]{2,1,0:T(8,128)(2,1)} %gather_fusion, pred[2048]{0:T(1024)(128)(4,1)S(1)} %broadcast_bitcast_fusion), kind=kLoop, calls=%fused_computation.5 | loop fusion | flops 2097152 | bytes 8390656 | tf_op jit(solution)/shard_map/jit(_take)/select_n | solution.py:170
  93.2 3.2 %slice.94 = bf16[8,128,1024]{2,1,0:T(8,128)(2,1)} slice(bf16[8,192,1024]{2,1,0:T(8,128)(2,1)} %all-to-all-done), slice={[0:8], [0:128], [0:1024]} | slice | bytes 4194304 | tf_op jit(solution)/shard_map/slice | solution.py:142
  96.4 6.1 %collective-permute-done.2 = bf16[8,64,512]{2,1,0:T(8,128)(2,1)S(1)} collective-permute-done((bf16[8,64,512]{2,1,0:T(8,128)(2,1)S(1)}, bf16[8,64,512]{2,1,0:T(8,128)(2,1)S(1)}, u32[]{:S(2)}, u32[]{:S(2)}) %collective-permute-start.2) | collective-permute-done | bytes 524320 | tf_op jit(solution)/shard_map/ppermute | solution.py:146
  102.9 1.7 fusion.21
  104.6 0.5 fusion.25
  105.8 1.1 pad_maximum_fusion.1.q_ref
  106.9 17.0 %shard_map.127 = bf16[8,256,128]{2,1,0:T(8,128)(2,1)} custom-call(s32[2]{0:T(128)} %pad_add_fusion.meta, bf16[8,256,128]{2,1,0:T(8,128)(2,1)} %pad_maximum_fusion.1.q_ref, bf16[2048,1024]{1,0:T(8,128)(2,1)} %bitcast_select_fusion.kc_ref.vc_ref, bf16[2048,1024]{1,0:T(8,128)(2,1)} %bitcast_select_fusion.kc_ref.vc_ref, bf16[1024,1024]{1,0:T(8,128)(2,1)} %bitcast.67, ...), custom_call_target="tpu_custom_call" | custom-call | tf_op jit(solution)/shard_map/pallas_call | solution.py:86
  123.9 1.4 slice_select_fusion
  125.7 1.6 fusion.38
  127.3 0.3 broadcast_select_fusion.1
  127.8 1.3 convolution_convert_fusion
  129.1 1.8 slice_bitcast_fusion.5
  131.0 34.2 %all_to_all.25 = bf16[16,64,1024]{2,1,0:T(8,128)(2,1)} all-to-all(bf16[16,64,1024]{2,1,0:T(8,128)(2,1)S(1)} %get-tuple-element.7), channel_id=1, replica_groups=mesh['tz'=8,'tc'=2,'ra'=2,'rb'=8] {'ra','rb'}, dimensions={0} | all-to-all | bytes 4194304 | tf_op jit(solution)/shard_map/all_to_all | solution.py:216
  165.2 3.7 %all-to-all-start.3 = ((bf16[16,64,1024]{2,1,0:T(8,128)(2,1)}), bf16[16,64,1024]{2,1,0:T(8,128)(2,1)S(1)}, u32[]{:S(2)}, u32[]{:S(2)}) async-start(bf16[16,64,1024]{2,1,0:T(8,128)(2,1)} %get-tuple-element.8), calls=%async_computation.3 | async-start | bytes 4194304 | tf_op jit(solution)/shard_map/all_to_all | solution.py:216
  168.9 6.5 %fusion.4 = f32[1024,1024]{1,0:T(8,128)} fusion(bf16[1024,1024]{1,0:T(8,128)(2,1)} %bitcast.81, bf16[2,1024,1024]{2,1,0:T(8,128)(2,1)} %all-gather.3.cloned.1.call-done), kind=kOutput, calls=%fused_computation.15 | convolution fusion | flops 2147483648 | bytes 8388608 | tf_op jit(solution)/shard_map/dot_general | solution.py:219
  175.5 5.2 %convolution_convert_fusion.2 = bf16[1024,1024]{1,0:T(8,128)(2,1)} fusion(f32[1024,1024]{1,0:T(8,128)} %fusion.4, bf16[2,512,1024]{2,1,0:T(8,128)(2,1)} %all-gather.5.cloned.1.call-done), kind=kOutput, calls=%fused_computation.20 | convolution fusion | flops 1077936128 | bytes 7340032 | tf_op jit(solution)/shard_map/dot_general | solution.py:221
  180.6 17.3 %all-to-all-done.3 = bf16[16,64,1024]{2,1,0:T(8,128)(2,1)S(1)} async-done(((bf16[16,64,1024]{2,1,0:T(8,128)(2,1)}), bf16[16,64,1024]{2,1,0:T(8,128)(2,1)S(1)}, u32[]{:S(2)}, u32[]{:S(2)}) %all-to-all-start.3) | async-done | bytes 2097184 | tf_op jit(solution)/shard_map/all_to_all | solution.py:216
  197.9 1.4 copy-done.3
  199.3 4.0 %all-to-all-start.2 = ((bf16[16,64,1024]{2,1,0:T(8,128)(2,1)}), bf16[16,64,1024]{2,1,0:T(8,128)(2,1)S(1)}, u32[]{:S(2)}, u32[]{:S(2)}) async-start(bf16[16,64,1024]{2,1,0:T(8,128)(2,1)} %bitcast.79), calls=%async_computation.2 | async-start | bytes 4194304 | tf_op jit(solution)/shard_map/all_to_all | solution.py:225
  203.3 4.7 %fusion.2 = f32[1024,1024]{1,0:T(8,128)S(1)} fusion(bf16[1024,1024]{1,0:T(8,128)(2,1)} %bitcast.78, bf16[2,1024,1024]{2,1,0:T(8,128)(2,1)} %all-gather.3.cloned.1.call-done), kind=kOutput, calls=%fused_computation.10 | convolution fusion | flops 2147483648 | bytes 8388608 | tf_op jit(solution)/shard_map/dot_general | solution.py:219
  208.0 2.6 convolution_convert_fusion.1
  210.6 20.2 %all-to-all-done.2 = bf16[16,64,1024]{2,1,0:T(8,128)(2,1)S(1)} async-done(((bf16[16,64,1024]{2,1,0:T(8,128)(2,1)}), bf16[16,64,1024]{2,1,0:T(8,128)(2,1)S(1)}, u32[]{:S(2)}, u32[]{:S(2)}) %all-to-all-start.2) | async-done | bytes 2097184 | tf_op jit(solution)/shard_map/all_to_all | solution.py:225
  230.8 4.8 %all-to-all-start.4 = ((bf16[16,64,1024]{2,1,0:T(8,128)(2,1)}), bf16[16,64,1024]{2,1,0:T(8,128)(2,1)}, u32[]{:S(2)}, u32[]{:S(2)}) async-start(bf16[16,64,1024]{2,1,0:T(8,128)(2,1)} %bitcast.80), calls=%async_computation.4 | async-start | bytes 4194304 | tf_op jit(solution)/shard_map/all_to_all | solution.py:225
  235.7 10.8 %select_reduce_fusion = f32[2048,128]{1,0:T(8,128)S(1)} fusion(f32[128,8]{0,1:T(8,128)S(1)} %copy-done.8, s32[128,8]{0,1:T(8,128)S(1)} %multiply_add_fusion), kind=kLoop, calls=%fused_computation.1 | loop fusion | flops 6029312 | bytes 1056768 | tf_op jit(solution)/shard_map/reduce_sum | solution.py:231
  246.5 16.5 %all-to-all-done.4 = bf16[16,64,1024]{2,1,0:T(8,128)(2,1)} async-done(((bf16[16,64,1024]{2,1,0:T(8,128)(2,1)}), bf16[16,64,1024]{2,1,0:T(8,128)(2,1)}, u32[]{:S(2)}, u32[]{:S(2)}) %all-to-all-start.4) | async-done | bytes 2097184 | tf_op jit(solution)/shard_map/all_to_all | solution.py:225
  263.0 2.0 pad_maximum_fusion
  265.0 2.8 %fusion.6 = bf16[128,1024]{1,0:T(8,128)(2,1)} fusion(f32[2048,128]{1,0:T(8,128)S(1)} %select_reduce_fusion, bf16[2048,1024]{1,0:T(8,128)(2,1)S(1)} %bitcast.70, bf16[128,1024]{1,0:T(8,128)(2,1)S(1)} %get-tuple-element.6), kind=kOutput, calls=%fused_computation.22 | convolution fusion | flops 3221618688 | bytes 5767168 | tf_op jit(solution)/shard_map/dot_general | solution.py:234
  (71 shorter events, 3.3 us)
Async XLA Ops:
  6.5 2.9 %copy-start = (bf16[1024,1024]{1,0:T(8,128)(2,1)S(1)}, bf16[1024,1024]{1,0:T(8,128)(2,1)}, u32[]{:S(2)}) copy-start(bf16[1024,1024]{1,0:T(8,128)(2,1)} %param.17) | copy-start | bytes 6291460
  6.5 162.4 %all-gather.3.cloned.1.call-start = ((), (), s32[]{:S(2)}) async-start(), calls=%async_computation.5 | async-start | bytes 4456448 | tf_op jit(solution)/shard_map/all_gather | solution.py:129
  9.5 0.7 copy-start.12
  9.5 2.3 copy-start.6
  9.9 2.2 copy-start.7
  14.3 6.3 %copy-start.5 = (s32[128,8]{0,1:T(8,128)S(1)}, s32[128,8]{0,1:T(8,128)}, u32[]{:S(2)}) copy-start(s32[128,8]{0,1:T(8,128)} %param.22) | copy-start | bytes 12292
  14.3 6.7 %copy-start.10 = (s32[2,16]{1,0:T(2,128)S(1)}, s32[2,16]{1,0:T(2,128)}, u32[]{:S(2)}) copy-start(s32[2,16]{1,0:T(2,128)} %param.20) | copy-start | bytes 388
  14.3 42.9 %all-to-all-start = ((bf16[8,192,1024]{2,1,0:T(8,128)(2,1)}), bf16[8,192,1024]{2,1,0:T(8,128)(2,1)}, u32[]{:S(2)}, u32[]{:S(2)}) async-start(bf16[8,192,1024]{2,1,0:T(8,128)(2,1)} %broadcast_in_dim.74), calls=%async_computation | async-start | bytes 6291456 | tf_op jit(solution)/shard_map/all_to_all | solution.py:100
  19.8 155.6 %all-gather.5.cloned.1.call-start = ((), (), s32[]{:S(2)}) async-start(), calls=%async_computation.6 | async-start | bytes 2228224 | tf_op jit(solution)/shard_map/all_gather | solution.py:130
  59.5 15.1 %collective-permute-start = (bf16[8,512,64]{1,2,0:T(8,128)(2,1)S(1)}, bf16[8,512,64]{1,2,0:T(8,128)(2,1)S(1)}, u32[]{:S(2)}, u32[]{:S(2)}) collective-permute-start(bf16[8,512,64]{1,2,0:T(8,128)(2,1)S(1)} %copy.45), channel_id=1, source_target_pairs={{0,8},{8,0},{1,9},{9,1},{2,10},{10,2},{3,11},{11,3},{4,12},{12,4},... | collective-permute-start | bytes 1572872 | tf_op jit(solution)/shard_map/ppermute | solution.py:146
  79.3 23.6 %collective-permute-start.1 = (bf16[512,1024]{0,1:T(8,128)(2,1)S(1)}, bf16[512,1024]{0,1:T(8,128)(2,1)}, u32[]{:S(2)}, u32[]{:S(2)}) collective-permute-start(bf16[512,1024]{0,1:T(8,128)(2,1)S(1)} %bitcast.72), channel_id=1, source_target_pairs={{0,16},{16,0},{1,17},{17,1},{2,18},{18,2},{3,19},{19,3},{4,20},{20... | collective-permute-start | bytes 3145736 | tf_op jit(solution)/shard_map/ppermute | solution.py:156
  86.6 15.9 %collective-permute-start.2 = (bf16[8,64,512]{2,1,0:T(8,128)(2,1)S(1)}, bf16[8,64,512]{2,1,0:T(8,128)(2,1)S(1)}, u32[]{:S(2)}, u32[]{:S(2)}) collective-permute-start(bf16[8,64,512]{2,1,0:T(8,128)(2,1)S(1)} %reshape.217), channel_id=1, source_target_pairs={{0,8},{8,0},{1,9},{9,1},{2,10},{10,2},{3,11},{11,3},{4,12},{12,4},... | collective-permute-start | bytes 1572872 | tf_op jit(solution)/shard_map/ppermute | solution.py:146
  102.6 23.0 %collective-permute-start.3 = (bf16[1024,512]{1,0:T(8,128)(2,1)S(1)}, bf16[1024,512]{1,0:T(8,128)(2,1)}, u32[]{:S(2)}, u32[]{:S(2)}) collective-permute-start(bf16[1024,512]{1,0:T(8,128)(2,1)S(1)} %bitcast.74), channel_id=1, source_target_pairs={{0,16},{16,0},{1,17},{17,1},{2,18},{18,2},{3,19},{19,3},{4,20},{20... | collective-permute-start | bytes 3145736 | tf_op jit(solution)/shard_map/ppermute | solution.py:156
  125.4 2.2 copy-start.2
  125.6 2.1 copy-start.4
  125.6 2.1 copy-start.9
  165.2 32.7 %all-to-all-start.3 = ((bf16[16,64,1024]{2,1,0:T(8,128)(2,1)}), bf16[16,64,1024]{2,1,0:T(8,128)(2,1)S(1)}, u32[]{:S(2)}, u32[]{:S(2)}) async-start(bf16[16,64,1024]{2,1,0:T(8,128)(2,1)} %get-tuple-element.8), calls=%async_computation.3 | async-start | bytes 4194304 | tf_op jit(solution)/shard_map/all_to_all | solution.py:216
  197.9 1.4 copy-start.3
  199.3 31.6 %all-to-all-start.2 = ((bf16[16,64,1024]{2,1,0:T(8,128)(2,1)}), bf16[16,64,1024]{2,1,0:T(8,128)(2,1)S(1)}, u32[]{:S(2)}, u32[]{:S(2)}) async-start(bf16[16,64,1024]{2,1,0:T(8,128)(2,1)} %bitcast.79), calls=%async_computation.2 | async-start | bytes 4194304 | tf_op jit(solution)/shard_map/all_to_all | solution.py:225
  203.3 4.7 %copy-start.11 = (bf16[2,512,1024]{2,1,0:T(8,128)(2,1)S(1)}, bf16[2,512,1024]{2,1,0:T(8,128)(2,1)}, u32[]{:S(2)}) copy-start(bf16[2,512,1024]{2,1,0:T(8,128)(2,1)} %all-gather.5.cloned.1.call-done) | copy-start | bytes 6291460
  230.8 4.8 %copy-start.8 = (f32[128,8]{0,1:T(8,128)S(1)}, f32[128,8]{0,1:T(8,128)}, u32[]{:S(2)}) copy-start(f32[128,8]{0,1:T(8,128)} %param.23) | copy-start | bytes 12292
  230.8 32.2 %all-to-all-start.4 = ((bf16[16,64,1024]{2,1,0:T(8,128)(2,1)}), bf16[16,64,1024]{2,1,0:T(8,128)(2,1)}, u32[]{:S(2)}, u32[]{:S(2)}) async-start(bf16[16,64,1024]{2,1,0:T(8,128)(2,1)} %bitcast.80), calls=%async_computation.4 | async-start | bytes 4194304 | tf_op jit(solution)/shard_map/all_to_all | solution.py:225
  265.0 2.8 %copy-start.1 = (bf16[1024,1024]{1,0:T(8,128)(2,1)S(1)}, bf16[1024,1024]{1,0:T(8,128)(2,1)}, u32[]{:S(2)}) copy-start(bf16[1024,1024]{1,0:T(8,128)(2,1)} %param.17) | copy-start | bytes 6291460
Sparse Core Ops, SparseCore 0:
  9.2 41.0 all-gather.2
  52.1 37.6 all-gather.4

commit v5 on v3

--- a/solution.py
+++ b/solution.py
@@ -127,16 +127,32 @@
     wq_half = lax.dynamic_slice_in_dim(w_query, core * half_rows, half_rows, 0)
     wo_half = lax.dynamic_slice_in_dim(w_out, core * half_rows, half_rows, 1)
     lanes = 128
+    quarter = half_rows // 2
+    pair_side = lax.axis_index("tz") % 2
+    part = (core * 2 + pair_side) * quarter
+    wq_part = lax.dynamic_slice_in_dim(w_query, part, quarter, 0)
+    wo_part = lax.dynamic_slice_in_dim(w_out, part, quarter, 1)
     pieces = gather_rows(
-        jnp.concatenate([wq_half.reshape(-1, lanes), wo_half.reshape(-1, lanes)], axis=0),
+        jnp.concatenate([wq_part.reshape(-1, lanes), wo_part.reshape(-1, lanes)], axis=0),
         TP,
         tp_size,
     )
-    q_rows = wq_half.size // lanes
-    wq_mine = jnp.transpose(
-        pieces[:, :q_rows].reshape(tp_size, half_rows, HEAD_DIM), (1, 0, 2)
-    ).reshape(half_rows, D)
-    wo_mine = pieces[:, q_rows:].reshape(D, half_rows)
+    q_rows = wq_part.size // lanes
+    wq_near = jnp.transpose(
+        pieces[:, :q_rows].reshape(tp_size, quarter, HEAD_DIM), (1, 0, 2)
+    ).reshape(quarter, D)
+    wo_near = pieces[:, q_rows:].reshape(D, quarter)
+    z_pairs = [(j, j ^ 1) for j in range(lax.axis_size("tz"))]
+    wq_pair, wo_pair = lax.ppermute((wq_near, wo_near), "tz", z_pairs)
+    low = pair_side == 0
+    wq_mine = jnp.where(
+        low, jnp.concatenate([wq_near, wq_pair]), jnp.concatenate([wq_pair, wq_near])
+    )
+    wo_mine = jnp.where(
+        low,
+        jnp.concatenate([wo_near, wo_pair], axis=1),
+        jnp.concatenate([wo_pair, wo_near], axis=1),
+    )
     wq_other, wo_other = lax.ppermute((wq_mine, wo_mine), "tc", [(0, 1), (1, 0)])
     gate_up_full = lax.all_gather(w_gate_up, TOK, axis=1, tiled=True)
     down_full = lax.all_gather(w_down, TOK, axis=1, tiled=True)

time: 248 us -> 273 us (1.10); the launches traced: 247 us -> 269 us
  waiting for transfers between devices: 73.9 us -> 82.4 us
  other arithmetic: 29.9 us -> 36.8 us
  matrix products: 27.6 us -> 30.6 us
    ppermute x0 -> x2, waiting for transfers between devices: none -> 16.4 us  [shards(): wq_pair, wo_pair = lax.ppermute((wq_near, wo_near), 'tz', z_pairs)]
    all_to_all x2, waiting for transfers between devices: 18.4 us -> 10.5 us  [gather_rows(): lax.all_to_all(send, axis_name, split_axis=0, concat_axis=0, tiled=True)]
    select_n x0 -> x2, other arithmetic: none -> 4.3 us  [the longest x1 2.48 us: shards(): jnp.where(low, jnp.concatenate([wo_near, wo_pair], axis=1), jnp.concatena...]
  transfers between devices with their start and end apart: 9 -> 11, of which waited for: 4 -> 6; matrix products, arithmetic and copies ran while one was open for 31% -> 32% of each run, Pallas kernels for 7% -> 6%
where the time goes in v5:
time: 273 us; the launch traced here: 269 us
  waiting for transfers between devices  82.4 us (30%)
  other arithmetic  36.8 us (13%)
  blocking collectives  35.4 us (13%)
  matrix products  30.6 us (11%)
  local copies, waits for them, and re-layouts  26.7 us (10%)
  starting transfers between devices  25.7 us (9%)
  Pallas kernels  17 us (6%)
  between operations  14.4 us (5%)
    all_to_all x2, waiting for transfers between devices, shards(): lax.all_to_all(produced.reshape(tp_size, capacity, D), TP, split_axis=0,...  36.9 us
    all_to_all x1, blocking collectives, shards(): lax.all_to_all(send_buffer[:, local], TP, split_axis=0, concat_axis=0, ti...  35.4 us
    all_to_all x1, waiting for transfers between devices, shards(): lax.all_to_all(send_buffer[:, local], TP, split_axis=0, concat_axis=0, ti...  17.1 us
    pallas_call x1, Pallas kernels, attend(): pl.pallas_call(attention_kernel, grid_spec=pltpu.PrefetchScalarGridSpec(n...  17 us
    ppermute x2, waiting for transfers between devices, shards(): wq_pair, wo_pair = lax.ppermute((wq_near, wo_near), 'tz', z_pairs)  16.4 us
    dot_general x2, matrix products, shards(): jnp.dot(received, gate_up_full[local], preferred_element_type=jnp.float32)  11.3 us
    reduce_sum x1, other arithmetic, shards(): mixing = jnp.sum(jnp.where(hits, gate_weights[None, :, :], 0.0), axis=2).T  10.8 us
    all_to_all x2, starting transfers between devices, gather_rows(): lax.all_to_all(send, axis_name, split_axis=0, concat_axis=0, tiled=True)  10.6 us
  transfers between devices with their start and end apart: 11, of which 6 were waited for; matrix products, arithmetic and copies ran while one was open for 32% of the time, Pallas kernels for 6%

profile of v5, /device:TPU:224, one launch (start us, length us, event | category | flops | bytes accessed | tf_op | source)
XLA Modules:
  0.0 269.1 jit_solution(15474370151510542974)
XLA Ops:
  9.1 1.2 broadcast_in_dim.80
  10.3 7.0 %all-to-all-start = ((bf16[16,256,128]{2,1,0:T(8,128)(2,1)}), bf16[16,256,128]{2,1,0:T(8,128)(2,1)S(1)}, u32[]{:S(2)}, u32[]{:S(2)}) async-start(bf16[16,256,128]{2,1,0:T(8,128)(2,1)} %broadcast_in_dim.80), calls=%async_computation | async-start | bytes 2097152 | tf_op jit(solution)/shard_map/all_to_all | solution.py:100
  19.1 1.2 fusion.32
  20.3 1.0 slice.86
  21.3 1.0 slice.136
  24.6 10.5 %all-to-all-done = bf16[16,256,128]{2,1,0:T(8,128)(2,1)S(1)} async-done(((bf16[16,256,128]{2,1,0:T(8,128)(2,1)}), bf16[16,256,128]{2,1,0:T(8,128)(2,1)S(1)}, u32[]{:S(2)}, u32[]{:S(2)}) %all-to-all-start) | async-done | bytes 1048608 | tf_op jit(solution)/shard_map/all_to_all | solution.py:100
  35.1 1.6 broadcast_in_dim.85
  36.7 3.6 %all-to-all-start.1 = ((bf16[8,128,1024]{2,1,0:T(8,128)(2,1)}), bf16[8,128,1024]{2,1,0:T(8,128)(2,1)S(1)}, u32[]{:S(2)}, u32[]{:S(2)}) async-start(bf16[8,128,1024]{2,1,0:T(8,128)(2,1)} %broadcast_in_dim.85), calls=%async_computation.1 | async-start | bytes 4194304 | tf_op jit(solution)/shard_map/all_to_all | solution.py:100
  40.3 1.0 fusion.31
  41.3 1.7 reshape.207
  43.0 1.1 copy.29
  44.1 1.0 collective-permute-start
  45.2 5.7 %gather_fusion = bf16[16,128,1024]{2,1,0:T(8,128)(2,1)} fusion(bf16[24,128,1024]{2,1,0:T(8,128)(2,1)} %param.19, s32[1024]{0:T(1024)S(1)} %pad_clamp_fusion), kind=kCustom, calls=%fused_computation | custom fusion | bytes 8388672 | tf_op jit(solution)/shard_map/jit(_take)/gather | solution.py:181
  50.9 6.1 %collective-permute-done = bf16[256,1024]{0,1:T(8,128)(2,1)} collective-permute-done((bf16[256,1024]{0,1:T(8,128)(2,1)}, bf16[256,1024]{0,1:T(8,128)(2,1)}, u32[]{:S(2)}, u32[]{:S(2)}) %collective-permute-start) | collective-permute-done | bytes 524320 | tf_op jit(solution)/shard_map/ppermute | solution.py:146
  57.0 1.8 maximum_select_fusion
  59.0 3.9 %bitcast_select_fusion.kc_ref.vc_ref = bf16[2048,1024]{1,0:T(8,128)(2,1)} fusion(bf16[16,128,1024]{2,1,0:T(8,128)(2,1)} %gather_fusion, pred[2048]{0:T(1024)(128)(4,1)S(1)} %broadcast_bitcast_fusion), kind=kLoop, calls=%fused_computation.5 | loop fusion | flops 2097152 | bytes 8390656 | tf_op jit(solution)/shard_map/jit(_take)/select_n | solution.py:181
  65.4 2.0 reshape.215
  67.4 1.5 collective-permute-start.2
  68.9 1.2 pad_add_fusion.meta
  70.8 8.1 %fusion = pred[2048,128]{1,0:T(8,128)(4,1)} fusion(s32[128,8]{0,1:T(8,128)S(1)} %multiply_add_fusion), kind=kLoop, calls=%fused_computation.3 | loop fusion | flops 3932160 | bytes 266240 | tf_op jit(solution)/shard_map/reduce_or | solution.py:219
  78.9 10.3 %collective-permute-done.2 = bf16[1024,256]{1,0:T(8,128)(2,1)S(1)} collective-permute-done((bf16[1024,256]{1,0:T(8,128)(2,1)}, bf16[1024,256]{1,0:T(8,128)(2,1)S(1)}, u32[]{:S(2)}, u32[]{:S(2)}) %collective-permute-start.2) | collective-permute-done | bytes 524320 | tf_op jit(solution)/shard_map/ppermute | solution.py:146
  89.2 2.5 maximum_select_fusion.1
  91.7 1.7 fusion.20
  93.4 1.3 convolution_add_fusion
  94.7 1.2 copy.30
  96.5 1.1 pad_maximum_fusion.1.q_ref
  97.6 1.4 copy-done.2
  99.0 17.0 %shard_map.127 = bf16[8,256,128]{2,1,0:T(8,128)(2,1)} custom-call(s32[2]{0:T(128)} %pad_add_fusion.meta, bf16[8,256,128]{2,1,0:T(8,128)(2,1)} %pad_maximum_fusion.1.q_ref, bf16[2048,1024]{1,0:T(8,128)(2,1)} %bitcast_select_fusion.kc_ref.vc_ref, bf16[2048,1024]{1,0:T(8,128)(2,1)} %bitcast_select_fusion.kc_ref.vc_ref, bf16[1024,1024]{1,0:T(8,128)(2,1)} %bitcast.65, ...), custom_call_target="tpu_custom_call" | custom-call | tf_op jit(solution)/shard_map/pallas_call | solution.py:86
  116.0 1.4 slice_select_fusion
  117.7 1.6 fusion.33
  119.3 1.6 broadcast_select_fusion.1
  121.1 1.3 convolution_convert_fusion
  122.4 1.9 slice_bitcast_fusion.5
  124.3 35.4 %all_to_all.30 = bf16[16,64,1024]{2,1,0:T(8,128)(2,1)} all-to-all(bf16[16,64,1024]{2,1,0:T(8,128)(2,1)S(1)} %get-tuple-element.7), channel_id=1, replica_groups=mesh['tz'=8,'tc'=2,'ra'=2,'rb'=8] {'ra','rb'}, dimensions={0} | all-to-all | bytes 4194304 | tf_op jit(solution)/shard_map/all_to_all | solution.py:227
  159.7 3.7 %all-to-all-start.4 = ((bf16[16,64,1024]{2,1,0:T(8,128)(2,1)}), bf16[16,64,1024]{2,1,0:T(8,128)(2,1)S(1)}, u32[]{:S(2)}, u32[]{:S(2)}) async-start(bf16[16,64,1024]{2,1,0:T(8,128)(2,1)} %get-tuple-element.8), calls=%async_computation.4 | async-start | bytes 4194304 | tf_op jit(solution)/shard_map/all_to_all | solution.py:227
  163.5 6.6 %fusion.4 = f32[1024,1024]{1,0:T(8,128)} fusion(bf16[1024,1024]{1,0:T(8,128)(2,1)} %bitcast.78, bf16[2,1024,1024]{2,1,0:T(8,128)(2,1)} %all-gather.3.cloned.1.call-done), kind=kOutput, calls=%fused_computation.15 | convolution fusion | flops 2147483648 | bytes 8388608 | tf_op jit(solution)/shard_map/dot_general | solution.py:230
  170.0 5.2 %convolution_convert_fusion.2 = bf16[1024,1024]{1,0:T(8,128)(2,1)} fusion(f32[1024,1024]{1,0:T(8,128)} %fusion.4, bf16[2,512,1024]{2,1,0:T(8,128)(2,1)} %all-gather.5.cloned.1.call-done), kind=kOutput, calls=%fused_computation.18 | convolution fusion | flops 1077936128 | bytes 7340032 | tf_op jit(solution)/shard_map/dot_general | solution.py:232
  175.2 17.1 %all-to-all-done.4 = bf16[16,64,1024]{2,1,0:T(8,128)(2,1)S(1)} async-done(((bf16[16,64,1024]{2,1,0:T(8,128)(2,1)}), bf16[16,64,1024]{2,1,0:T(8,128)(2,1)S(1)}, u32[]{:S(2)}, u32[]{:S(2)}) %all-to-all-start.4) | async-done | bytes 2097184 | tf_op jit(solution)/shard_map/all_to_all | solution.py:227
  192.3 1.3 copy-done.7
  193.7 3.9 %all-to-all-start.3 = ((bf16[16,64,1024]{2,1,0:T(8,128)(2,1)}), bf16[16,64,1024]{2,1,0:T(8,128)(2,1)S(1)}, u32[]{:S(2)}, u32[]{:S(2)}) async-start(bf16[16,64,1024]{2,1,0:T(8,128)(2,1)} %bitcast.76), calls=%async_computation.3 | async-start | bytes 4194304 | tf_op jit(solution)/shard_map/all_to_all | solution.py:236
  197.6 4.7 %fusion.2 = f32[1024,1024]{1,0:T(8,128)S(1)} fusion(bf16[1024,1024]{1,0:T(8,128)(2,1)} %bitcast.75, bf16[2,1024,1024]{2,1,0:T(8,128)(2,1)} %all-gather.3.cloned.1.call-done), kind=kOutput, calls=%fused_computation.10 | convolution fusion | flops 2147483648 | bytes 8388608 | tf_op jit(solution)/shard_map/dot_general | solution.py:230
  202.3 2.6 convolution_convert_fusion.1
  205.0 20.2 %all-to-all-done.3 = bf16[16,64,1024]{2,1,0:T(8,128)(2,1)S(1)} async-done(((bf16[16,64,1024]{2,1,0:T(8,128)(2,1)}), bf16[16,64,1024]{2,1,0:T(8,128)(2,1)S(1)}, u32[]{:S(2)}, u32[]{:S(2)}) %all-to-all-start.3) | async-done | bytes 2097184 | tf_op jit(solution)/shard_map/all_to_all | solution.py:236
  225.2 4.8 %all-to-all-start.5 = ((bf16[16,64,1024]{2,1,0:T(8,128)(2,1)}), bf16[16,64,1024]{2,1,0:T(8,128)(2,1)}, u32[]{:S(2)}, u32[]{:S(2)}) async-start(bf16[16,64,1024]{2,1,0:T(8,128)(2,1)} %bitcast.77), calls=%async_computation.5 | async-start | bytes 4194304 | tf_op jit(solution)/shard_map/all_to_all | solution.py:236
  230.0 10.8 %select_reduce_fusion = f32[2048,128]{1,0:T(8,128)S(1)} fusion(f32[128,8]{0,1:T(8,128)S(1)} %copy-done.13, s32[128,8]{0,1:T(8,128)S(1)} %multiply_add_fusion), kind=kLoop, calls=%fused_computation.1 | loop fusion | flops 6029312 | bytes 1056768 | tf_op jit(solution)/shard_map/reduce_sum | solution.py:242
  240.9 16.6 %all-to-all-done.5 = bf16[16,64,1024]{2,1,0:T(8,128)(2,1)} async-done(((bf16[16,64,1024]{2,1,0:T(8,128)(2,1)}), bf16[16,64,1024]{2,1,0:T(8,128)(2,1)}, u32[]{:S(2)}, u32[]{:S(2)}) %all-to-all-start.5) | async-done | bytes 2097184 | tf_op jit(solution)/shard_map/all_to_all | solution.py:236
  257.5 2.0 pad_maximum_fusion
  259.5 2.8 %fusion.5 = bf16[128,1024]{1,0:T(8,128)(2,1)} fusion(f32[2048,128]{1,0:T(8,128)S(1)} %select_reduce_fusion, bf16[2048,1024]{1,0:T(8,128)(2,1)S(1)} %bitcast.68, bf16[128,1024]{1,0:T(8,128)(2,1)S(1)} %get-tuple-element.6), kind=kOutput, calls=%fused_computation.21 | convolution fusion | flops 3221618688 | bytes 5767168 | tf_op jit(solution)/shard_map/dot_general | solution.py:245
  (82 shorter events, 10.2 us)
Async XLA Ops:
  6.5 12.6 %copy-start = (bf16[1024,1024]{1,0:T(8,128)(2,1)S(1)}, bf16[1024,1024]{1,0:T(8,128)(2,1)}, u32[]{:S(2)}) copy-start(bf16[1024,1024]{1,0:T(8,128)(2,1)} %param.17) | copy-start | bytes 6291460
  6.5 11.6 %copy-start.3 = (bf16[128,1024]{1,0:T(8,128)(2,1)S(1)}, bf16[128,1024]{1,0:T(8,128)(2,1)}, u32[]{:S(2)}) copy-start(bf16[128,1024]{1,0:T(8,128)(2,1)} %param.13) | copy-start | bytes 786436
  6.5 156.9 %all-gather.3.cloned.1.call-start = ((), (), s32[]{:S(2)}) async-start(), calls=%async_computation.6 | async-start | bytes 4456448 | tf_op jit(solution)/shard_map/all_gather | solution.py:157
  7.3 11.0 %copy-start.12 = (f32[1024]{0:T(1024)S(1)}, f32[1024]{0:T(1024)}, u32[]{:S(2)}) copy-start(f32[1024]{0:T(1024)} %param.14) | copy-start | bytes 12292
  10.3 24.8 %all-to-all-start = ((bf16[16,256,128]{2,1,0:T(8,128)(2,1)}), bf16[16,256,128]{2,1,0:T(8,128)(2,1)S(1)}, u32[]{:S(2)}, u32[]{:S(2)}) async-start(bf16[16,256,128]{2,1,0:T(8,128)(2,1)} %broadcast_in_dim.80), calls=%async_computation | async-start | bytes 2097152 | tf_op jit(solution)/shard_map/all_to_all | solution.py:100
  17.3 152.7 %all-gather.5.cloned.1.call-start = ((), (), s32[]{:S(2)}) async-start(), calls=%async_computation.7 | async-start | bytes 2228224 | tf_op jit(solution)/shard_map/all_gather | solution.py:158
  18.4 0.7 copy-start.5
  19.1 3.3 %copy-start.17 = (s32[2]{0:T(128)S(1)}, s32[2]{0:T(128)}, u32[]{:S(2)}) copy-start(s32[2]{0:T(128)} %param.21) | copy-start | bytes 28
  23.8 0.6 copy-start.9
  36.7 60.9 %all-to-all-start.1 = ((bf16[8,128,1024]{2,1,0:T(8,128)(2,1)}), bf16[8,128,1024]{2,1,0:T(8,128)(2,1)S(1)}, u32[]{:S(2)}, u32[]{:S(2)}) async-start(bf16[8,128,1024]{2,1,0:T(8,128)(2,1)} %broadcast_in_dim.85), calls=%async_computation.1 | async-start | bytes 4194304 | tf_op jit(solution)/shard_map/all_to_all | solution.py:100
  41.3 3.8 %copy-start.15 = (s32[2,16]{1,0:T(2,128)S(1)}, s32[2,16]{1,0:T(2,128)}, u32[]{:S(2)}) copy-start(s32[2,16]{1,0:T(2,128)} %param.20) | copy-start | bytes 388
  44.1 12.9 %collective-permute-start = (bf16[256,1024]{0,1:T(8,128)(2,1)}, bf16[256,1024]{0,1:T(8,128)(2,1)}, u32[]{:S(2)}, u32[]{:S(2)}) collective-permute-start(bf16[256,1024]{0,1:T(8,128)(2,1)} %bitcast.73), channel_id=1, source_target_pairs={{0,32},{32,0},{64,96},{96,64},{128,160},{160,128},{192,224},{224,1... | collective-permute-start | bytes 1572872 | tf_op jit(solution)/shard_map/ppermute | solution.py:146
  58.9 4.0 %copy-start.11 = (s32[128,8]{0,1:T(8,128)S(1)}, s32[128,8]{0,1:T(8,128)}, u32[]{:S(2)}) copy-start(s32[128,8]{0,1:T(8,128)} %param.22) | copy-start | bytes 12292
  58.9 32.8 %collective-permute-start.1 = (bf16[512,1024]{0,1:T(8,128)(2,1)S(1)}, bf16[512,1024]{0,1:T(8,128)(2,1)}, u32[]{:S(2)}, u32[]{:S(2)}) collective-permute-start(bf16[512,1024]{0,1:T(8,128)(2,1)S(1)} %maximum_select_fusion), channel_id=1, source_target_pairs={{0,16},{16,0},{1,17},{17,1},{2,18},{18,2},{3,19},{19,3},{4,20},{20... | collective-permute-start | bytes 3145736 | tf_op jit(solution)/shard_map/ppermute | solution.py:156
  62.9 28.8 %copy-start.6 = (bf16[128,1024]{1,0:T(8,128)(2,1)S(1)}, bf16[128,1024]{1,0:T(8,128)(2,1)}, u32[]{:S(2)}) copy-start(bf16[128,1024]{1,0:T(8,128)(2,1)} %copy-done.5) | copy-start | bytes 786436
  67.4 21.8 %collective-permute-start.2 = (bf16[1024,256]{1,0:T(8,128)(2,1)}, bf16[1024,256]{1,0:T(8,128)(2,1)S(1)}, u32[]{:S(2)}, u32[]{:S(2)}) collective-permute-start(bf16[1024,256]{1,0:T(8,128)(2,1)} %reshape.215), channel_id=1, source_target_pairs={{0,32},{32,0},{64,96},{96,64},{128,160},{160,128},{192,224},{224,1... | collective-permute-start | bytes 1572872 | tf_op jit(solution)/shard_map/ppermute | solution.py:146
  91.6 4.3 %copy-start.10 = (f32[128,32]{0,1:T(8,128)S(1)}, f32[128,32]{0,1:T(8,128)}, u32[]{:S(2)}) copy-start(f32[128,32]{0,1:T(8,128)} %copy-done.9) | copy-start | bytes 49156
  91.6 26.1 %collective-permute-start.3 = (bf16[1024,512]{1,0:T(8,128)(2,1)}, bf16[1024,512]{1,0:T(8,128)(2,1)}, u32[]{:S(2)}, u32[]{:S(2)}) collective-permute-start(bf16[1024,512]{1,0:T(8,128)(2,1)} %maximum_select_fusion.1), channel_id=1, source_target_pairs={{0,16},{16,0},{1,17},{17,1},{2,18},{18,2},{3,19},{19,3},{4,20},{20... | collective-permute-start | bytes 3145736 | tf_op jit(solution)/shard_map/ppermute | solution.py:156
  97.6 1.4 copy-start.2
  117.5 3.4 %copy-start.4 = (bf16[128,1024]{1,0:T(8,128)(2,1)S(1)}, bf16[128,1024]{1,0:T(8,128)(2,1)}, u32[]{:S(2)}) copy-start(bf16[128,1024]{1,0:T(8,128)(2,1)} %param.13) | copy-start | bytes 786436
  117.7 3.4 %copy-start.8 = (pred[2048,128]{1,0:T(8,128)(4,1)S(1)}, pred[2048,128]{1,0:T(8,128)(4,1)}, u32[]{:S(2)}) copy-start(pred[2048,128]{1,0:T(8,128)(4,1)} %fusion) | copy-start | bytes 786436
  117.7 3.4 %copy-start.14 = (f32[1024]{0:T(1024)S(1)}, f32[1024]{0:T(1024)}, u32[]{:S(2)}) copy-start(f32[1024]{0:T(1024)} %param.15) | copy-start | bytes 12292
  159.7 32.6 %all-to-all-start.4 = ((bf16[16,64,1024]{2,1,0:T(8,128)(2,1)}), bf16[16,64,1024]{2,1,0:T(8,128)(2,1)S(1)}, u32[]{:S(2)}, u32[]{:S(2)}) async-start(bf16[16,64,1024]{2,1,0:T(8,128)(2,1)} %get-tuple-element.8), calls=%async_computation.4 | async-start | bytes 4194304 | tf_op jit(solution)/shard_map/all_to_all | solution.py:227
  192.3 1.3 copy-start.7
  193.7 31.5 %all-to-all-start.3 = ((bf16[16,64,1024]{2,1,0:T(8,128)(2,1)}), bf16[16,64,1024]{2,1,0:T(8,128)(2,1)S(1)}, u32[]{:S(2)}, u32[]{:S(2)}) async-start(bf16[16,64,1024]{2,1,0:T(8,128)(2,1)} %bitcast.76), calls=%async_computation.3 | async-start | bytes 4194304 | tf_op jit(solution)/shard_map/all_to_all | solution.py:236
  197.6 4.7 %copy-start.16 = (bf16[2,512,1024]{2,1,0:T(8,128)(2,1)S(1)}, bf16[2,512,1024]{2,1,0:T(8,128)(2,1)}, u32[]{:S(2)}) copy-start(bf16[2,512,1024]{2,1,0:T(8,128)(2,1)} %all-gather.5.cloned.1.call-done) | copy-start | bytes 6291460
  225.2 4.8 %copy-start.13 = (f32[128,8]{0,1:T(8,128)S(1)}, f32[128,8]{0,1:T(8,128)}, u32[]{:S(2)}) copy-start(f32[128,8]{0,1:T(8,128)} %param.23) | copy-start | bytes 12292
  225.2 32.3 %all-to-all-start.5 = ((bf16[16,64,1024]{2,1,0:T(8,128)(2,1)}), bf16[16,64,1024]{2,1,0:T(8,128)(2,1)}, u32[]{:S(2)}, u32[]{:S(2)}) async-start(bf16[16,64,1024]{2,1,0:T(8,128)(2,1)} %bitcast.77), calls=%async_computation.5 | async-start | bytes 4194304 | tf_op jit(solution)/shard_map/all_to_all | solution.py:236
  259.5 2.8 %copy-start.1 = (bf16[1024,1024]{1,0:T(8,128)(2,1)S(1)}, bf16[1024,1024]{1,0:T(8,128)(2,1)}, u32[]{:S(2)}) copy-start(bf16[1024,1024]{1,0:T(8,128)(2,1)} %param.17) | copy-start | bytes 6291460
Sparse Core Ops, SparseCore 0:
  9.2 42.8 all-gather.2
  54.0 38.4 all-gather.4

commit v6 on v3

--- a/solution.py
+++ b/solution.py
@@ -57,10 +57,10 @@
     contract = (((1,), (1,)), ((), ()))
     s_old = lax.dot_general(query, kc_ref[...], contract, preferred_element_type=jnp.float32) * ATTN_SCALE
     s_new = lax.dot_general(query, kn_ref[...], contract, preferred_element_type=jnp.float32) * ATTN_SCALE
-    old_index = lax.broadcasted_iota(jnp.int32, s_old.shape, 1)
+    old_index = lax.broadcasted_iota(jnp.int32, (1, s_old.shape[1]), 1)
     s_old = jnp.where(old_index < length, s_old, -1e30)
-    new_index = lax.broadcasted_iota(jnp.int32, s_new.shape, 1)
-    query_index = lax.broadcasted_iota(jnp.int32, s_new.shape, 0) % (rows // 2) + first_query
+    new_index = lax.broadcasted_iota(jnp.int32, (1, s_new.shape[1]), 1)
+    query_index = lax.broadcasted_iota(jnp.int32, (rows, 1), 0) % (rows // 2) + first_query
     s_new = jnp.where(new_index <= query_index, s_new, -1e30)
     top = jnp.maximum(jnp.max(s_old, axis=1, keepdims=True), jnp.max(s_new, axis=1, keepdims=True))
     e_old = jnp.exp(s_old - top)

time: 248 us -> 248 us (level)
  no operation moved by 1% of the time
where the time goes in v6:
time: 248 us; the launch traced here: 247 us
  waiting for transfers between devices  73.9 us (30%)
  blocking collectives  34 us (14%)
  other arithmetic  29.9 us (12%)
  matrix products  27.6 us (11%)
  local copies, waits for them, and re-layouts  26.3 us (11%)
  starting transfers between devices  23.9 us (10%)
  Pallas kernels  17 us (7%)
  between operations  14.6 us (6%)
    all_to_all x2, waiting for transfers between devices, shards(): lax.all_to_all(produced.reshape(tp_size, capacity, D), TP, split_axis=0,...  37 us
    all_to_all x1, blocking collectives, shards(): lax.all_to_all(send_buffer[:, local], TP, split_axis=0, concat_axis=0, ti...  34 us
    all_to_all x2, waiting for transfers between devices, gather_rows(): lax.all_to_all(send, axis_name, split_axis=0, concat_axis=0, tiled=True)  18.4 us
    all_to_all x1, waiting for transfers between devices, shards(): lax.all_to_all(send_buffer[:, local], TP, split_axis=0, concat_axis=0, ti...  17 us
    pallas_call x1, Pallas kernels, attend(): pl.pallas_call(attention_kernel, grid_spec=pltpu.PrefetchScalarGridSpec(n...  17 us
    dot_general x2, matrix products, shards(): jnp.dot(received, gate_up_full[local], preferred_element_type=jnp.float32)  11.2 us
    all_to_all x2, starting transfers between devices, gather_rows(): lax.all_to_all(send, axis_name, split_axis=0, concat_axis=0, tiled=True)  10.8 us
    reduce_sum x1, other arithmetic, shards(): mixing = jnp.sum(jnp.where(hits, gate_weights[None, :, :], 0.0), axis=2).T  10.8 us
  transfers between devices with their start and end apart: 9, of which 4 were waited for; matrix products, arithmetic and copies ran while one was open for 31% of the time, Pallas kernels for 7%

profile of v6, /device:TPU:224, one launch (start us, length us, event | category | flops | bytes accessed | tf_op | source)
XLA Modules:
  0.0 247.3 jit_solution(15189198262751416515)
XLA Ops:
  6.5 0.7 all-gather.3.cloned.1.call-update
  7.3 0.8 constant_dynamic-slice_fusion.2
  8.4 0.9 constant_dynamic-slice_fusion.1
  9.3 1.8 broadcast_in_dim.80
  11.1 7.2 %all-to-all-start = ((bf16[16,512,128]{2,1,0:T(8,128)(2,1)}), bf16[16,512,128]{2,1,0:T(8,128)(2,1)}, u32[]{:S(2)}, u32[]{:S(2)}) async-start(bf16[16,512,128]{2,1,0:T(8,128)(2,1)} %broadcast_in_dim.80), calls=%async_computation | async-start | bytes 4194304 | tf_op jit(solution)/shard_map/all_to_all | solution.py:100
  18.3 0.7 all-gather.5.cloned.1.call-update
  19.4 0.6 dynamic_slice.18
  20.6 0.4 fusion.32
  22.2 8.1 %fusion = pred[2048,128]{1,0:T(8,128)(4,1)} fusion(s32[128,8]{0,1:T(8,128)S(1)} %multiply_add_fusion), kind=kLoop, calls=%fused_computation.3 | loop fusion | flops 3932160 | bytes 266240 | tf_op jit(solution)/shard_map/reduce_or | solution.py:203
  30.4 18.4 %all-to-all-done = bf16[16,512,128]{2,1,0:T(8,128)(2,1)} async-done(((bf16[16,512,128]{2,1,0:T(8,128)(2,1)}), bf16[16,512,128]{2,1,0:T(8,128)(2,1)}, u32[]{:S(2)}, u32[]{:S(2)}) %all-to-all-start) | async-done | bytes 2097184 | tf_op jit(solution)/shard_map/all_to_all | solution.py:100
  48.7 1.6 broadcast_in_dim.85
  50.3 3.6 %all-to-all-start.1 = ((bf16[8,128,1024]{2,1,0:T(8,128)(2,1)}), bf16[8,128,1024]{2,1,0:T(8,128)(2,1)S(1)}, u32[]{:S(2)}, u32[]{:S(2)}) async-start(bf16[8,128,1024]{2,1,0:T(8,128)(2,1)} %broadcast_in_dim.85), calls=%async_computation.1 | async-start | bytes 4194304 | tf_op jit(solution)/shard_map/all_to_all | solution.py:100
  53.9 2.7 %fusion.31 = (bf16[16,256,128]{2,1,0:T(8,128)(2,1)}, bf16[16,256,128]{2,1,0:T(8,128)(2,1)S(1)}) fusion(bf16[16,512,128]{2,1,0:T(8,128)(2,1)} %all-to-all-done), kind=kLoop, calls=%fused_computation.85 | loop fusion | bytes 4194304 | tf_op jit(solution)/shard_map/slice | solution.py:139
  56.7 1.8 reshape.207
  58.5 1.9 copy.29
  60.5 5.6 %gather_fusion = bf16[16,128,1024]{2,1,0:T(8,128)(2,1)} fusion(bf16[24,128,1024]{2,1,0:T(8,128)(2,1)} %param.19, s32[1024]{0:T(1024)S(1)} %pad_clamp_fusion), kind=kCustom, calls=%fused_computation | custom fusion | bytes 8388672 | tf_op jit(solution)/shard_map/jit(_take)/gather | solution.py:165
  66.1 1.3 pad_add_fusion.meta
  67.4 3.9 %bitcast_select_fusion.kc_ref.vc_ref = bf16[2048,1024]{1,0:T(8,128)(2,1)} fusion(bf16[16,128,1024]{2,1,0:T(8,128)(2,1)} %gather_fusion, pred[2048]{0:T(1024)(128)(4,1)S(1)} %broadcast_bitcast_fusion), kind=kLoop, calls=%fused_computation.5 | loop fusion | flops 2097152 | bytes 8390656 | tf_op jit(solution)/shard_map/jit(_take)/select_n | solution.py:165
  71.3 2.5 %reshape.215 = bf16[1024,512]{1,0:T(8,128)(2,1)} reshape(bf16[16,256,128]{2,1,0:T(8,128)(2,1)} %get-tuple-element.9) | data formatting | bytes 2097152 | tf_op jit(solution)/shard_map/reshape | solution.py:139
  73.8 0.6 collective-permute-start.1
  74.4 0.5 fusion.21
  74.9 1.7 convolution_add_fusion
  76.6 0.2 copy.30
  76.9 0.3 copy.31
  77.3 1.1 pad_maximum_fusion.1.q_ref
  78.4 1.4 copy-done.2
  79.8 17.0 %shard_map.127 = bf16[8,256,128]{2,1,0:T(8,128)(2,1)} custom-call(s32[2]{0:T(128)} %pad_add_fusion.meta, bf16[8,256,128]{2,1,0:T(8,128)(2,1)} %pad_maximum_fusion.1.q_ref, bf16[2048,1024]{1,0:T(8,128)(2,1)} %bitcast_select_fusion.kc_ref.vc_ref, bf16[2048,1024]{1,0:T(8,128)(2,1)} %bitcast_select_fusion.kc_ref.vc_ref, bf16[1024,1024]{1,0:T(8,128)(2,1)} %bitcast.65, ...), custom_call_target="tpu_custom_call" | custom-call | tf_op jit(solution)/shard_map/pallas_call | solution.py:86
  96.8 1.5 slice_select_fusion
  98.3 0.2 copy.34
  98.6 0.3 fusion.33
  98.9 1.6 broadcast_select_fusion.1
  100.7 1.3 convolution_convert_fusion
  102.0 1.9 slice_bitcast_fusion.5
  103.9 34.0 %all_to_all.30 = bf16[16,64,1024]{2,1,0:T(8,128)(2,1)} all-to-all(bf16[16,64,1024]{2,1,0:T(8,128)(2,1)S(1)} %get-tuple-element.7), channel_id=1, replica_groups=mesh['tz'=8,'tc'=2,'ra'=2,'rb'=8] {'ra','rb'}, dimensions={0} | all-to-all | bytes 4194304 | tf_op jit(solution)/shard_map/all_to_all | solution.py:211
  137.9 3.9 %all-to-all-start.4 = ((bf16[16,64,1024]{2,1,0:T(8,128)(2,1)}), bf16[16,64,1024]{2,1,0:T(8,128)(2,1)S(1)}, u32[]{:S(2)}, u32[]{:S(2)}) async-start(bf16[16,64,1024]{2,1,0:T(8,128)(2,1)} %get-tuple-element.8), calls=%async_computation.4 | async-start | bytes 4194304 | tf_op jit(solution)/shard_map/all_to_all | solution.py:211
  141.8 6.5 %fusion.4 = f32[1024,1024]{1,0:T(8,128)} fusion(bf16[1024,1024]{1,0:T(8,128)(2,1)} %bitcast.78, bf16[2,1024,1024]{2,1,0:T(8,128)(2,1)} %all-gather.3.cloned.1.call-done), kind=kOutput, calls=%fused_computation.15 | convolution fusion | flops 2147483648 | bytes 8388608 | tf_op jit(solution)/shard_map/dot_general | solution.py:214
  148.3 5.2 %convolution_convert_fusion.2 = bf16[1024,1024]{1,0:T(8,128)(2,1)} fusion(f32[1024,1024]{1,0:T(8,128)} %fusion.4, bf16[2,512,1024]{2,1,0:T(8,128)(2,1)} %all-gather.5.cloned.1.call-done), kind=kOutput, calls=%fused_computation.18 | convolution fusion | flops 1077936128 | bytes 7340032 | tf_op jit(solution)/shard_map/dot_general | solution.py:216
  153.5 17.0 %all-to-all-done.4 = bf16[16,64,1024]{2,1,0:T(8,128)(2,1)S(1)} async-done(((bf16[16,64,1024]{2,1,0:T(8,128)(2,1)}), bf16[16,64,1024]{2,1,0:T(8,128)(2,1)S(1)}, u32[]{:S(2)}, u32[]{:S(2)}) %all-to-all-start.4) | async-done | bytes 2097184 | tf_op jit(solution)/shard_map/all_to_all | solution.py:211
  170.5 1.3 copy-done.6
  171.9 3.7 %all-to-all-start.3 = ((bf16[16,64,1024]{2,1,0:T(8,128)(2,1)}), bf16[16,64,1024]{2,1,0:T(8,128)(2,1)S(1)}, u32[]{:S(2)}, u32[]{:S(2)}) async-start(bf16[16,64,1024]{2,1,0:T(8,128)(2,1)} %bitcast.76), calls=%async_computation.3 | async-start | bytes 4194304 | tf_op jit(solution)/shard_map/all_to_all | solution.py:220
  175.6 4.7 %fusion.2 = f32[1024,1024]{1,0:T(8,128)S(1)} fusion(bf16[1024,1024]{1,0:T(8,128)(2,1)} %bitcast.75, bf16[2,1024,1024]{2,1,0:T(8,128)(2,1)} %all-gather.3.cloned.1.call-done), kind=kOutput, calls=%fused_computation.10 | convolution fusion | flops 2147483648 | bytes 8388608 | tf_op jit(solution)/shard_map/dot_general | solution.py:214
  180.3 2.6 %convolution_convert_fusion.1 = bf16[1024,1024]{1,0:T(8,128)(2,1)} fusion(f32[1024,1024]{1,0:T(8,128)S(1)} %fusion.2, bf16[2,512,1024]{2,1,0:T(8,128)(2,1)S(1)} %copy-done.13), kind=kOutput, calls=%fused_computation.17 | convolution fusion | flops 1077936128 | bytes 7340032 | tf_op jit(solution)/shard_map/dot_general | solution.py:216
  183.0 20.3 %all-to-all-done.3 = bf16[16,64,1024]{2,1,0:T(8,128)(2,1)S(1)} async-done(((bf16[16,64,1024]{2,1,0:T(8,128)(2,1)}), bf16[16,64,1024]{2,1,0:T(8,128)(2,1)S(1)}, u32[]{:S(2)}, u32[]{:S(2)}) %all-to-all-start.3) | async-done | bytes 2097184 | tf_op jit(solution)/shard_map/all_to_all | solution.py:220
  203.3 4.8 %all-to-all-start.5 = ((bf16[16,64,1024]{2,1,0:T(8,128)(2,1)}), bf16[16,64,1024]{2,1,0:T(8,128)(2,1)}, u32[]{:S(2)}, u32[]{:S(2)}) async-start(bf16[16,64,1024]{2,1,0:T(8,128)(2,1)} %bitcast.77), calls=%async_computation.5 | async-start | bytes 4194304 | tf_op jit(solution)/shard_map/all_to_all | solution.py:220
  208.1 10.8 %select_reduce_fusion = f32[2048,128]{1,0:T(8,128)S(1)} fusion(f32[128,8]{0,1:T(8,128)S(1)} %copy-done.10, s32[128,8]{0,1:T(8,128)S(1)} %multiply_add_fusion), kind=kLoop, calls=%fused_computation.1 | loop fusion | flops 6029312 | bytes 1056768 | tf_op jit(solution)/shard_map/reduce_sum | solution.py:226
  218.9 16.7 %all-to-all-done.5 = bf16[16,64,1024]{2,1,0:T(8,128)(2,1)} async-done(((bf16[16,64,1024]{2,1,0:T(8,128)(2,1)}), bf16[16,64,1024]{2,1,0:T(8,128)(2,1)}, u32[]{:S(2)}, u32[]{:S(2)}) %all-to-all-start.5) | async-done | bytes 2097184 | tf_op jit(solution)/shard_map/all_to_all | solution.py:220
  235.7 2.0 pad_maximum_fusion
  237.6 2.8 %fusion.5 = bf16[128,1024]{1,0:T(8,128)(2,1)} fusion(f32[2048,128]{1,0:T(8,128)S(1)} %select_reduce_fusion, bf16[2048,1024]{1,0:T(8,128)(2,1)S(1)} %bitcast.68, bf16[128,1024]{1,0:T(8,128)(2,1)S(1)} %get-tuple-element.6), kind=kOutput, calls=%fused_computation.21 | convolution fusion | flops 3221618688 | bytes 5767168 | tf_op jit(solution)/shard_map/dot_general | solution.py:229
  (70 shorter events, 2.2 us)
Async XLA Ops:
  6.5 14.1 %copy-start = (bf16[1024,1024]{1,0:T(8,128)(2,1)S(1)}, bf16[1024,1024]{1,0:T(8,128)(2,1)}, u32[]{:S(2)}) copy-start(bf16[1024,1024]{1,0:T(8,128)(2,1)} %param.17) | copy-start | bytes 6291460
  6.5 135.2 %all-gather.3.cloned.1.call-start = ((), (), s32[]{:S(2)}) async-start(), calls=%async_computation.6 | async-start | bytes 4456448 | tf_op jit(solution)/shard_map/all_gather | solution.py:141
  11.0 8.0 %copy-start.4 = (bf16[128,1024]{1,0:T(8,128)(2,1)S(1)}, bf16[128,1024]{1,0:T(8,128)(2,1)}, u32[]{:S(2)}) copy-start(bf16[128,1024]{1,0:T(8,128)(2,1)} %param.13) | copy-start | bytes 786436
  11.1 8.2 %copy-start.9 = (f32[1024]{0:T(1024)S(1)}, f32[1024]{0:T(1024)}, u32[]{:S(2)}) copy-start(f32[1024]{0:T(1024)} %param.14) | copy-start | bytes 12292
  11.1 8.3 %copy-start.14 = (s32[2]{0:T(128)S(1)}, s32[2]{0:T(128)}, u32[]{:S(2)}) copy-start(s32[2]{0:T(128)} %param.21) | copy-start | bytes 28
  11.1 37.7 %all-to-all-start = ((bf16[16,512,128]{2,1,0:T(8,128)(2,1)}), bf16[16,512,128]{2,1,0:T(8,128)(2,1)}, u32[]{:S(2)}, u32[]{:S(2)}) async-start(bf16[16,512,128]{2,1,0:T(8,128)(2,1)} %broadcast_in_dim.80), calls=%async_computation | async-start | bytes 4194304 | tf_op jit(solution)/shard_map/all_to_all | solution.py:100
  18.3 130.0 %all-gather.5.cloned.1.call-start = ((), (), s32[]{:S(2)}) async-start(), calls=%async_computation.7 | async-start | bytes 2228224 | tf_op jit(solution)/shard_map/all_gather | solution.py:142
  20.6 1.0 copy-start.8
  21.1 0.9 copy-start.12
  50.3 28.1 %all-to-all-start.1 = ((bf16[8,128,1024]{2,1,0:T(8,128)(2,1)}), bf16[8,128,1024]{2,1,0:T(8,128)(2,1)S(1)}, u32[]{:S(2)}, u32[]{:S(2)}) async-start(bf16[8,128,1024]{2,1,0:T(8,128)(2,1)} %broadcast_in_dim.85), calls=%async_computation.1 | async-start | bytes 4194304 | tf_op jit(solution)/shard_map/all_to_all | solution.py:100
  60.4 14.4 %collective-permute-start = (bf16[512,1024]{0,1:T(8,128)(2,1)S(1)}, bf16[512,1024]{0,1:T(8,128)(2,1)}, u32[]{:S(2)}, u32[]{:S(2)}) collective-permute-start(bf16[512,1024]{0,1:T(8,128)(2,1)S(1)} %bitcast.71), channel_id=1, source_target_pairs={{0,16},{16,0},{1,17},{17,1},{2,18},{18,2},{3,19},{19,3},{4,20},{20... | collective-permute-start | bytes 3145736 | tf_op jit(solution)/shard_map/ppermute | solution.py:140
  73.8 25.1 %collective-permute-start.1 = (bf16[1024,512]{1,0:T(8,128)(2,1)}, bf16[1024,512]{1,0:T(8,128)(2,1)}, u32[]{:S(2)}, u32[]{:S(2)}) collective-permute-start(bf16[1024,512]{1,0:T(8,128)(2,1)} %reshape.215), channel_id=1, source_target_pairs={{0,16},{16,0},{1,17},{17,1},{2,18},{18,2},{3,19},{19,3},{4,20},{20... | collective-permute-start | bytes 3145736 | tf_op jit(solution)/shard_map/ppermute | solution.py:140
  78.4 1.4 copy-start.2
  96.8 1.7 copy-start.3
  98.3 2.2 copy-start.5
  98.5 2.1 copy-start.7
  98.6 2.1 copy-start.11
  137.9 32.6 %all-to-all-start.4 = ((bf16[16,64,1024]{2,1,0:T(8,128)(2,1)}), bf16[16,64,1024]{2,1,0:T(8,128)(2,1)S(1)}, u32[]{:S(2)}, u32[]{:S(2)}) async-start(bf16[16,64,1024]{2,1,0:T(8,128)(2,1)} %get-tuple-element.8), calls=%async_computation.4 | async-start | bytes 4194304 | tf_op jit(solution)/shard_map/all_to_all | solution.py:211
  170.5 1.3 copy-start.6
  171.9 31.4 %all-to-all-start.3 = ((bf16[16,64,1024]{2,1,0:T(8,128)(2,1)}), bf16[16,64,1024]{2,1,0:T(8,128)(2,1)S(1)}, u32[]{:S(2)}, u32[]{:S(2)}) async-start(bf16[16,64,1024]{2,1,0:T(8,128)(2,1)} %bitcast.76), calls=%async_computation.3 | async-start | bytes 4194304 | tf_op jit(solution)/shard_map/all_to_all | solution.py:220
  175.6 4.7 %copy-start.13 = (bf16[2,512,1024]{2,1,0:T(8,128)(2,1)S(1)}, bf16[2,512,1024]{2,1,0:T(8,128)(2,1)}, u32[]{:S(2)}) copy-start(bf16[2,512,1024]{2,1,0:T(8,128)(2,1)} %all-gather.5.cloned.1.call-done) | copy-start | bytes 6291460
  203.3 4.8 %copy-start.10 = (f32[128,8]{0,1:T(8,128)S(1)}, f32[128,8]{0,1:T(8,128)}, u32[]{:S(2)}) copy-start(f32[128,8]{0,1:T(8,128)} %param.23) | copy-start | bytes 12292
  203.3 32.4 %all-to-all-start.5 = ((bf16[16,64,1024]{2,1,0:T(8,128)(2,1)}), bf16[16,64,1024]{2,1,0:T(8,128)(2,1)}, u32[]{:S(2)}, u32[]{:S(2)}) async-start(bf16[16,64,1024]{2,1,0:T(8,128)(2,1)} %bitcast.77), calls=%async_computation.5 | async-start | bytes 4194304 | tf_op jit(solution)/shard_map/all_to_all | solution.py:220
  237.6 2.8 %copy-start.1 = (bf16[1024,1024]{1,0:T(8,128)(2,1)S(1)}, bf16[1024,1024]{1,0:T(8,128)(2,1)}, u32[]{:S(2)}) copy-start(bf16[1024,1024]{1,0:T(8,128)(2,1)} %param.17) | copy-start | bytes 6291460
Sparse Core Ops, SparseCore 0:
  9.2 40.9 all-gather.2
  52.0 37.6 all-gather.4

commit v7 on v6

--- a/solution.py
+++ b/solution.py
@@ -221,16 +221,17 @@
                 produced.reshape(tp_size, capacity, D), TP, split_axis=0, concat_axis=0, tiled=True
             )
         )
-    returned = jnp.stack(returned, axis=1)
-    returned = returned.reshape(EXPERTS * capacity, D)
-    mixing = jnp.sum(
-        jnp.where(hits, gate_weights[None, :, :], 0.0), axis=2
-    ).T
-    mixture = jnp.dot(
-        mixing,
-        returned.astype(jnp.float32),
-        precision=lax.Precision.HIGHEST,
-        preferred_element_type=jnp.float32,
+    mixing = jnp.sum(jnp.where(hits, gate_weights[None, :, :], 0.0), axis=2).T.reshape(
+        tok_rows, tp_size, experts_local, capacity
+    )
+    mixture = sum(
+        jnp.dot(
+            mixing[:, :, local].reshape(tok_rows, tp_size * capacity),
+            returned[local].reshape(tp_size * capacity, D).astype(jnp.float32),
+            precision=lax.Precision.HIGHEST,
+            preferred_element_type=jnp.float32,
+        )
+        for local in range(experts_local)
     )
     return (middle.astype(jnp.float32) + mixture).astype(jnp.bfloat16)
 

time: 248 us -> 249 us (level)
  matrix products: 27.6 us -> 30.4 us
  transfers between devices with their start and end apart: 9 -> 9, of which waited for: 4 -> 4; matrix products, arithmetic and copies ran while one was open for 31% -> 32% of each run, Pallas kernels for 7% -> 7%
where the time goes in v7:
time: 249 us; the launch traced here: 248 us
  waiting for transfers between devices  72.7 us (29%)
  blocking collectives  34.1 us (14%)
  matrix products  30.4 us (12%)
  local copies, waits for them, and re-layouts  27.8 us (11%)
  other arithmetic  27.8 us (11%)
  starting transfers between devices  23.8 us (10%)
  Pallas kernels  17 us (7%)
  between operations  14.5 us (6%)
    all_to_all x2, waiting for transfers between devices, shards(): lax.all_to_all(produced.reshape(tp_size, capacity, D), TP, split_axis=0,...  35.8 us
    all_to_all x1, blocking collectives, shards(): lax.all_to_all(send_buffer[:, local], TP, split_axis=0, concat_axis=0, ti...  34.1 us
    all_to_all x2, waiting for transfers between devices, gather_rows(): lax.all_to_all(send, axis_name, split_axis=0, concat_axis=0, tiled=True)  18.4 us
    pallas_call x1, Pallas kernels, attend(): pl.pallas_call(attention_kernel, grid_spec=pltpu.PrefetchScalarGridSpec(n...  17 us
    all_to_all x1, waiting for transfers between devices, shards(): lax.all_to_all(send_buffer[:, local], TP, split_axis=0, concat_axis=0, ti...  17 us
    dot_general x2, matrix products, shards(): jnp.dot(received, gate_up_full[local], preferred_element_type=jnp.float32)  11.3 us
    all_to_all x2, starting transfers between devices, gather_rows(): lax.all_to_all(send, axis_name, split_axis=0, concat_axis=0, tiled=True)  10.8 us
    reduce_sum x1, other arithmetic, shards(): jnp.sum(jnp.where(hits, gate_weights[None, :, :], 0.0), axis=2)  10.8 us
  transfers between devices with their start and end apart: 9, of which 4 were waited for; matrix products, arithmetic and copies ran while one was open for 32% of the time, Pallas kernels for 7%

profile of v7, /device:TPU:224, one launch (start us, length us, event | category | flops | bytes accessed | tf_op | source)
XLA Modules:
  0.0 248.0 jit_solution(14443047961260294255)
XLA Ops:
  6.5 0.7 all-gather.3.cloned.1.call-update
  7.3 0.8 constant_dynamic-slice_fusion.2
  8.4 0.9 constant_dynamic-slice_fusion.1
  9.3 1.8 broadcast_in_dim.80
  11.1 7.2 %all-to-all-start = ((bf16[16,512,128]{2,1,0:T(8,128)(2,1)}), bf16[16,512,128]{2,1,0:T(8,128)(2,1)}, u32[]{:S(2)}, u32[]{:S(2)}) async-start(bf16[16,512,128]{2,1,0:T(8,128)(2,1)} %broadcast_in_dim.80), calls=%async_computation | async-start | bytes 4194304 | tf_op jit(solution)/shard_map/all_to_all | solution.py:100
  18.4 0.7 all-gather.5.cloned.1.call-update
  19.4 0.6 dynamic_slice.18
  20.6 0.4 fusion.34
  22.1 8.1 %fusion = pred[2048,128]{1,0:T(8,128)(4,1)} fusion(s32[128,8]{0,1:T(8,128)S(1)} %multiply_add_fusion), kind=kLoop, calls=%fused_computation.3 | loop fusion | flops 3932160 | bytes 266240 | tf_op jit(solution)/shard_map/reduce_or | solution.py:203
  30.3 18.4 %all-to-all-done = bf16[16,512,128]{2,1,0:T(8,128)(2,1)} async-done(((bf16[16,512,128]{2,1,0:T(8,128)(2,1)}), bf16[16,512,128]{2,1,0:T(8,128)(2,1)}, u32[]{:S(2)}, u32[]{:S(2)}) %all-to-all-start) | async-done | bytes 2097184 | tf_op jit(solution)/shard_map/all_to_all | solution.py:100
  48.8 1.6 broadcast_in_dim.85
  50.4 3.6 %all-to-all-start.1 = ((bf16[8,128,1024]{2,1,0:T(8,128)(2,1)}), bf16[8,128,1024]{2,1,0:T(8,128)(2,1)S(1)}, u32[]{:S(2)}, u32[]{:S(2)}) async-start(bf16[8,128,1024]{2,1,0:T(8,128)(2,1)} %broadcast_in_dim.85), calls=%async_computation.1 | async-start | bytes 4194304 | tf_op jit(solution)/shard_map/all_to_all | solution.py:100
  54.0 2.7 %fusion.32 = (bf16[16,256,128]{2,1,0:T(8,128)(2,1)}, bf16[16,256,128]{2,1,0:T(8,128)(2,1)S(1)}) fusion(bf16[16,512,128]{2,1,0:T(8,128)(2,1)} %all-to-all-done), kind=kLoop, calls=%fused_computation.85 | loop fusion | bytes 4194304 | tf_op jit(solution)/shard_map/slice | solution.py:139
  56.7 1.8 reshape.213
  58.5 1.9 copy.29
  60.5 5.6 %gather_fusion = bf16[16,128,1024]{2,1,0:T(8,128)(2,1)} fusion(bf16[24,128,1024]{2,1,0:T(8,128)(2,1)} %param.19, s32[1024]{0:T(1024)S(1)} %pad_clamp_fusion), kind=kCustom, calls=%fused_computation | custom fusion | bytes 8388672 | tf_op jit(solution)/shard_map/jit(_take)/gather | solution.py:165
  66.1 1.1 pad_add_fusion.meta
  67.3 3.9 %bitcast_select_fusion.kc_ref.vc_ref = bf16[2048,1024]{1,0:T(8,128)(2,1)} fusion(bf16[16,128,1024]{2,1,0:T(8,128)(2,1)} %gather_fusion, pred[2048]{0:T(1024)(128)(4,1)S(1)} %broadcast_bitcast_fusion), kind=kLoop, calls=%fused_computation.4 | loop fusion | flops 2097152 | bytes 8390656 | tf_op jit(solution)/shard_map/jit(_take)/select_n | solution.py:165
  71.2 2.5 reshape.221
  73.6 0.6 collective-permute-start.1
  74.2 1.4 fusion.22
  75.6 1.8 convolution_add_fusion
  77.7 0.3 copy.31
  78.1 1.1 pad_maximum_fusion.q_ref
  79.2 1.4 copy-done.2
  80.6 17.0 %shard_map.127 = bf16[8,256,128]{2,1,0:T(8,128)(2,1)} custom-call(s32[2]{0:T(128)} %pad_add_fusion.meta, bf16[8,256,128]{2,1,0:T(8,128)(2,1)} %pad_maximum_fusion.q_ref, bf16[2048,1024]{1,0:T(8,128)(2,1)} %bitcast_select_fusion.kc_ref.vc_ref, bf16[2048,1024]{1,0:T(8,128)(2,1)} %bitcast_select_fusion.kc_ref.vc_ref, bf16[1024,1024]{1,0:T(8,128)(2,1)} %bitcast.71, ...), custom_call_target="tpu_custom_call" | custom-call | tf_op jit(solution)/shard_map/pallas_call | solution.py:86
  97.6 1.5 slice_select_fusion
  99.2 0.2 copy.34
  99.4 0.3 fusion.35
  99.8 1.6 broadcast_select_fusion.1
  101.5 1.3 convolution_convert_fusion
  102.8 1.9 slice_bitcast_fusion.2
  104.7 34.1 %all_to_all.30 = bf16[16,64,1024]{2,1,0:T(8,128)(2,1)} all-to-all(bf16[16,64,1024]{2,1,0:T(8,128)(2,1)S(1)} %get-tuple-element.8), channel_id=1, replica_groups=mesh['tz'=8,'tc'=2,'ra'=2,'rb'=8] {'ra','rb'}, dimensions={0} | all-to-all | bytes 4194304 | tf_op jit(solution)/shard_map/all_to_all | solution.py:211
  138.8 3.9 %all-to-all-start.4 = ((bf16[16,64,1024]{2,1,0:T(8,128)(2,1)}), bf16[16,64,1024]{2,1,0:T(8,128)(2,1)S(1)}, u32[]{:S(2)}, u32[]{:S(2)}) async-start(bf16[16,64,1024]{2,1,0:T(8,128)(2,1)} %get-tuple-element.7), calls=%async_computation.4 | async-start | bytes 4194304 | tf_op jit(solution)/shard_map/all_to_all | solution.py:211
  142.7 6.6 %fusion.4 = f32[1024,1024]{1,0:T(8,128)} fusion(bf16[1024,1024]{1,0:T(8,128)(2,1)} %bitcast.84, bf16[2,1024,1024]{2,1,0:T(8,128)(2,1)} %all-gather.3.cloned.1.call-done), kind=kOutput, calls=%fused_computation.14 | convolution fusion | flops 2147483648 | bytes 8388608 | tf_op jit(solution)/shard_map/dot_general | solution.py:214
  149.3 5.2 %convolution_convert_fusion.2 = bf16[1024,1024]{1,0:T(8,128)(2,1)} fusion(f32[1024,1024]{1,0:T(8,128)} %fusion.4, bf16[2,512,1024]{2,1,0:T(8,128)(2,1)} %all-gather.5.cloned.1.call-done), kind=kOutput, calls=%fused_computation.17 | convolution fusion | flops 1077936128 | bytes 7340032 | tf_op jit(solution)/shard_map/dot_general | solution.py:216
  154.4 17.0 %all-to-all-done.4 = bf16[16,64,1024]{2,1,0:T(8,128)(2,1)S(1)} async-done(((bf16[16,64,1024]{2,1,0:T(8,128)(2,1)}), bf16[16,64,1024]{2,1,0:T(8,128)(2,1)S(1)}, u32[]{:S(2)}, u32[]{:S(2)}) %all-to-all-start.4) | async-done | bytes 2097184 | tf_op jit(solution)/shard_map/all_to_all | solution.py:211
  171.4 1.3 copy-done.8
  172.8 3.7 %all-to-all-start.3 = ((bf16[16,64,1024]{2,1,0:T(8,128)(2,1)}), bf16[16,64,1024]{2,1,0:T(8,128)(2,1)S(1)}, u32[]{:S(2)}, u32[]{:S(2)}) async-start(bf16[16,64,1024]{2,1,0:T(8,128)(2,1)} %bitcast.83), calls=%async_computation.3 | async-start | bytes 4194304 | tf_op jit(solution)/shard_map/all_to_all | solution.py:220
  176.5 4.7 %fusion.2 = f32[1024,1024]{1,0:T(8,128)S(1)} fusion(bf16[1024,1024]{1,0:T(8,128)(2,1)} %bitcast.81, bf16[2,1024,1024]{2,1,0:T(8,128)(2,1)} %all-gather.3.cloned.1.call-done), kind=kOutput, calls=%fused_computation.9 | convolution fusion | flops 2147483648 | bytes 8388608 | tf_op jit(solution)/shard_map/dot_general | solution.py:214
  181.2 2.6 %convolution_convert_fusion.1 = bf16[1024,1024]{1,0:T(8,128)(2,1)} fusion(f32[1024,1024]{1,0:T(8,128)S(1)} %fusion.2, bf16[2,512,1024]{2,1,0:T(8,128)(2,1)S(1)} %copy-done.15), kind=kOutput, calls=%fused_computation.16 | convolution fusion | flops 1077936128 | bytes 7340032 | tf_op jit(solution)/shard_map/dot_general | solution.py:216
  183.9 20.3 %all-to-all-done.3 = bf16[16,64,1024]{2,1,0:T(8,128)(2,1)S(1)} async-done(((bf16[16,64,1024]{2,1,0:T(8,128)(2,1)}), bf16[16,64,1024]{2,1,0:T(8,128)(2,1)S(1)}, u32[]{:S(2)}, u32[]{:S(2)}) %all-to-all-start.3) | async-done | bytes 2097184 | tf_op jit(solution)/shard_map/all_to_all | solution.py:220
  204.2 1.3 copy-done.3
  205.6 4.7 %all-to-all-start.5 = ((bf16[16,64,1024]{2,1,0:T(8,128)(2,1)}), bf16[16,64,1024]{2,1,0:T(8,128)(2,1)}, u32[]{:S(2)}, u32[]{:S(2)}) async-start(bf16[16,64,1024]{2,1,0:T(8,128)(2,1)} %bitcast.82), calls=%async_computation.5 | async-start | bytes 4194304 | tf_op jit(solution)/shard_map/all_to_all | solution.py:220
  210.2 10.8 %select_reduce_fusion = f32[2048,128]{1,0:T(8,128)S(1)} fusion(f32[128,8]{0,1:T(8,128)S(1)} %copy-done.12, s32[128,8]{0,1:T(8,128)S(1)} %multiply_add_fusion), kind=kLoop, calls=%fused_computation.1 | loop fusion | flops 6029312 | bytes 1056768 | tf_op jit(solution)/shard_map/reduce_sum | solution.py:224
  221.2 1.1 fusion.36
  222.3 15.5 %all-to-all-done.5 = bf16[16,64,1024]{2,1,0:T(8,128)(2,1)} async-done(((bf16[16,64,1024]{2,1,0:T(8,128)(2,1)}), bf16[16,64,1024]{2,1,0:T(8,128)(2,1)}, u32[]{:S(2)}, u32[]{:S(2)}) %all-to-all-start.5) | async-done | bytes 2097184 | tf_op jit(solution)/shard_map/all_to_all | solution.py:220
  237.8 3.4 %fusion.6 = bf16[128,1024]{1,0:T(8,128)(2,1)} fusion(f32[128,1024]{1,0:T(8,128)S(1)} %fusion.36, f32[128,1024]{0,1:T(8,128)S(1)} %bitcast.85, bf16[1024,1024]{1,0:T(8,128)(2,1)} %bitcast.38, bf16[128,1024]{1,0:T(8,128)(2,1)S(1)} %get-tuple-element.6), kind=kOutput, calls=%fused_computation.21 | convolution fusion | flops 1611137024 | bytes 3670016 | tf_op jit(solution)/shard_map/dot_general | solution.py:228
  (75 shorter events, 2.5 us)
Async XLA Ops:
  6.5 14.1 %copy-start = (bf16[1024,1024]{1,0:T(8,128)(2,1)S(1)}, bf16[1024,1024]{1,0:T(8,128)(2,1)}, u32[]{:S(2)}) copy-start(bf16[1024,1024]{1,0:T(8,128)(2,1)} %param.17) | copy-start | bytes 6291460
  6.5 136.2 %all-gather.3.cloned.1.call-start = ((), (), s32[]{:S(2)}) async-start(), calls=%async_computation.6 | async-start | bytes 4456448 | tf_op jit(solution)/shard_map/all_gather | solution.py:141
  11.1 8.0 %copy-start.6 = (bf16[128,1024]{1,0:T(8,128)(2,1)S(1)}, bf16[128,1024]{1,0:T(8,128)(2,1)}, u32[]{:S(2)}) copy-start(bf16[128,1024]{1,0:T(8,128)(2,1)} %param.13) | copy-start | bytes 786436
  11.1 8.2 %copy-start.11 = (f32[1024]{0:T(1024)S(1)}, f32[1024]{0:T(1024)}, u32[]{:S(2)}) copy-start(f32[1024]{0:T(1024)} %param.14) | copy-start | bytes 12292
  11.1 8.3 %copy-start.16 = (s32[2]{0:T(128)S(1)}, s32[2]{0:T(128)}, u32[]{:S(2)}) copy-start(s32[2]{0:T(128)} %param.21) | copy-start | bytes 28
  11.1 37.7 %all-to-all-start = ((bf16[16,512,128]{2,1,0:T(8,128)(2,1)}), bf16[16,512,128]{2,1,0:T(8,128)(2,1)}, u32[]{:S(2)}, u32[]{:S(2)}) async-start(bf16[16,512,128]{2,1,0:T(8,128)(2,1)} %broadcast_in_dim.80), calls=%async_computation | async-start | bytes 4194304 | tf_op jit(solution)/shard_map/all_to_all | solution.py:100
  18.3 131.0 %all-gather.5.cloned.1.call-start = ((), (), s32[]{:S(2)}) async-start(), calls=%async_computation.7 | async-start | bytes 2228224 | tf_op jit(solution)/shard_map/all_gather | solution.py:142
  19.4 1.9 copy-start.7
  20.6 1.0 copy-start.10
  21.1 0.9 copy-start.14
  50.4 28.9 %all-to-all-start.1 = ((bf16[8,128,1024]{2,1,0:T(8,128)(2,1)}), bf16[8,128,1024]{2,1,0:T(8,128)(2,1)S(1)}, u32[]{:S(2)}, u32[]{:S(2)}) async-start(bf16[8,128,1024]{2,1,0:T(8,128)(2,1)} %broadcast_in_dim.85), calls=%async_computation.1 | async-start | bytes 4194304 | tf_op jit(solution)/shard_map/all_to_all | solution.py:100
  60.4 15.2 %collective-permute-start = (bf16[512,1024]{0,1:T(8,128)(2,1)S(1)}, bf16[512,1024]{0,1:T(8,128)(2,1)}, u32[]{:S(2)}, u32[]{:S(2)}) collective-permute-start(bf16[512,1024]{0,1:T(8,128)(2,1)S(1)} %bitcast.76), channel_id=1, source_target_pairs={{0,16},{16,0},{1,17},{17,1},{2,18},{18,2},{3,19},{19,3},{4,20},{20... | collective-permute-start | bytes 3145736 | tf_op jit(solution)/shard_map/ppermute | solution.py:140
  73.6 26.1 %collective-permute-start.1 = (bf16[1024,512]{1,0:T(8,128)(2,1)}, bf16[1024,512]{1,0:T(8,128)(2,1)}, u32[]{:S(2)}, u32[]{:S(2)}) collective-permute-start(bf16[1024,512]{1,0:T(8,128)(2,1)} %reshape.221), channel_id=1, source_target_pairs={{0,16},{16,0},{1,17},{17,1},{2,18},{18,2},{3,19},{19,3},{4,20},{20... | collective-permute-start | bytes 3145736 | tf_op jit(solution)/shard_map/ppermute | solution.py:140
  79.2 1.4 copy-start.2
  97.6 1.7 copy-start.5
  99.4 2.1 copy-start.9
  99.4 2.1 copy-start.13
  138.8 32.6 %all-to-all-start.4 = ((bf16[16,64,1024]{2,1,0:T(8,128)(2,1)}), bf16[16,64,1024]{2,1,0:T(8,128)(2,1)S(1)}, u32[]{:S(2)}, u32[]{:S(2)}) async-start(bf16[16,64,1024]{2,1,0:T(8,128)(2,1)} %get-tuple-element.7), calls=%async_computation.4 | async-start | bytes 4194304 | tf_op jit(solution)/shard_map/all_to_all | solution.py:211
  171.4 1.3 copy-start.8
  172.8 31.4 %all-to-all-start.3 = ((bf16[16,64,1024]{2,1,0:T(8,128)(2,1)}), bf16[16,64,1024]{2,1,0:T(8,128)(2,1)S(1)}, u32[]{:S(2)}, u32[]{:S(2)}) async-start(bf16[16,64,1024]{2,1,0:T(8,128)(2,1)} %bitcast.83), calls=%async_computation.3 | async-start | bytes 4194304 | tf_op jit(solution)/shard_map/all_to_all | solution.py:220
  176.5 4.7 %copy-start.15 = (bf16[2,512,1024]{2,1,0:T(8,128)(2,1)S(1)}, bf16[2,512,1024]{2,1,0:T(8,128)(2,1)}, u32[]{:S(2)}) copy-start(bf16[2,512,1024]{2,1,0:T(8,128)(2,1)} %all-gather.5.cloned.1.call-done) | copy-start | bytes 6291460
  204.2 1.3 copy-start.3
  204.2 6.0 %copy-start.12 = (f32[128,8]{0,1:T(8,128)S(1)}, f32[128,8]{0,1:T(8,128)}, u32[]{:S(2)}) copy-start(f32[128,8]{0,1:T(8,128)} %param.23) | copy-start | bytes 12292
  205.6 32.2 %all-to-all-start.5 = ((bf16[16,64,1024]{2,1,0:T(8,128)(2,1)}), bf16[16,64,1024]{2,1,0:T(8,128)(2,1)}, u32[]{:S(2)}, u32[]{:S(2)}) async-start(bf16[16,64,1024]{2,1,0:T(8,128)(2,1)} %bitcast.82), calls=%async_computation.5 | async-start | bytes 4194304 | tf_op jit(solution)/shard_map/all_to_all | solution.py:220
  210.2 10.9 %copy-start.4 = (bf16[16,64,1024]{2,1,0:T(8,128)(2,1)S(1)}, bf16[16,64,1024]{2,1,0:T(8,128)(2,1)}, u32[]{:S(2)}) copy-start(bf16[16,64,1024]{2,1,0:T(8,128)(2,1)} %copy-done.3) | copy-start | bytes 6291460
  221.2 20.0 %copy-start.1 = (bf16[1024,1024]{1,0:T(8,128)(2,1)S(1)}, bf16[1024,1024]{1,0:T(8,128)(2,1)}, u32[]{:S(2)}) copy-start(bf16[1024,1024]{1,0:T(8,128)(2,1)} %param.17) | copy-start | bytes 6291460
Sparse Core Ops, SparseCore 0:
  9.2 41.0 all-gather.2
  52.1 37.5 all-gather.4
